TPU v7x, 256 devices: a whole 4x4x8 slice. The times are simulated.
256 devices in a mesh: dp: 64 (over z_lo, x, y, core), fsdp: 4 (over z_hi).
Axes of the slice: x: 4, y: 4, z: 8 (z_hi: 4, z_lo: 2; z = z_hi * 2 + z_lo), core: 2. Of those that a mesh axis runs over, the one named last changes fastest.
Arguments:
- latents: bfloat16 [64, 2, 256, 2432], P('dp', None, 'fsdp'), may hold values from -6 to 6
- targets: bfloat16 [64, 2, 256, 2432], P('dp', None, 'fsdp'), may hold values from -6 to 6
- frozen_weight: bfloat16 [2432, 2432], P('fsdp'), may hold values from -0.125 to 0.125
- adapter_down: bfloat16 [7, 64, 2432], P(None, None, 'dp'), may hold values from -0.125 to 0.125
- adapter_up: bfloat16 [7, 64, 2432], P(None, None, 'dp'), may hold values from -0.75 to 0.75
- categories: int32 [64], P('dp'), may hold values from 0 to 6
- timesteps: int32 [64], P('dp'), may hold values from 0 to 999
Outputs:
- grad_down: float32 [7, 64, 2432], P(None, None, 'dp')
- grad_up: float32 [7, 64, 2432], P(None, None, 'dp')
- losses: float32 [64], P('dp')
All inputs are finite; a program needn't handle non-finite values.
Results may differ from a plain program's by a relative error of at most 0.0048.
Values may be sent and summed in bfloat16 or wider, within the bound.
No kernel may reach another device: no remote copies, remote signals or barrier semaphores. Data moves between devices by JAX's collectives and lax.ppermute only.
A program may use at most 128 MiB of HBM per device.

v0:
```python
import jax
import jax.numpy as jnp
from jax import lax
from jax.sharding import PartitionSpec as P

ADAPTER_SCALE = 0.5
BETA = 1.0
LOSS_SCALE = 64.0


def local(latents, targets, frozen_weight, adapter_down, adapter_up, categories, timesteps):
    pair_local, _, row_local, feat_width = latents.shape
    class_total = adapter_down.shape[0]
    adapter_rank_width = adapter_down.shape[1]
    sample_rows = row_local * lax.axis_size("fsdp")
    flat_in = latents.reshape(pair_local * 2 * row_local, feat_width)
    down_full, up_full = (
        lax.all_gather(adapter_down, "dp", axis=2, tiled=True),
        lax.all_gather(adapter_up, "dp", axis=2, tiled=True),
    )
    base_out = jnp.dot(
        flat_in,
        lax.all_gather(frozen_weight, "fsdp", axis=0, tiled=True),
        preferred_element_type=jnp.float32,
    )
    selected_down = jnp.take(down_full, categories, axis=0)
    selected_up = jnp.take(up_full, categories, axis=0)
    grouped = latents.reshape(pair_local, 2 * row_local, feat_width)
    hidden_state = jnp.einsum(
        "psd,prd->psr", grouped, selected_down, preferred_element_type=jnp.float32
    ).astype(jnp.bfloat16)
    weight_change = ADAPTER_SCALE * jnp.einsum(
        "psr,prd->psd", hidden_state, selected_up, preferred_element_type=jnp.float32
    )
    weight_change = weight_change.reshape(pair_local, 2, row_local, feat_width)
    resid = base_out.reshape(pair_local, 2, row_local, feat_width) - targets.astype(jnp.float32)
    partial_err = jnp.sum(weight_change * (2.0 * resid + weight_change), axis=(2, 3))
    onehot = (categories[:, None] == jnp.arange(class_total, dtype=jnp.int32)[None, :]).astype(
        jnp.float32
    )
    errdiff = lax.psum(partial_err, "fsdp") / sample_rows
    counts = lax.psum(jnp.sum(onehot, axis=0), "dp")
    kappa = BETA * (0.5 + timesteps.astype(jnp.float32) / 1000.0)
    zvalue = kappa * (errdiff[:, 0] - errdiff[:, 1])
    losses = jax.nn.softplus(zvalue)
    pair_total = jnp.sum(onehot * counts[None, :], axis=1)
    coef_pair = LOSS_SCALE * kappa * jax.nn.sigmoid(zvalue) / pair_total
    signs = jnp.array([2.0, -2.0], dtype=jnp.float32)
    coefficient = coef_pair[:, None] * signs[None, :] / sample_rows
    update = (resid + weight_change).astype(jnp.bfloat16)
    hidden_k = hidden_state.reshape(pair_local, 2, row_local, adapter_rank_width)
    up_gradient_k = jnp.einsum(
        "pktr,pktd->pkrd", hidden_k, update, preferred_element_type=jnp.float32
    )
    back = jnp.einsum(
        "pktd,prd->pktr", update, selected_up, preferred_element_type=jnp.float32
    ).astype(jnp.bfloat16)
    down_gradient_k = jnp.einsum(
        "pktr,pktd->pkrd", back, latents, preferred_element_type=jnp.float32
    )
    pairwise_up = ADAPTER_SCALE * jnp.sum(coefficient[:, :, None, None] * up_gradient_k, axis=1)
    pairwise_down = ADAPTER_SCALE * jnp.sum(coefficient[:, :, None, None] * down_gradient_k, axis=1)
    pairwise_down, pairwise_up = lax.psum((pairwise_down, pairwise_up), "fsdp")
    dense_down = jnp.einsum("pc,prd->crd", onehot, pairwise_down, precision=lax.Precision.HIGHEST)
    dense_up = jnp.einsum("pc,prd->crd", onehot, pairwise_up, precision=lax.Precision.HIGHEST)
    grad_down, grad_up = (
        lax.psum_scatter(dense_down, "dp", scatter_dimension=2, tiled=True),
        lax.psum_scatter(dense_up, "dp", scatter_dimension=2, tiled=True),
    )
    return (grad_down, grad_up, losses)


def solution(mesh):
    placed = (
        P("dp", None, "fsdp", None),
        P("dp", None, "fsdp", None),
        P("fsdp", None),
        P(None, None, "dp"),
        P(None, None, "dp"),
        P("dp"),
        P("dp"),
    )
    return jax.shard_map(
        local,
        mesh=mesh,
        in_specs=placed,
        out_specs=(P(None, None, "dp"), P(None, None, "dp"), P("dp")),
        check_vma=False,
    )
```

profile of v0, /device:TPU:32, one launch (start us, length us, event | category | flops | bytes accessed | tf_op | source)
XLA Modules:
  0.0 1162.4 jit_solution(6137936658721011508)
XLA Ops:
  7.2 0.0 copy-start
  7.2 0.0 all-gather.4.cloned.1.call-start
  7.2 1.6 copy.17
  8.8 0.0 all-gather.4.cloned.1.call-update
  8.8 0.0 all-gather.6.cloned.1.call-start
  8.9 1.5 copy.19
  10.4 0.0 all-gather.6.cloned.1.call-update
  10.4 0.0 all-gather.8.cloned.1.call-start
  10.5 0.7 all-gather.8.cloned.1.call-update
  11.2 0.0 all-reduce.9.cloned.1.call-start
  11.9 142.7 %psum.29 = f32[7]{0:T(128)S(1)} all-reduce(f32[7]{0:T(128)S(1)} %compare_convert_fusion.1), channel_id=1, replica_groups=mesh['dp'=64,'fsdp'=4] {'dp'}, use_global_device_ids=true, to_apply=%region_2.4 | all-reduce | flops 7 | bytes 56 | tf_op jit(solution)/shard_map/psum | solution.py:42
  155.2 0.6 fusion.25
  155.8 0.0 all-gather.4.cloned.1.call-done
  155.9 3.8 constant_dynamic-slice_fusion.3
  159.6 1.2 copy.30
  160.8 70.0 %all-gather.6.cloned.1.call-done = bf16[7,64,2432]{1,0,2:T(8,128)(2,1)} async-done(((bf16[7,64,38]{1,0,2:T(8,128)(2,1)}), bf16[7,64,2432]{1,0,2:T(8,128)(2,1)}) %all-gather.6.cloned.1.call-update) | async-done | bytes 2179088 | tf_op jit(solution)/shard_map/all_gather | solution.py:19
  230.9 3.8 constant_dynamic-slice_fusion.2
  234.6 1.2 copy.31
  235.8 0.0 copy-done
  235.9 0.0 copy-start.2
  235.9 0.3 convolution_convert_fusion.1
  236.2 0.1 reshape.148
  236.3 0.4 convolution_multiply_fusion.2
  236.7 207.3 %all-gather.8.cloned.1.call-done = bf16[2432,2432]{1,0:T(8,128)(2,1)} async-done(((bf16[608,2432]{1,0:T(8,128)(2,1)}), bf16[2432,2432]{1,0:T(8,128)(2,1)}) %all-gather.8.cloned.1.call-update) | async-done | bytes 11829264 | tf_op jit(solution)/shard_map/all_gather | solution.py:23
  443.9 0.0 copy-done.2
  443.9 0.0 copy-start.5
  443.9 6.5 fusion.10
  450.4 11.0 psum.28
  461.4 0.6 fusion.31
  464.0 0.0 copy-done.5
  464.1 0.9 fusion.8
  465.0 0.3 fusion.9
  465.3 1.1 broadcast_multiply_fusion.2
  466.4 0.0 all-reduce.9.cloned.1.call-update
  466.5 0.0 all-reduce.7.cloned.1.call-start
  466.5 69.4 %all-reduce.9.cloned.1.call-done = (f32[64,2432]{1,0:T(8,128)}, f32[64,2432]{1,0:T(8,128)}) async-done(((f32[64,2432]{1,0:T(8,128)}, f32[64,2432]{1,0:T(8,128)}), (f32[64,2432]{1,0:T(8,128)}, f32[64,2432]{1,0:T(8,128)})) %all-reduce.9.cloned.1.call-update) | async-done | bytes 1245200 | tf_op jit(solution)/shard_map/psum | solution.py:63
  535.9 1.5 copy.22
  537.4 0.0 copy-done.3
  537.4 0.4 copy.24
  537.8 7.6 broadcast_multiply_fusion
  545.5 0.0 all-reduce.7.cloned.1.call-update
  545.5 0.0 copy-start.1
  545.5 0.6 copy-done.4
  546.1 0.6 dynamic-slice.7
  547.5 604.1 %all-reduce.7.cloned.1.call-done = (f32[7,64,2432]{1,2,0:T(8,128)}, f32[7,64,2432]{1,2,0:T(8,128)}) async-done(((f32[7,64,2432]{1,2,0:T(8,128)}, f32[7,64,2432]{1,2,0:T(8,128)}), (f32[7,64,2432]{1,2,0:T(8,128)}, f32[7,64,2432]{1,2,0:T(8,128)})) %all-reduce.7.cloned.1.call-update) | async-done | bytes 8716304
  1151.6 1.6 constant_dynamic-slice_fusion
  1153.2 1.6 constant_dynamic-slice_fusion.1
  1154.8 0.0 copy-done.1
  (6 shorter events, 0.0 us)
Async XLA Ops:
  7.2 228.7 %copy-start = (bf16[1,2,64,2432]{3,2,1,0:T(8,128)(2,1)S(1)}, bf16[1,2,64,2432]{3,2,1,0:T(8,128)(2,1)}, u32[]{:S(2)}) copy-start(bf16[1,2,64,2432]{3,2,1,0:T(8,128)(2,1)} %param.10) | copy-start | bytes 1867780
  7.2 148.7 %all-gather.4.cloned.1.call-start = ((), (), s32[]{:S(2)}) async-start(), calls=%async_computation | async-start | bytes 5058560 | tf_op jit(solution)/shard_map/all_gather | solution.py:18
  8.8 222.0 %all-gather.6.cloned.1.call-start = ((), (), s32[]{:S(2)}) async-start(), calls=%async_computation.1 | async-start | bytes 5058560 | tf_op jit(solution)/shard_map/all_gather | solution.py:19
  10.4 433.5 %all-gather.8.cloned.1.call-start = ((), (), s32[]{:S(2)}) async-start(), calls=%async_computation.2 | async-start | bytes 14786560 | tf_op jit(solution)/shard_map/all_gather | solution.py:23
  11.2 524.7 %all-reduce.9.cloned.1.call-start = ((), (), s32[]{:S(2)}) async-start(), calls=%async_computation.4 | async-start | bytes 2490368 | tf_op jit(solution)/shard_map/psum | solution.py:63
  235.9 208.1 %copy-start.2 = (bf16[1,2,64,2432]{3,2,1,0:T(8,128)(2,1)S(1)}, bf16[1,2,64,2432]{3,2,1,0:T(8,128)(2,1)}, u32[]{:S(2)}) copy-start(bf16[1,2,64,2432]{3,2,1,0:T(8,128)(2,1)} %param.11) | copy-start | bytes 1867780
  443.9 20.1 %copy-start.5 = (f32[2]{0:T(128)S(1)}, f32[2]{0:T(128)}, u32[]{:S(2)}) copy-start(f32[2]{0:T(128)} %constant.37.clone) | copy-start | bytes 28
  466.5 685.1 %all-reduce.7.cloned.1.call-start = ((), (), s32[]{:S(2)}) async-start(), calls=%async_computation.3 | async-start | bytes 34865152
  535.9 1.5 copy-start.3
  545.5 0.7 copy-start.4
  545.5 609.3 %copy-start.1 = (bf16[1,2,64,2432]{3,2,1,0:T(8,128)(2,1)S(1)}, bf16[1,2,64,2432]{3,2,1,0:T(8,128)(2,1)}, u32[]{:S(2)}) copy-start(bf16[1,2,64,2432]{3,2,1,0:T(8,128)(2,1)} %param.10) | copy-start | bytes 1867780
Sparse Core Ops, SparseCore 0:
  10.4 110.6 all-gather.3
  123.5 107.3 all-gather.5
  232.7 211.2 all-gather.7
  466.6 69.2 all-reduce.8
  545.6 605.9 all-reduce.6
where the time goes:
time: 1160 us
  waiting for transfers between devices  952 us (82%)
  blocking collectives  154 us (13%)
  local copies, waits for them, and re-layouts  20.1 us (2%)
  between operations  19.2 us (2%)
    unnamed x6, waiting for transfers between devices  605 us
    all_gather x1, waiting for transfers between devices, local(): lax.all_gather(frozen_weight, 'fsdp', axis=0, tiled=True)  207 us
    psum x1, blocking collectives, local(): counts = lax.psum(jnp.sum(onehot, axis=0), 'dp')  143 us
    all_gather x1, waiting for transfers between devices, local(): lax.all_gather(adapter_up, 'dp', axis=2, tiled=True)  70 us
    psum x1, waiting for transfers between devices, local(): pairwise_down, pairwise_up = lax.psum((pairwise_down, pairwise_up), 'fsdp')  69.4 us
  transfers between devices with their start and end apart: 5, of which 4 were waited for; matrix products, arithmetic and copies ran while one was open for 1% of the time, Pallas kernels for 0%

commit v1 on v0

--- a/solution.py
+++ b/solution.py
@@ -10,21 +10,38 @@
 
 def local(latents, targets, frozen_weight, adapter_down, adapter_up, categories, timesteps):
     pair_local, _, row_local, feat_width = latents.shape
-    class_total = adapter_down.shape[0]
-    adapter_rank_width = adapter_down.shape[1]
-    sample_rows = row_local * lax.axis_size("fsdp")
-    flat_in = latents.reshape(pair_local * 2 * row_local, feat_width)
-    down_full, up_full = (
-        lax.all_gather(adapter_down, "dp", axis=2, tiled=True),
-        lax.all_gather(adapter_up, "dp", axis=2, tiled=True),
+    class_total, adapter_rank_width, col_local = adapter_down.shape
+    fsdp_size = lax.axis_size("fsdp")
+    dp_size = lax.axis_size("dp")
+    in_local = frozen_weight.shape[0]
+    sample_rows = row_local * fsdp_size
+
+    cats_all = lax.all_gather(categories, "dp", tiled=True)
+    onehot_all = (cats_all[:, None] == jnp.arange(class_total, dtype=jnp.int32)[None, :]).astype(
+        jnp.float32
     )
-    base_out = jnp.dot(
-        flat_in,
-        lax.all_gather(frozen_weight, "fsdp", axis=0, tiled=True),
+    counts = jnp.sum(onehot_all, axis=0)
+
+    both = jnp.stack([adapter_down, adapter_up], axis=1)
+    send = jnp.take(both, cats_all.reshape(dp_size, pair_local), axis=0)
+    recv = lax.all_to_all(send, "dp", 0, 0, tiled=True)
+    selected = recv.transpose(1, 2, 3, 0, 4).reshape(
+        pair_local, 2, adapter_rank_width, dp_size * col_local
+    )
+    selected_down = selected[:, 0]
+    selected_up = selected[:, 1]
+
+    x_split = latents.reshape(pair_local, 2, row_local, fsdp_size, in_local).transpose(3, 0, 1, 2, 4)
+    x_slice = lax.all_to_all(x_split, "fsdp", 0, 0, tiled=True)
+    partial = jnp.dot(
+        x_slice.reshape(fsdp_size * pair_local * 2 * row_local, in_local),
+        frozen_weight,
         preferred_element_type=jnp.float32,
+    ).reshape(fsdp_size, pair_local * 2 * row_local, feat_width)
+    base_out = lax.psum_scatter(partial, "fsdp", scatter_dimension=0, tiled=True).reshape(
+        pair_local, 2, row_local, feat_width
     )
-    selected_down = jnp.take(down_full, categories, axis=0)
-    selected_up = jnp.take(up_full, categories, axis=0)
+
     grouped = latents.reshape(pair_local, 2 * row_local, feat_width)
     hidden_state = jnp.einsum(
         "psd,prd->psr", grouped, selected_down, preferred_element_type=jnp.float32
@@ -33,13 +50,12 @@
         "psr,prd->psd", hidden_state, selected_up, preferred_element_type=jnp.float32
     )
     weight_change = weight_change.reshape(pair_local, 2, row_local, feat_width)
-    resid = base_out.reshape(pair_local, 2, row_local, feat_width) - targets.astype(jnp.float32)
+    resid = base_out - targets.astype(jnp.float32)
     partial_err = jnp.sum(weight_change * (2.0 * resid + weight_change), axis=(2, 3))
     onehot = (categories[:, None] == jnp.arange(class_total, dtype=jnp.int32)[None, :]).astype(
         jnp.float32
     )
     errdiff = lax.psum(partial_err, "fsdp") / sample_rows
-    counts = lax.psum(jnp.sum(onehot, axis=0), "dp")
     kappa = BETA * (0.5 + timesteps.astype(jnp.float32) / 1000.0)
     zvalue = kappa * (errdiff[:, 0] - errdiff[:, 1])
     losses = jax.nn.softplus(zvalue)
@@ -60,13 +76,18 @@
     )
     pairwise_up = ADAPTER_SCALE * jnp.sum(coefficient[:, :, None, None] * up_gradient_k, axis=1)
     pairwise_down = ADAPTER_SCALE * jnp.sum(coefficient[:, :, None, None] * down_gradient_k, axis=1)
-    pairwise_down, pairwise_up = lax.psum((pairwise_down, pairwise_up), "fsdp")
-    dense_down = jnp.einsum("pc,prd->crd", onehot, pairwise_down, precision=lax.Precision.HIGHEST)
-    dense_up = jnp.einsum("pc,prd->crd", onehot, pairwise_up, precision=lax.Precision.HIGHEST)
-    grad_down, grad_up = (
-        lax.psum_scatter(dense_down, "dp", scatter_dimension=2, tiled=True),
-        lax.psum_scatter(dense_up, "dp", scatter_dimension=2, tiled=True),
+
+    grads = jnp.stack([pairwise_down, pairwise_up], axis=1).reshape(
+        pair_local, 2, adapter_rank_width, dp_size, col_local
     )
+    grads = grads.transpose(3, 0, 1, 2, 4)
+    gathered = lax.all_to_all(grads, "dp", 0, 0, tiled=True).reshape(
+        dp_size * pair_local, 2 * adapter_rank_width * col_local
+    )
+    dense = jnp.dot(onehot_all.T, gathered, precision=lax.Precision.HIGHEST)
+    dense = lax.psum(dense, "fsdp").reshape(class_total, 2, adapter_rank_width, col_local)
+    grad_down = dense[:, 0]
+    grad_up = dense[:, 1]
     return (grad_down, grad_up, losses)
 
 

time: 1160 us -> 301 us (0.26)
  waiting for transfers between devices: 952 us -> 91.5 us
  blocking collectives: 154 us -> 86.9 us
  local copies, waits for them, and re-layouts: 20.1 us -> 61.7 us
    unnamed x6 -> x2, waiting for transfers between devices: 605 us -> 0.03 us
    all_gather x3 -> x0, waiting for transfers between devices: 277 us -> none  [the longest x1 207 us: local(): lax.all_gather(frozen_weight, 'fsdp', axis=0, tiled=True)]
    psum x1 -> x0, blocking collectives: 143 us -> none  [local(): counts = lax.psum(jnp.sum(onehot, axis=0), 'dp')]
    all_to_all x0 -> x2, blocking collectives: none -> 55 us  [the longest x1 28.5 us: local(): lax.all_to_all(grads, 'dp', 0, 0, tiled=True)]
    all_to_all x0 -> x1, waiting for transfers between devices: none -> 36.9 us  [local(): recv = lax.all_to_all(send, 'dp', 0, 0, tiled=True)]
    psum x1, waiting for transfers between devices: 69.4 us -> 47.6 us  [local(): lax.psum(dense, 'fsdp')]
    unnamed x0 -> x1, blocking collectives: none -> 20 us
    unnamed x19 -> x20, local copies, waits for them, and re-layouts: 9.95 us -> 22.6 us
  transfers between devices with their start and end apart: 5 -> 3, of which waited for: 4 -> 3; matrix products, arithmetic and copies ran while one was open for 1% -> 10% of each run, Pallas kernels for 0% -> 0%
where the time goes in v1:
time: 301 us; the launch traced here: 299 us
  waiting for transfers between devices  91.5 us (30%)
  blocking collectives  86.9 us (29%)
  local copies, waits for them, and re-layouts  61.7 us (20%)
  other arithmetic  19.3 us (6%)
  between operations  18.8 us (6%)
  matrix products  15 us (5%)
  starting transfers between devices  6.06 us (2%)
    psum x1, waiting for transfers between devices, local(): lax.psum(dense, 'fsdp')  47.6 us
    all_to_all x1, waiting for transfers between devices, local(): recv = lax.all_to_all(send, 'dp', 0, 0, tiled=True)  36.9 us
    all_to_all x1, blocking collectives, local(): lax.all_to_all(grads, 'dp', 0, 0, tiled=True)  28.5 us
    all_to_all x1, blocking collectives, local(): x_slice = lax.all_to_all(x_split, 'fsdp', 0, 0, tiled=True)  26.6 us
    unnamed x20, local copies, waits for them, and re-layouts  22.6 us
    unnamed x1, blocking collectives  20 us
    psum x1, blocking collectives, local(): errdiff = lax.psum(partial_err, 'fsdp') / sample_rows  11.9 us
    reduce_scatter x1, waiting for transfers between devices, local(): lax.psum_scatter(partial, 'fsdp', scatter_dimension=0, tiled=True)  6.89 us
  transfers between devices with their start and end apart: 3, of which 3 were waited for; matrix products, arithmetic and copies ran while one was open for 10% of the time, Pallas kernels for 0%

profile of v1, /device:TPU:32, one launch (start us, length us, event | category | flops | bytes accessed | tf_op | source)
XLA Modules:
  0.0 299.2 jit_solution(16782055142274667343)
XLA Ops:
  7.2 2.9 reshape.156
  10.2 1.2 copy.65
  11.3 26.6 %all_to_all.15 = bf16[4,1,2,64,608]{4,3,2,1,0:T(8,128)(2,1)S(1)} all-to-all(bf16[4,1,2,64,608]{4,3,2,1,0:T(8,128)(2,1)S(1)} %copy.65), channel_id=1, replica_groups=mesh['dp'=64,'fsdp'=4] {'fsdp'}, dimensions={0} | all-to-all | bytes 1245184 | tf_op jit(solution)/shard_map/all_to_all | solution.py:35
  37.9 4.4 %fusion = f32[4,128,2432]{2,1,0:T(8,128)} fusion(bf16[4,128,608]{2,1,0:T(8,128)(2,1)S(1)} %bitcast.85, bf16[608,2432]{1,0:T(8,128)(2,1)S(1)} %copy-done), kind=kOutput, calls=%fused_computation.4 | convolution fusion | flops 1514143744 | bytes 8560640 | tf_op jit(solution)/shard_map/dot_general | solution.py:36
  43.0 0.1 copy-done.1
  43.4 0.6 dynamic-slice
  44.0 0.8 dynamic-update-slice
  44.7 20.0 %all-reduce = s32[64]{0:T(128)S(1)} all-reduce(s32[64]{0:T(128)S(1)} %dynamic-update-slice), channel_id=1, replica_groups=mesh['dp'=64,'fsdp'=4] {'dp'}, use_global_device_ids=true, to_apply=%add | all-reduce | flops 64 | bytes 512
  64.7 0.4 pad_maximum_fusion
  65.1 4.0 %gather_fusion = bf16[64,2,64,38]{2,1,3,0:T(2,128)(2,1)} fusion(bf16[7,2,64,38]{2,1,3,0:T(2,128)(2,1)S(1)} %pad_maximum_fusion, s32[1024]{0:T(1024)S(1)} %pad_clamp_fusion), kind=kCustom, calls=%fused_computation | custom fusion | bytes 1245440 | tf_op jit(solution)/shard_map/jit(_take)/gather | solution.py:26
  69.1 3.6 %fusion.17 = bf16[64,1,38,2,64]{4,3,2,1,0:T(2,128)(2,1)} fusion(bf16[64,2,64,38]{2,1,3,0:T(2,128)(2,1)} %gather_fusion, pred[64]{0:T(512)(128)(4,1)S(1)} %compare_and_fusion), kind=kLoop, calls=%fused_computation.42 | loop fusion | flops 311296 | bytes 1245248
  72.7 4.2 %reshape.179 = bf16[64,2,2432]{2,1,0:T(2,128)(2,1)} reshape(bf16[64,1,38,2,64]{4,3,2,1,0:T(2,128)(2,1)} %fusion.17) | data formatting | bytes 1245184
  77.0 5.8 %all-to-all-start = ((bf16[64,2,2432]{2,1,0:T(2,128)(2,1)}), bf16[64,2,2432]{2,1,0:T(2,128)(2,1)}, u32[]{:S(2)}, u32[]{:S(2)}) async-start(bf16[64,2,2432]{2,1,0:T(2,128)(2,1)} %reshape.179), calls=%async_computation | async-start | bytes 1245184 | tf_op jit(solution)/shard_map/all_to_all | solution.py:27
  82.8 0.2 all-reduce.3.cloned.1.call-start
  83.8 0.6 fusion.14
  84.4 36.9 %all-to-all-done = bf16[64,2,2432]{2,1,0:T(2,128)(2,1)} async-done(((bf16[64,2,2432]{2,1,0:T(2,128)(2,1)}), bf16[64,2,2432]{2,1,0:T(2,128)(2,1)}, u32[]{:S(2)}, u32[]{:S(2)}) %all-to-all-start) | async-done | bytes 622624 | tf_op jit(solution)/shard_map/all_to_all | solution.py:27
  121.3 4.2 %reshape.180 = bf16[64,1,38,2,64]{4,3,2,1,0:T(2,128)(2,1)} reshape(bf16[64,2,2432]{2,1,0:T(2,128)(2,1)} %all-to-all-done) | data formatting | bytes 1245184
  125.5 5.2 %fusion.15 = (bf16[1,1,64,2432]{2,1,3,0:T(2,128)(2,1)}, bf16[1,1,64,2432]{2,1,3,0:T(2,128)(2,1)}) fusion(bf16[1,2,64,2432]{2,1,3,0:T(2,128)(2,1)} %bitcast.79), kind=kLoop, calls=%fused_computation.39 | loop fusion | bytes 1245184 | tf_op jit(solution)/shard_map/slice | solution.py:32
  130.7 2.5 copy.80
  133.2 1.8 convolution_convert_fusion.1
  135.1 1.4 convolution_multiply_fusion.2
  136.5 6.9 %reduce-scatter.2.cloned.1.call-done = f32[1,128,2432]{2,1,0:T(8,128)} async-done(((f32[4,128,2432]{2,1,0:T(8,128)}), f32[1,128,2432]{2,1,0:T(8,128)}) %reduce-scatter.2.cloned.1.call-update) | async-done | bytes 1245200 | tf_op jit(solution)/shard_map/reduce_scatter | solution.py:41
  143.4 3.9 %fusion.4 = (f32[2]{0:T(128)S(1)}, bf16[2,64,2432]{2,1,0:T(8,128)(2,1)}) fusion(f32[1,2,64,2432]{3,2,1,0:T(8,128)} %bitcast.78, f32[1,2,64,2432]{3,2,1,0:T(8,128)} %bitcast.83, bf16[1,2,64,2432]{3,2,1,0:T(8,128)(2,1)} %param.9, f32[128,2432]{1,0:T(8,128)} %convolution_multiply_fusion.2, f32[1,128,2432]{2,1,0:T(8,128)} %reduce-scatter.2.cloned.1.call-done), kind=kLoop, calls=%fused_computation.11 | loop fusion | flops 2801662 | bytes 6225928 | tf_op jit(solution)/shard_map/reduce_sum | solution.py:54
  147.3 11.9 %psum.14 = f32[1,2]{1,0:T(1,128)S(1)} all-reduce(f32[1,2]{1,0:T(1,128)S(1)} %bitcast.89), channel_id=1, replica_groups=mesh['dp'=64,'fsdp'=4] {'fsdp'}, use_global_device_ids=true, to_apply=%region_2.3 | all-reduce | flops 2 | bytes 16 | tf_op jit(solution)/shard_map/psum | solution.py:58
  159.1 0.6 fusion.16
  161.8 3.0 %fusion.2 = f32[64,2432]{1,0:T(8,128)} fusion(bf16[2,64,2432]{2,1,0:T(8,128)(2,1)} %get-tuple-element.21, bf16[1,2,64,2432]{3,2,1,0:T(8,128)(2,1)} %param.8, f32[2]{0:T(128)S(1)} %multiply_multiply_fusion, bf16[1,1,64,2432]{3,2,1,0:T(8,128)(2,1)S(1)} %copy.80), kind=kOutput, calls=%fused_computation.9 | convolution fusion | flops 80166912 | bytes 2179080 | tf_op jit(solution)/shard_map/pktr,pktd->pkrd/dot_general | solution.py:74
  164.8 1.9 broadcast_multiply_fusion.1
  166.8 2.5 copy.68
  169.3 2.4 mul.102
  171.7 1.4 fusion.3
  173.1 0.9 broadcast_multiply_fusion
  174.0 2.5 copy.70
  176.6 2.4 mul.105
  179.0 1.9 maximum_bitcast_fusion
  180.9 3.4 %copy.86 = f32[64,1,2,64,38]{3,2,4,1,0:T(2,128)} copy(f32[64,1,2,64,38]{3,4,0,2,1:T(8,128)S(1)} %maximum_bitcast_fusion) | data formatting | bytes 2490368 | tf_op jit(solution)/shard_map/transpose | solution.py:83
  184.3 4.7 %reshape.181 = f32[64,1,4864]{2,1,0:T(1,128)} reshape(f32[64,1,38,2,64]{4,3,2,1,0:T(2,128)} %bitcast.80) | data formatting | bytes 2490368
  188.9 28.5 %all_to_all.16 = f32[64,1,4864]{2,1,0:T(1,128)} all-to-all(f32[64,1,4864]{2,1,0:T(1,128)} %reshape.181), channel_id=1, replica_groups=mesh['dp'=64,'fsdp'=4] {'dp'}, dimensions={0} | all-to-all | bytes 2490368 | tf_op jit(solution)/shard_map/all_to_all | solution.py:84
  217.4 0.5 broadcast.97
  217.9 6.0 %reduce.6 = f32[64,4864]{1,0:T(8,128)} reduce(f32[64,1,4864]{2,1,0:T(1,128)} %all_to_all.16, f32[]{:T(128)} %broadcast.97), dimensions={1}, to_apply=%all_to_all.11.reduce_sub_computation | reduce | bytes 2490372 | tf_op jit(solution)/shard_map/all_to_all | solution.py:84
  223.8 3.8 %reshape.182 = f32[64,1,38,2,64]{4,3,2,1,0:T(2,128)} reshape(f32[64,4864]{1,0:T(8,128)} %reduce.6) | data formatting | bytes 2490368
  227.7 5.4 %copy.72 = f32[64,1,2,64,38]{0,4,3,2,1:T(8,128)} copy(f32[64,1,2,64,38]{3,2,4,1,0:T(2,128)} %bitcast.81) | data formatting | bytes 2490368 | tf_op jit(solution)/shard_map/all_to_all | solution.py:84
  233.0 3.4 %reshape.161 = f32[64,4864]{0,1:T(8,128)} reshape(f32[64,1,2,64,38]{0,4,3,2,1:T(8,128)} %copy.72) | data formatting | bytes 2490368 | tf_op jit(solution)/shard_map/reshape | solution.py:84
  236.4 3.0 %fusion.12 = f32[7,4864]{1,0:T(8,128)S(1)} fusion(f32[64,4864]{0,1:T(8,128)} %reshape.161, s32[64]{0:T(128)S(1)} %all-reduce), kind=kOutput, calls=%fused_computation.31 | convolution fusion | flops 26149312 | bytes 1381632 | tf_op jit(solution)/shard_map/dot_general | solution.py:87
  239.4 1.3 reshape.162
  240.9 47.6 %all-reduce.3.cloned.1.call-done = f32[7,2,64,38]{3,2,1,0:T(8,128)} async-done(((f32[7,2,64,38]{3,2,1,0:T(8,128)}), f32[7,2,64,38]{3,2,1,0:T(8,128)}) %all-reduce.3.cloned.1.call-update) | async-done | bytes 136208 | tf_op jit(solution)/shard_map/psum | solution.py:88
  288.5 1.1 slice_bitcast_fusion
  289.6 0.8 copy.73
  290.4 0.8 copy.74
  (22 shorter events, 0.5 us)
Async XLA Ops:
  7.2 30.7 %copy-start = (bf16[608,2432]{1,0:T(8,128)(2,1)S(1)}, bf16[608,2432]{1,0:T(8,128)(2,1)}, u32[]{:S(2)}) copy-start(bf16[608,2432]{1,0:T(8,128)(2,1)} %param.10) | copy-start | bytes 8871940
  7.2 136.2 %reduce-scatter.2.cloned.1.call-start = ((), (), s32[]{:S(2)}) async-start(), calls=%async_computation.4 | async-start | bytes 6225920 | tf_op jit(solution)/shard_map/reduce_scatter | solution.py:41
  42.3 0.9 copy-start.1
  42.3 1.0 copy-start.2
  42.3 1.1 copy-start.3
  77.0 44.3 %all-to-all-start = ((bf16[64,2,2432]{2,1,0:T(2,128)(2,1)}), bf16[64,2,2432]{2,1,0:T(2,128)(2,1)}, u32[]{:S(2)}, u32[]{:S(2)}) async-start(bf16[64,2,2432]{2,1,0:T(2,128)(2,1)} %reshape.179), calls=%async_computation | async-start | bytes 1245184 | tf_op jit(solution)/shard_map/all_to_all | solution.py:27
  82.8 205.8 %all-reduce.3.cloned.1.call-start = ((), (), s32[]{:S(2)}) async-start(), calls=%async_computation.5 | async-start | bytes 917504 | tf_op jit(solution)/shard_map/psum | solution.py:88
  143.4 18.4 %copy-start.4 = (f32[2]{0:T(128)S(1)}, f32[2]{0:T(128)}, u32[]{:S(2)}) copy-start(f32[2]{0:T(128)} %constant.42.clone) | copy-start | bytes 28
Sparse Core Ops, SparseCore 0:
  42.4 100.9 reduce-scatter.1
  240.9 47.5 all-reduce.2

commit v2 on v1

--- a/solution.py
+++ b/solution.py
@@ -6,6 +6,13 @@
 ADAPTER_SCALE = 0.5
 BETA = 1.0
 LOSS_SCALE = 64.0
+
+
+def fsdp_sum(value, fsdp_size):
+    if fsdp_size != 4:
+        return lax.psum(value, "fsdp")
+    value = value + lax.ppermute(value, "fsdp", [(0, 1), (1, 0), (2, 3), (3, 2)])
+    return value + lax.ppermute(value, "fsdp", [(0, 3), (3, 0), (1, 2), (2, 1)])
 
 
 def local(latents, targets, frozen_weight, adapter_down, adapter_up, categories, timesteps):
@@ -24,6 +31,7 @@
 
     both = jnp.stack([adapter_down, adapter_up], axis=1)
     send = jnp.take(both, cats_all.reshape(dp_size, pair_local), axis=0)
+    send, latents = lax.optimization_barrier((send, latents))
     recv = lax.all_to_all(send, "dp", 0, 0, tiled=True)
     selected = recv.transpose(1, 2, 3, 0, 4).reshape(
         pair_local, 2, adapter_rank_width, dp_size * col_local
@@ -38,9 +46,9 @@
         frozen_weight,
         preferred_element_type=jnp.float32,
     ).reshape(fsdp_size, pair_local * 2 * row_local, feat_width)
-    base_out = lax.psum_scatter(partial, "fsdp", scatter_dimension=0, tiled=True).reshape(
-        pair_local, 2, row_local, feat_width
-    )
+    base_out = lax.psum_scatter(
+        partial.astype(jnp.bfloat16), "fsdp", scatter_dimension=0, tiled=True
+    ).astype(jnp.float32).reshape(pair_local, 2, row_local, feat_width)
 
     grouped = latents.reshape(pair_local, 2 * row_local, feat_width)
     hidden_state = jnp.einsum(
@@ -85,7 +93,7 @@
         dp_size * pair_local, 2 * adapter_rank_width * col_local
     )
     dense = jnp.dot(onehot_all.T, gathered, precision=lax.Precision.HIGHEST)
-    dense = lax.psum(dense, "fsdp").reshape(class_total, 2, adapter_rank_width, col_local)
+    dense = fsdp_sum(dense, fsdp_size).reshape(class_total, 2, adapter_rank_width, col_local)
     grad_down = dense[:, 0]
     grad_up = dense[:, 1]
     return (grad_down, grad_up, losses)

time: 301 us -> 258 us (0.86)
  waiting for transfers between devices: 91.5 us -> 43.7 us
  blocking collectives: 86.9 us -> 79.4 us
  local copies, waits for them, and re-layouts: 61.7 us -> 68.6 us
  starting transfers between devices: 6.06 us -> 12 us
    psum x1 -> x0, waiting for transfers between devices: 47.6 us -> none  [local(): lax.psum(dense, 'fsdp')]
    ppermute x0 -> x2, waiting for transfers between devices: none -> 13.7 us  [the longest x1 7.74 us: fsdp_sum(): return value + lax.ppermute(value, 'fsdp', [(0, 3), (3, 0), (1, 2), (2, 1)])]
    reduce_scatter x1, waiting for transfers between devices: 6.89 us -> 0.01 us  [local(): lax.psum_scatter(partial.astype(jnp.bfloat16), 'fsdp', scatter_dimension=...]
    all_to_all x1, waiting for transfers between devices: 36.9 us -> 30 us  [local(): recv = lax.all_to_all(send, 'dp', 0, 0, tiled=True)]
    ppermute x0 -> x2, starting transfers between devices: none -> 5.65 us  [the longest x1 3.46 us: fsdp_sum(): return value + lax.ppermute(value, 'fsdp', [(0, 3), (3, 0), (1, 2), (2, 1)])]
    unnamed x20 -> x15, local copies, waits for them, and re-layouts: 22.6 us -> 28.2 us
    unnamed x1 -> x0, other arithmetic: 3.58 us -> none
    select_n x1 -> x2, other arithmetic: 0.01 us -> 3.58 us  [local(): send = jnp.take(both, cats_all.reshape(dp_size, pair_local), axis=0)]
  transfers between devices with their start and end apart: 3 -> 4, of which waited for: 3 -> 3; matrix products, arithmetic and copies ran while one was open for 10% -> 9% of each run, Pallas kernels for 0% -> 0%
where the time goes in v2:
time: 258 us; the launch traced here: 257 us
  blocking collectives  79.4 us (31%)
  local copies, waits for them, and re-layouts  68.6 us (27%)
  waiting for transfers between devices  43.7 us (17%)
  other arithmetic  19.6 us (8%)
  between operations  18.9 us (7%)
  matrix products  14.4 us (6%)
  starting transfers between devices  12 us (5%)
    all_to_all x1, waiting for transfers between devices, local(): recv = lax.all_to_all(send, 'dp', 0, 0, tiled=True)  30 us
    unnamed x15, local copies, waits for them, and re-layouts  28.2 us
    all_to_all x1, blocking collectives, local(): lax.all_to_all(grads, 'dp', 0, 0, tiled=True)  25.8 us
    all_to_all x1, blocking collectives, local(): x_slice = lax.all_to_all(x_split, 'fsdp', 0, 0, tiled=True)  23.6 us
    unnamed x1, blocking collectives  18.6 us
    psum x1, blocking collectives, local(): errdiff = lax.psum(partial_err, 'fsdp') / sample_rows  11.4 us
    ppermute x1, waiting for transfers between devices, fsdp_sum(): return value + lax.ppermute(value, 'fsdp', [(0, 3), (3, 0), (1, 2), (2, 1)])  7.74 us
    all_to_all x1, starting transfers between devices, local(): recv = lax.all_to_all(send, 'dp', 0, 0, tiled=True)  6.29 us
  transfers between devices with their start and end apart: 4, of which 3 were waited for; matrix products, arithmetic and copies ran while one was open for 9% of the time, Pallas kernels for 0%

profile of v2, /device:TPU:32, one launch (start us, length us, event | category | flops | bytes accessed | tf_op | source)
XLA Modules:
  0.0 256.5 jit_solution(13606634665351997470)
XLA Ops:
  8.0 1.3 dynamic-slice
  9.3 0.8 dynamic-update-slice
  10.1 18.6 %all-reduce = s32[64]{0:T(128)S(1)} all-reduce(s32[64]{0:T(128)S(1)} %dynamic-update-slice), channel_id=1, replica_groups=mesh['dp'=64,'fsdp'=4] {'dp'}, use_global_device_ids=true, to_apply=%add | all-reduce | flops 64 | bytes 512
  28.7 1.0 copy.61
  29.7 1.0 copy.62
  31.1 4.0 %gather_fusion = bf16[64,2,64,38]{2,1,3,0:T(2,128)(2,1)} fusion(bf16[7,2,64,38]{2,1,3,0:T(2,128)(2,1)S(1)} %pad_maximum_fusion, s32[1024]{0:T(1024)S(1)} %pad_clamp_fusion), kind=kCustom, calls=%fused_computation | custom fusion | bytes 1245440 | tf_op jit(solution)/shard_map/jit(_take)/gather | solution.py:33
  35.1 3.6 %broadcast_select_fusion = bf16[64,1,2,64,38]{3,2,4,0,1:T(2,128)(2,1)} fusion(pred[64]{0:T(512)(128)(4,1)S(1)} %compare_and_fusion, bf16[64,2,64,38]{2,1,3,0:T(2,128)(2,1)} %gather_fusion), kind=kLoop, calls=%fused_computation.7 | loop fusion | flops 311296 | bytes 1245248 | tf_op jit(solution)/shard_map/jit(_take)/select_n | solution.py:33
  38.7 2.8 %reshape.159 = bf16[1,2,64,4,608]{4,3,2,1,0:T(4,128)(2,1)} reshape(bf16[1,2,64,2432]{3,2,1,0:T(8,128)(2,1)} %param.8) | data formatting | bytes 1245184 | tf_op jit(solution)/shard_map/reshape | solution.py:42
  41.5 1.2 copy.66
  42.7 23.6 %all_to_all.15 = bf16[4,1,2,64,608]{4,3,2,1,0:T(8,128)(2,1)S(1)} all-to-all(bf16[4,1,2,64,608]{4,3,2,1,0:T(8,128)(2,1)S(1)} %copy.66), channel_id=1, replica_groups=mesh['dp'=64,'fsdp'=4] {'fsdp'}, dimensions={0} | all-to-all | bytes 1245184 | tf_op jit(solution)/shard_map/all_to_all | solution.py:43
  66.2 3.6 %convolution_convert_fusion = bf16[4,128,2432]{2,1,0:T(8,128)(2,1)} fusion(bf16[4,128,608]{2,1,0:T(8,128)(2,1)S(1)} %bitcast.79, bf16[608,2432]{1,0:T(8,128)(2,1)S(1)} %copy-done), kind=kOutput, calls=%fused_computation.1 | convolution fusion | flops 1515388928 | bytes 6070272 | tf_op jit(solution)/shard_map/dot_general | solution.py:44
  69.9 3.2 %bitcast_bitcast_fusion = bf16[64,1,38,2,64]{4,3,2,1,0:T(2,128)(2,1)} fusion(bf16[64,1,2,64,38]{3,2,4,0,1:T(2,128)(2,1)} %broadcast_select_fusion), kind=kLoop, calls=%fused_computation.41 | loop fusion | bytes 1245184
  73.1 4.2 %reshape.185 = bf16[64,2,2432]{2,1,0:T(2,128)(2,1)} reshape(bf16[64,1,38,2,64]{4,3,2,1,0:T(2,128)(2,1)} %bitcast_bitcast_fusion) | data formatting | bytes 1245184
  77.3 6.3 %all-to-all-start = ((bf16[64,2,2432]{2,1,0:T(2,128)(2,1)}), bf16[64,2,2432]{2,1,0:T(2,128)(2,1)}, u32[]{:S(2)}, u32[]{:S(2)}) async-start(bf16[64,2,2432]{2,1,0:T(2,128)(2,1)} %reshape.185), calls=%async_computation | async-start | bytes 1245184 | tf_op jit(solution)/shard_map/all_to_all | solution.py:35
  84.9 30.0 %all-to-all-done = bf16[64,2,2432]{2,1,0:T(2,128)(2,1)} async-done(((bf16[64,2,2432]{2,1,0:T(2,128)(2,1)}), bf16[64,2,2432]{2,1,0:T(2,128)(2,1)}, u32[]{:S(2)}, u32[]{:S(2)}) %all-to-all-start) | async-done | bytes 622624 | tf_op jit(solution)/shard_map/all_to_all | solution.py:35
  115.0 4.2 %reshape.186 = bf16[64,1,38,2,64]{4,3,2,1,0:T(2,128)(2,1)} reshape(bf16[64,2,2432]{2,1,0:T(2,128)(2,1)} %all-to-all-done) | data formatting | bytes 1245184
  119.1 5.0 %fusion.13 = (bf16[1,1,64,2432]{2,1,3,0:T(2,128)(2,1)}, bf16[1,1,64,2432]{2,1,3,0:T(2,128)(2,1)}) fusion(bf16[1,2,64,2432]{2,1,3,0:T(2,128)(2,1)} %bitcast.73), kind=kLoop, calls=%fused_computation.38 | loop fusion | bytes 1245184 | tf_op jit(solution)/shard_map/slice | solution.py:40
  124.2 2.5 copy.81
  126.7 1.9 convolution_convert_fusion.2
  128.7 1.4 convolution_multiply_fusion.2
  130.1 3.5 %fusion.3 = (f32[2]{0:T(128)S(1)}, bf16[2,64,2432]{2,1,0:T(8,128)(2,1)}) fusion(f32[1,2,64,2432]{3,2,1,0:T(8,128)} %bitcast.72, bf16[1,2,64,2432]{3,2,1,0:T(8,128)(2,1)} %param.9, bf16[1,2,64,2432]{3,2,1,0:T(8,128)(2,1)} %bitcast.78, f32[128,2432]{1,0:T(8,128)} %convolution_multiply_fusion.2, bf16[1,128,2432]{2,1,0:T(8,128)(2,1)} %reduce-scatter.2.cloned.1.call-done), kind=kLoop, calls=%fused_computation.11 | loop fusion | flops 3424254 | bytes 4980744 | tf_op jit(solution)/shard_map/reduce_sum | solution.py:62
  133.6 11.4 %psum.7 = f32[1,2]{1,0:T(1,128)S(1)} all-reduce(f32[1,2]{1,0:T(1,128)S(1)} %bitcast.82), channel_id=1, replica_groups=mesh['dp'=64,'fsdp'=4] {'fsdp'}, use_global_device_ids=true, to_apply=%region_2.3 | all-reduce | flops 2 | bytes 16 | tf_op jit(solution)/shard_map/psum | solution.py:66
  147.7 3.0 %fusion.1 = f32[64,2432]{1,0:T(8,128)} fusion(bf16[2,64,2432]{2,1,0:T(8,128)(2,1)} %get-tuple-element.25, bf16[1,2,64,2432]{3,2,1,0:T(8,128)(2,1)} %param.8, f32[2]{0:T(128)S(1)} %multiply_multiply_fusion, bf16[1,1,64,2432]{3,2,1,0:T(8,128)(2,1)S(1)} %copy.81), kind=kOutput, calls=%fused_computation.9 | convolution fusion | flops 80166912 | bytes 2179080 | tf_op jit(solution)/shard_map/pktr,pktd->pkrd/dot_general | solution.py:82
  150.8 2.0 broadcast_multiply_fusion.1
  152.7 2.5 copy.69
  155.2 2.4 mul.102
  157.6 1.4 fusion.2
  159.1 0.9 broadcast_multiply_fusion
  160.0 2.5 copy.71
  162.5 2.4 mul.105
  164.9 1.9 maximum_bitcast_fusion
  166.8 3.4 %copy.87 = f32[64,1,2,64,38]{3,2,4,1,0:T(2,128)} copy(f32[64,1,2,64,38]{3,4,0,2,1:T(8,128)S(1)} %maximum_bitcast_fusion) | data formatting | bytes 2490368 | tf_op jit(solution)/shard_map/transpose | solution.py:91
  170.2 4.7 %reshape.187 = f32[64,1,4864]{2,1,0:T(1,128)} reshape(f32[64,1,38,2,64]{4,3,2,1,0:T(2,128)} %bitcast.74) | data formatting | bytes 2490368
  174.9 25.8 %all_to_all.16 = f32[64,1,4864]{2,1,0:T(1,128)} all-to-all(f32[64,1,4864]{2,1,0:T(1,128)} %reshape.187), channel_id=1, replica_groups=mesh['dp'=64,'fsdp'=4] {'dp'}, dimensions={0} | all-to-all | bytes 2490368 | tf_op jit(solution)/shard_map/all_to_all | solution.py:92
  201.2 6.0 %reduce.6 = f32[64,4864]{1,0:T(8,128)} reduce(f32[64,1,4864]{2,1,0:T(1,128)} %all_to_all.16, f32[]{:T(128)} %broadcast.97), dimensions={1}, to_apply=%all_to_all.11.reduce_sub_computation | reduce | bytes 2490372 | tf_op jit(solution)/shard_map/all_to_all | solution.py:92
  207.1 3.8 %reshape.188 = f32[64,1,38,2,64]{4,3,2,1,0:T(2,128)} reshape(f32[64,4864]{1,0:T(8,128)} %reduce.6) | data formatting | bytes 2490368
  211.0 5.4 %copy.73 = f32[64,1,2,64,38]{0,4,3,2,1:T(8,128)} copy(f32[64,1,2,64,38]{3,2,4,1,0:T(2,128)} %bitcast.75) | data formatting | bytes 2490368 | tf_op jit(solution)/shard_map/all_to_all | solution.py:92
  216.3 3.4 %reshape.165 = f32[64,4864]{0,1:T(8,128)} reshape(f32[64,1,2,64,38]{0,4,3,2,1:T(8,128)} %copy.73) | data formatting | bytes 2490368 | tf_op jit(solution)/shard_map/reshape | solution.py:92
  219.7 3.0 %fusion.10 = f32[7,4864]{1,0:T(8,128)S(1)} fusion(f32[64,4864]{0,1:T(8,128)} %reshape.165, s32[64]{0:T(128)S(1)} %all-reduce), kind=kOutput, calls=%fused_computation.30 | convolution fusion | flops 26149312 | bytes 1381632 | tf_op jit(solution)/shard_map/dot_general | solution.py:95
  222.7 2.2 collective-permute-start
  224.9 5.9 %collective-permute-done = f32[7,4864]{1,0:T(8,128)S(1)} collective-permute-done((f32[7,4864]{1,0:T(8,128)S(1)}, f32[7,4864]{1,0:T(8,128)S(1)}, u32[]{:S(2)}, u32[]{:S(2)}) %collective-permute-start) | collective-permute-done | bytes 136224 | tf_op jit(solution)/shard_map/ppermute | solution.py:14
  230.8 3.5 %collective-permute-start.1 = (f32[7,4864]{1,0:T(8,128)S(1)}, f32[7,4864]{1,0:T(8,128)S(1)}, u32[]{:S(2)}, u32[]{:S(2)}) collective-permute-start(f32[7,4864]{1,0:T(8,128)S(1)} %add.41), channel_id=1, source_target_pairs={{0,3},{3,0},{1,2},{2,1},{4,7},{7,4},{5,6},{6,5},{8,11},{11,8},{9,1... | collective-permute-start | bytes 408584 | tf_op jit(solution)/shard_map/ppermute | solution.py:15
  234.4 7.7 %collective-permute-done.1 = f32[7,4864]{1,0:T(8,128)S(1)} collective-permute-done((f32[7,4864]{1,0:T(8,128)S(1)}, f32[7,4864]{1,0:T(8,128)S(1)}, u32[]{:S(2)}, u32[]{:S(2)}) %collective-permute-start.1) | collective-permute-done | bytes 136224 | tf_op jit(solution)/shard_map/ppermute | solution.py:15
  242.1 0.7 add.42
  242.8 1.4 reshape.166
  244.3 0.8 slice_bitcast_fusion
  245.1 1.7 copy.74
  246.8 1.7 copy.75
  (20 shorter events, 2.4 us)
Async XLA Ops:
  7.2 59.1 %copy-start = (bf16[608,2432]{1,0:T(8,128)(2,1)S(1)}, bf16[608,2432]{1,0:T(8,128)(2,1)}, u32[]{:S(2)}) copy-start(bf16[608,2432]{1,0:T(8,128)(2,1)} %param.10) | copy-start | bytes 8871940
  7.2 122.9 %reduce-scatter.2.cloned.1.call-start = ((), (), s32[]{:S(2)}) async-start(), calls=%async_computation.4 | async-start | bytes 3112960 | tf_op jit(solution)/shard_map/reduce_scatter | solution.py:49
  77.3 37.7 %all-to-all-start = ((bf16[64,2,2432]{2,1,0:T(2,128)(2,1)}), bf16[64,2,2432]{2,1,0:T(2,128)(2,1)}, u32[]{:S(2)}, u32[]{:S(2)}) async-start(bf16[64,2,2432]{2,1,0:T(2,128)(2,1)} %reshape.185), calls=%async_computation | async-start | bytes 1245184 | tf_op jit(solution)/shard_map/all_to_all | solution.py:35
  130.1 17.6 %copy-start.1 = (f32[2]{0:T(128)S(1)}, f32[2]{0:T(128)}, u32[]{:S(2)}) copy-start(f32[2]{0:T(128)} %constant.42.clone) | copy-start | bytes 28
  222.7 8.1 %collective-permute-start = (f32[7,4864]{1,0:T(8,128)S(1)}, f32[7,4864]{1,0:T(8,128)S(1)}, u32[]{:S(2)}, u32[]{:S(2)}) collective-permute-start(f32[7,4864]{1,0:T(8,128)S(1)} %fusion.10), channel_id=1, source_target_pairs={{0,1},{1,0},{2,3},{3,2},{4,5},{5,4},{6,7},{7,6},{8,9},{9,8},{10,11... | collective-permute-start | bytes 408584 | tf_op jit(solution)/shard_map/ppermute | solution.py:14
  230.8 11.3 %collective-permute-start.1 = (f32[7,4864]{1,0:T(8,128)S(1)}, f32[7,4864]{1,0:T(8,128)S(1)}, u32[]{:S(2)}, u32[]{:S(2)}) collective-permute-start(f32[7,4864]{1,0:T(8,128)S(1)} %add.41), channel_id=1, source_target_pairs={{0,3},{3,0},{1,2},{2,1},{4,7},{7,4},{5,6},{6,5},{8,11},{11,8},{9,1... | collective-permute-start | bytes 408584 | tf_op jit(solution)/shard_map/ppermute | solution.py:15
Sparse Core Ops, SparseCore 0:
  70.0 54.8 reduce-scatter.1

commit v3 on v2

--- a/solution.py
+++ b/solution.py
@@ -46,9 +46,9 @@
         frozen_weight,
         preferred_element_type=jnp.float32,
     ).reshape(fsdp_size, pair_local * 2 * row_local, feat_width)
-    base_out = lax.psum_scatter(
-        partial.astype(jnp.bfloat16), "fsdp", scatter_dimension=0, tiled=True
-    ).astype(jnp.float32).reshape(pair_local, 2, row_local, feat_width)
+    base_out = lax.psum_scatter(partial, "fsdp", scatter_dimension=0, tiled=True).reshape(
+        pair_local, 2, row_local, feat_width
+    )
 
     grouped = latents.reshape(pair_local, 2 * row_local, feat_width)
     hidden_state = jnp.einsum(

time: 258 us -> 298 us (1.16)
  waiting for transfers between devices: 43.7 us -> 78.7 us
  blocking collectives: 79.4 us -> 83.6 us
    reduce_scatter x1, waiting for transfers between devices: 0.01 us -> 28.9 us  [local(): lax.psum_scatter(partial, 'fsdp', scatter_dimension=0, tiled=True)]
    all_to_all x1, waiting for transfers between devices: 30 us -> 36.3 us  [local(): recv = lax.all_to_all(send, 'dp', 0, 0, tiled=True)]
    all_to_all x1, blocking collectives: 25.8 us -> 29 us  [local(): lax.all_to_all(grads, 'dp', 0, 0, tiled=True)]
  transfers between devices with their start and end apart: 4 -> 4, of which waited for: 3 -> 4; matrix products, arithmetic and copies ran while one was open for 9% -> 8% of each run, Pallas kernels for 0% -> 0%
where the time goes in v3:
time: 298 us; the launch traced here: 296 us
  blocking collectives  83.6 us (28%)
  waiting for transfers between devices  78.7 us (26%)
  local copies, waits for them, and re-layouts  68.8 us (23%)
  other arithmetic  19.9 us (7%)
  between operations  18.9 us (6%)
  matrix products  15.1 us (5%)
  starting transfers between devices  11.1 us (4%)
    all_to_all x1, waiting for transfers between devices, local(): recv = lax.all_to_all(send, 'dp', 0, 0, tiled=True)  36.3 us
    all_to_all x1, blocking collectives, local(): lax.all_to_all(grads, 'dp', 0, 0, tiled=True)  29 us
    reduce_scatter x1, waiting for transfers between devices, local(): lax.psum_scatter(partial, 'fsdp', scatter_dimension=0, tiled=True)  28.9 us
    unnamed x15, local copies, waits for them, and re-layouts  28.2 us
    all_to_all x1, blocking collectives, local(): x_slice = lax.all_to_all(x_split, 'fsdp', 0, 0, tiled=True)  23.6 us
    unnamed x1, blocking collectives  18.6 us
    psum x1, blocking collectives, local(): errdiff = lax.psum(partial_err, 'fsdp') / sample_rows  12.3 us
    ppermute x1, waiting for transfers between devices, fsdp_sum(): return value + lax.ppermute(value, 'fsdp', [(0, 3), (3, 0), (1, 2), (2, 1)])  7.26 us
  transfers between devices with their start and end apart: 4, of which 4 were waited for; matrix products, arithmetic and copies ran while one was open for 8% of the time, Pallas kernels for 0%

profile of v3, /device:TPU:32, one launch (start us, length us, event | category | flops | bytes accessed | tf_op | source)
XLA Modules:
  0.0 296.1 jit_solution(6998492903180167699)
XLA Ops:
  8.0 1.3 dynamic-slice
  9.3 0.8 dynamic-update-slice
  10.1 18.6 %all-reduce = s32[64]{0:T(128)S(1)} all-reduce(s32[64]{0:T(128)S(1)} %dynamic-update-slice), channel_id=1, replica_groups=mesh['dp'=64,'fsdp'=4] {'dp'}, use_global_device_ids=true, to_apply=%add | all-reduce | flops 64 | bytes 512
  28.7 1.0 copy.61
  29.7 1.0 copy.62
  31.1 4.0 %gather_fusion = bf16[64,2,64,38]{2,1,3,0:T(2,128)(2,1)} fusion(bf16[7,2,64,38]{2,1,3,0:T(2,128)(2,1)S(1)} %pad_maximum_fusion, s32[1024]{0:T(1024)S(1)} %pad_clamp_fusion), kind=kCustom, calls=%fused_computation | custom fusion | bytes 1245440 | tf_op jit(solution)/shard_map/jit(_take)/gather | solution.py:33
  35.2 3.6 %broadcast_select_fusion = bf16[64,1,2,64,38]{3,2,4,0,1:T(2,128)(2,1)} fusion(pred[64]{0:T(512)(128)(4,1)S(1)} %compare_and_fusion, bf16[64,2,64,38]{2,1,3,0:T(2,128)(2,1)} %gather_fusion), kind=kLoop, calls=%fused_computation.7 | loop fusion | flops 311296 | bytes 1245248 | tf_op jit(solution)/shard_map/jit(_take)/select_n | solution.py:33
  38.7 2.8 reshape.156
  41.5 1.2 copy.66
  42.7 23.6 %all_to_all.15 = bf16[4,1,2,64,608]{4,3,2,1,0:T(8,128)(2,1)S(1)} all-to-all(bf16[4,1,2,64,608]{4,3,2,1,0:T(8,128)(2,1)S(1)} %copy.66), channel_id=1, replica_groups=mesh['dp'=64,'fsdp'=4] {'fsdp'}, dimensions={0} | all-to-all | bytes 1245184 | tf_op jit(solution)/shard_map/all_to_all | solution.py:43
  66.3 4.4 %fusion = f32[4,128,2432]{2,1,0:T(8,128)} fusion(bf16[4,128,608]{2,1,0:T(8,128)(2,1)S(1)} %bitcast.78, bf16[608,2432]{1,0:T(8,128)(2,1)S(1)} %copy-done), kind=kOutput, calls=%fused_computation.4 | convolution fusion | flops 1514143744 | bytes 8560640 | tf_op jit(solution)/shard_map/dot_general | solution.py:44
  70.6 3.2 %bitcast_bitcast_fusion = bf16[64,1,38,2,64]{4,3,2,1,0:T(2,128)(2,1)} fusion(bf16[64,1,2,64,38]{3,2,4,0,1:T(2,128)(2,1)} %broadcast_select_fusion), kind=kLoop, calls=%fused_computation.41 | loop fusion | bytes 1245184
  73.8 4.2 %reshape.179 = bf16[64,2,2432]{2,1,0:T(2,128)(2,1)} reshape(bf16[64,1,38,2,64]{4,3,2,1,0:T(2,128)(2,1)} %bitcast_bitcast_fusion) | data formatting | bytes 1245184
  78.1 6.3 %all-to-all-start = ((bf16[64,2,2432]{2,1,0:T(2,128)(2,1)}), bf16[64,2,2432]{2,1,0:T(2,128)(2,1)}, u32[]{:S(2)}, u32[]{:S(2)}) async-start(bf16[64,2,2432]{2,1,0:T(2,128)(2,1)} %reshape.179), calls=%async_computation | async-start | bytes 1245184 | tf_op jit(solution)/shard_map/all_to_all | solution.py:35
  85.8 36.3 %all-to-all-done = bf16[64,2,2432]{2,1,0:T(2,128)(2,1)} async-done(((bf16[64,2,2432]{2,1,0:T(2,128)(2,1)}), bf16[64,2,2432]{2,1,0:T(2,128)(2,1)}, u32[]{:S(2)}, u32[]{:S(2)}) %all-to-all-start) | async-done | bytes 622624 | tf_op jit(solution)/shard_map/all_to_all | solution.py:35
  122.1 4.2 %reshape.180 = bf16[64,1,38,2,64]{4,3,2,1,0:T(2,128)(2,1)} reshape(bf16[64,2,2432]{2,1,0:T(2,128)(2,1)} %all-to-all-done) | data formatting | bytes 1245184
  126.3 5.2 %fusion.14 = (bf16[1,1,64,2432]{2,1,3,0:T(2,128)(2,1)}, bf16[1,1,64,2432]{2,1,3,0:T(2,128)(2,1)}) fusion(bf16[1,2,64,2432]{2,1,3,0:T(2,128)(2,1)} %bitcast.72), kind=kLoop, calls=%fused_computation.38 | loop fusion | bytes 1245184 | tf_op jit(solution)/shard_map/slice | solution.py:40
  131.5 2.5 copy.81
  134.0 1.9 convolution_convert_fusion.1
  136.0 1.4 convolution_multiply_fusion.2
  137.4 28.9 %reduce-scatter.2.cloned.1.call-done = f32[1,128,2432]{2,1,0:T(8,128)} async-done(((f32[4,128,2432]{2,1,0:T(8,128)}), f32[1,128,2432]{2,1,0:T(8,128)}) %reduce-scatter.2.cloned.1.call-update) | async-done | bytes 1245200 | tf_op jit(solution)/shard_map/reduce_scatter | solution.py:49
  166.3 3.9 %fusion.4 = (f32[2]{0:T(128)S(1)}, bf16[2,64,2432]{2,1,0:T(8,128)(2,1)}) fusion(f32[1,2,64,2432]{3,2,1,0:T(8,128)} %bitcast.71, f32[1,2,64,2432]{3,2,1,0:T(8,128)} %bitcast.76, bf16[1,2,64,2432]{3,2,1,0:T(8,128)(2,1)} %param.9, f32[128,2432]{1,0:T(8,128)} %convolution_multiply_fusion.2, f32[1,128,2432]{2,1,0:T(8,128)} %reduce-scatter.2.cloned.1.call-done), kind=kLoop, calls=%fused_computation.11 | loop fusion | flops 2801662 | bytes 6225928 | tf_op jit(solution)/shard_map/reduce_sum | solution.py:62
  170.2 12.3 %psum.7 = f32[1,2]{1,0:T(1,128)S(1)} all-reduce(f32[1,2]{1,0:T(1,128)S(1)} %bitcast.81), channel_id=1, replica_groups=mesh['dp'=64,'fsdp'=4] {'fsdp'}, use_global_device_ids=true, to_apply=%region_2.3 | all-reduce | flops 2 | bytes 16 | tf_op jit(solution)/shard_map/psum | solution.py:66
  185.3 3.0 %fusion.2 = f32[64,2432]{1,0:T(8,128)} fusion(bf16[2,64,2432]{2,1,0:T(8,128)(2,1)} %get-tuple-element.25, bf16[1,2,64,2432]{3,2,1,0:T(8,128)(2,1)} %param.8, f32[2]{0:T(128)S(1)} %multiply_multiply_fusion, bf16[1,1,64,2432]{3,2,1,0:T(8,128)(2,1)S(1)} %copy.81), kind=kOutput, calls=%fused_computation.9 | convolution fusion | flops 80166912 | bytes 2179080 | tf_op jit(solution)/shard_map/pktr,pktd->pkrd/dot_general | solution.py:82
  188.3 1.9 broadcast_multiply_fusion.1
  190.2 2.5 copy.69
  192.8 2.4 mul.102
  195.1 1.4 fusion.3
  196.6 0.9 broadcast_multiply_fusion
  197.5 2.5 copy.71
  200.0 2.4 mul.105
  202.4 1.9 maximum_bitcast_fusion
  204.3 3.4 %copy.87 = f32[64,1,2,64,38]{3,2,4,1,0:T(2,128)} copy(f32[64,1,2,64,38]{3,4,0,2,1:T(8,128)S(1)} %maximum_bitcast_fusion) | data formatting | bytes 2490368 | tf_op jit(solution)/shard_map/transpose | solution.py:91
  207.7 4.7 %reshape.181 = f32[64,1,4864]{2,1,0:T(1,128)} reshape(f32[64,1,38,2,64]{4,3,2,1,0:T(2,128)} %bitcast.73) | data formatting | bytes 2490368
  212.4 29.0 %all_to_all.16 = f32[64,1,4864]{2,1,0:T(1,128)} all-to-all(f32[64,1,4864]{2,1,0:T(1,128)} %reshape.181), channel_id=1, replica_groups=mesh['dp'=64,'fsdp'=4] {'dp'}, dimensions={0} | all-to-all | bytes 2490368 | tf_op jit(solution)/shard_map/all_to_all | solution.py:92
  241.9 6.0 %reduce.6 = f32[64,4864]{1,0:T(8,128)} reduce(f32[64,1,4864]{2,1,0:T(1,128)} %all_to_all.16, f32[]{:T(128)} %broadcast.97), dimensions={1}, to_apply=%all_to_all.11.reduce_sub_computation | reduce | bytes 2490372 | tf_op jit(solution)/shard_map/all_to_all | solution.py:92
  247.9 3.8 %reshape.182 = f32[64,1,38,2,64]{4,3,2,1,0:T(2,128)} reshape(f32[64,4864]{1,0:T(8,128)} %reduce.6) | data formatting | bytes 2490368
  251.7 5.4 %copy.73 = f32[64,1,2,64,38]{0,4,3,2,1:T(8,128)} copy(f32[64,1,2,64,38]{3,2,4,1,0:T(2,128)} %bitcast.74) | data formatting | bytes 2490368 | tf_op jit(solution)/shard_map/all_to_all | solution.py:92
  257.1 3.4 %reshape.161 = f32[64,4864]{0,1:T(8,128)} reshape(f32[64,1,2,64,38]{0,4,3,2,1:T(8,128)} %copy.73) | data formatting | bytes 2490368 | tf_op jit(solution)/shard_map/reshape | solution.py:92
  260.4 3.0 %fusion.11 = f32[7,4864]{1,0:T(8,128)S(1)} fusion(f32[64,4864]{0,1:T(8,128)} %reshape.161, s32[64]{0:T(128)S(1)} %all-reduce), kind=kOutput, calls=%fused_computation.30 | convolution fusion | flops 26149312 | bytes 1381632 | tf_op jit(solution)/shard_map/dot_general | solution.py:95
  263.5 6.2 %collective-permute-done = f32[7,4864]{1,0:T(8,128)S(1)} collective-permute-done((f32[7,4864]{1,0:T(8,128)S(1)}, f32[7,4864]{1,0:T(8,128)S(1)}, u32[]{:S(2)}, u32[]{:S(2)}) %collective-permute-start) | collective-permute-done | bytes 136224 | tf_op jit(solution)/shard_map/ppermute | solution.py:14
  269.7 4.7 %collective-permute-start.1 = (f32[7,4864]{1,0:T(8,128)S(1)}, f32[7,4864]{1,0:T(8,128)S(1)}, u32[]{:S(2)}, u32[]{:S(2)}) collective-permute-start(f32[7,4864]{1,0:T(8,128)S(1)} %add.41), channel_id=1, source_target_pairs={{0,3},{3,0},{1,2},{2,1},{4,7},{7,4},{5,6},{6,5},{8,11},{11,8},{9,1... | collective-permute-start | bytes 408584 | tf_op jit(solution)/shard_map/ppermute | solution.py:15
  274.5 7.3 %collective-permute-done.1 = f32[7,4864]{1,0:T(8,128)S(1)} collective-permute-done((f32[7,4864]{1,0:T(8,128)S(1)}, f32[7,4864]{1,0:T(8,128)S(1)}, u32[]{:S(2)}, u32[]{:S(2)}) %collective-permute-start.1) | collective-permute-done | bytes 136224 | tf_op jit(solution)/shard_map/ppermute | solution.py:15
  281.7 0.7 add.42
  282.4 1.4 reshape.162
  283.9 0.8 slice_bitcast_fusion
  284.7 1.7 copy.74
  286.4 1.7 copy.75
  (20 shorter events, 2.5 us)
Async XLA Ops:
  7.2 59.1 %copy-start = (bf16[608,2432]{1,0:T(8,128)(2,1)S(1)}, bf16[608,2432]{1,0:T(8,128)(2,1)}, u32[]{:S(2)}) copy-start(bf16[608,2432]{1,0:T(8,128)(2,1)} %param.10) | copy-start | bytes 8871940
  7.2 159.2 %reduce-scatter.2.cloned.1.call-start = ((), (), s32[]{:S(2)}) async-start(), calls=%async_computation.4 | async-start | bytes 6225920 | tf_op jit(solution)/shard_map/reduce_scatter | solution.py:49
  78.1 44.0 %all-to-all-start = ((bf16[64,2,2432]{2,1,0:T(2,128)(2,1)}), bf16[64,2,2432]{2,1,0:T(2,128)(2,1)}, u32[]{:S(2)}, u32[]{:S(2)}) async-start(bf16[64,2,2432]{2,1,0:T(2,128)(2,1)} %reshape.179), calls=%async_computation | async-start | bytes 1245184 | tf_op jit(solution)/shard_map/all_to_all | solution.py:35
  166.3 18.9 %copy-start.1 = (f32[2]{0:T(128)S(1)}, f32[2]{0:T(128)}, u32[]{:S(2)}) copy-start(f32[2]{0:T(128)} %constant.42.clone) | copy-start | bytes 28
  263.4 6.3 %collective-permute-start = (f32[7,4864]{1,0:T(8,128)S(1)}, f32[7,4864]{1,0:T(8,128)S(1)}, u32[]{:S(2)}, u32[]{:S(2)}) collective-permute-start(f32[7,4864]{1,0:T(8,128)S(1)} %fusion.11), channel_id=1, source_target_pairs={{0,1},{1,0},{2,3},{3,2},{4,5},{5,4},{6,7},{7,6},{8,9},{9,8},{10,11... | collective-permute-start | bytes 408584 | tf_op jit(solution)/shard_map/ppermute | solution.py:14
  269.7 12.0 %collective-permute-start.1 = (f32[7,4864]{1,0:T(8,128)S(1)}, f32[7,4864]{1,0:T(8,128)S(1)}, u32[]{:S(2)}, u32[]{:S(2)}) collective-permute-start(f32[7,4864]{1,0:T(8,128)S(1)} %add.41), channel_id=1, source_target_pairs={{0,3},{3,0},{1,2},{2,1},{4,7},{7,4},{5,6},{6,5},{8,11},{11,8},{9,1... | collective-permute-start | bytes 408584 | tf_op jit(solution)/shard_map/ppermute | solution.py:15
Sparse Core Ops, SparseCore 0:
  70.8 95.5 reduce-scatter.1

commit v4 on v3

--- a/solution.py
+++ b/solution.py
@@ -31,7 +31,6 @@
 
     both = jnp.stack([adapter_down, adapter_up], axis=1)
     send = jnp.take(both, cats_all.reshape(dp_size, pair_local), axis=0)
-    send, latents = lax.optimization_barrier((send, latents))
     recv = lax.all_to_all(send, "dp", 0, 0, tiled=True)
     selected = recv.transpose(1, 2, 3, 0, 4).reshape(
         pair_local, 2, adapter_rank_width, dp_size * col_local
@@ -39,27 +38,34 @@
     selected_down = selected[:, 0]
     selected_up = selected[:, 1]
 
-    x_split = latents.reshape(pair_local, 2, row_local, fsdp_size, in_local).transpose(3, 0, 1, 2, 4)
-    x_slice = lax.all_to_all(x_split, "fsdp", 0, 0, tiled=True)
-    partial = jnp.dot(
-        x_slice.reshape(fsdp_size * pair_local * 2 * row_local, in_local),
-        frozen_weight,
-        preferred_element_type=jnp.float32,
-    ).reshape(fsdp_size, pair_local * 2 * row_local, feat_width)
-    base_out = lax.psum_scatter(partial, "fsdp", scatter_dimension=0, tiled=True).reshape(
-        pair_local, 2, row_local, feat_width
+    highest = lax.Precision.HIGHEST
+    hidden_state = jnp.einsum(
+        "pktd,prd->pktr", latents, selected_down, preferred_element_type=jnp.float32
+    ).astype(jnp.bfloat16)
+    hidden_f = hidden_state.astype(jnp.float32)
+    v_block = jnp.einsum(
+        "prd,ed->pre", selected_up, frozen_weight, preferred_element_type=jnp.float32
     )
+    v_full = lax.all_gather(v_block, "fsdp", axis=2, tiled=True)
+    a_k = jnp.einsum(
+        "pktr,pktd->pkrd", hidden_state, latents, preferred_element_type=jnp.float32
+    ).reshape(pair_local, 2, adapter_rank_width, fsdp_size, in_local)
+    a_k = lax.psum_scatter(
+        a_k.transpose(3, 0, 1, 2, 4), "fsdp", scatter_dimension=0, tiled=True
+    ).reshape(pair_local, 2, adapter_rank_width, in_local)
+    base_up = jnp.einsum("pktd,prd->pktr", latents, v_full, precision=highest)
+    target_up = jnp.einsum(
+        "pktd,prd->pktr", targets, selected_up, preferred_element_type=jnp.float32
+    )
+    up_gram = jnp.einsum(
+        "prd,pqd->prq", selected_up, selected_up, preferred_element_type=jnp.float32
+    )
+    delta_up = ADAPTER_SCALE * jnp.einsum("pktr,prq->pktq", hidden_f, up_gram, precision=highest)
+    partial_err = jnp.sum(
+        hidden_f * (base_up - target_up + 0.5 * delta_up), axis=(2, 3)
+    ) * (2.0 * ADAPTER_SCALE)
+    back = base_up - target_up + delta_up
 
-    grouped = latents.reshape(pair_local, 2 * row_local, feat_width)
-    hidden_state = jnp.einsum(
-        "psd,prd->psr", grouped, selected_down, preferred_element_type=jnp.float32
-    ).astype(jnp.bfloat16)
-    weight_change = ADAPTER_SCALE * jnp.einsum(
-        "psr,prd->psd", hidden_state, selected_up, preferred_element_type=jnp.float32
-    )
-    weight_change = weight_change.reshape(pair_local, 2, row_local, feat_width)
-    resid = base_out - targets.astype(jnp.float32)
-    partial_err = jnp.sum(weight_change * (2.0 * resid + weight_change), axis=(2, 3))
     onehot = (categories[:, None] == jnp.arange(class_total, dtype=jnp.int32)[None, :]).astype(
         jnp.float32
     )
@@ -71,17 +77,16 @@
     coef_pair = LOSS_SCALE * kappa * jax.nn.sigmoid(zvalue) / pair_total
     signs = jnp.array([2.0, -2.0], dtype=jnp.float32)
     coefficient = coef_pair[:, None] * signs[None, :] / sample_rows
-    update = (resid + weight_change).astype(jnp.bfloat16)
-    hidden_k = hidden_state.reshape(pair_local, 2, row_local, adapter_rank_width)
-    up_gradient_k = jnp.einsum(
-        "pktr,pktd->pkrd", hidden_k, update, preferred_element_type=jnp.float32
+
+    hidden_gram = jnp.einsum(
+        "pktr,pktq->pkrq", hidden_state, hidden_state, preferred_element_type=jnp.float32
     )
-    back = jnp.einsum(
-        "pktd,prd->pktr", update, selected_up, preferred_element_type=jnp.float32
-    ).astype(jnp.bfloat16)
-    down_gradient_k = jnp.einsum(
-        "pktr,pktd->pkrd", back, latents, preferred_element_type=jnp.float32
+    up_gradient_k = (
+        jnp.einsum("pkre,ed->pkrd", a_k, frozen_weight, precision=highest)
+        - jnp.einsum("pktr,pktd->pkrd", hidden_state, targets, preferred_element_type=jnp.float32)
+        + ADAPTER_SCALE * jnp.einsum("pkrq,pqd->pkrd", hidden_gram, selected_up, precision=highest)
     )
+    down_gradient_k = jnp.einsum("pktr,pktd->pkrd", back, latents, precision=highest)
     pairwise_up = ADAPTER_SCALE * jnp.sum(coefficient[:, :, None, None] * up_gradient_k, axis=1)
     pairwise_down = ADAPTER_SCALE * jnp.sum(coefficient[:, :, None, None] * down_gradient_k, axis=1)
 

time: 298 us -> 250 us (0.84)
  waiting for transfers between devices: 78.7 us -> 31.3 us
  local copies, waits for them, and re-layouts: 68.8 us -> 74 us
  other arithmetic: 19.9 us -> 15 us
  blocking collectives: 83.6 us -> 80.3 us
    all_to_all x1, waiting for transfers between devices: 36.3 us -> 11.3 us  [local(): recv = lax.all_to_all(send, 'dp', 0, 0, tiled=True)]
    all_to_all x1 -> x0, blocking collectives: 23.6 us -> none  [local(): x_slice = lax.all_to_all(x_split, 'fsdp', 0, 0, tiled=True)]
    reduce_scatter x1, waiting for transfers between devices: 28.9 us -> 6.22 us  [local(): lax.psum_scatter(a_k.transpose(3, 0, 1, 2, 4), 'fsdp', scatter_dimension=...]
    all_gather x0 -> x1, blocking collectives: none -> 21.4 us  [local(): v_full = lax.all_gather(v_block, 'fsdp', axis=2, tiled=True)]
    reduce_sum x1 -> x0, other arithmetic: 3.88 us -> none  [local(): jnp.sum(weight_change * (2.0 * resid + weight_change), axis=(2, 3))]
    select_n x2 -> x1, other arithmetic: 3.58 us -> 0.01 us  [local(): send = jnp.take(both, cats_all.reshape(dp_size, pair_local), axis=0)]
    unnamed x0 -> x1, other arithmetic: none -> 3.56 us
    unnamed x15 -> x22, local copies, waits for them, and re-layouts: 28.2 us -> 30.7 us
  transfers between devices with their start and end apart: 4 -> 4, of which waited for: 4 -> 4; matrix products, arithmetic and copies ran while one was open for 8% -> 5% of each run, Pallas kernels for 0% -> 0%
where the time goes in v4:
time: 250 us; the launch traced here: 248 us
  blocking collectives  80.3 us (32%)
  local copies, waits for them, and re-layouts  74 us (30%)
  waiting for transfers between devices  31.3 us (13%)
  between operations  19 us (8%)
  matrix products  15.9 us (6%)
  other arithmetic  15 us (6%)
  starting transfers between devices  13.1 us (5%)
    unnamed x22, local copies, waits for them, and re-layouts  30.7 us
    all_to_all x1, blocking collectives, local(): lax.all_to_all(grads, 'dp', 0, 0, tiled=True)  28 us
    all_gather x1, blocking collectives, local(): v_full = lax.all_gather(v_block, 'fsdp', axis=2, tiled=True)  21.4 us
    unnamed x1, blocking collectives  18.6 us
    psum x1, blocking collectives, local(): errdiff = lax.psum(partial_err, 'fsdp') / sample_rows  12.2 us
    all_to_all x1, waiting for transfers between devices, local(): recv = lax.all_to_all(send, 'dp', 0, 0, tiled=True)  11.3 us
    ppermute x1, waiting for transfers between devices, fsdp_sum(): return value + lax.ppermute(value, 'fsdp', [(0, 3), (3, 0), (1, 2), (2, 1)])  7.78 us
    all_to_all x1, starting transfers between devices, local(): recv = lax.all_to_all(send, 'dp', 0, 0, tiled=True)  6.95 us
  transfers between devices with their start and end apart: 4, of which 4 were waited for; matrix products, arithmetic and copies ran while one was open for 5% of the time, Pallas kernels for 0%

profile of v4, /device:TPU:32, one launch (start us, length us, event | category | flops | bytes accessed | tf_op | source)
XLA Modules:
  0.0 248.5 jit_solution(10234908573288323563)
XLA Ops:
  8.0 1.4 dynamic-slice
  10.1 18.6 %all-reduce = s32[64]{0:T(128)S(1)} all-reduce(s32[64]{0:T(128)S(1)} %dynamic-update-slice), channel_id=1, replica_groups=mesh['dp'=64,'fsdp'=4] {'dp'}, use_global_device_ids=true, to_apply=%add | all-reduce | flops 64 | bytes 512
  28.7 1.0 copy.78
  29.7 1.0 copy.79
  31.1 4.0 %gather_fusion = bf16[64,2,64,38]{2,1,3,0:T(2,128)(2,1)} fusion(bf16[7,2,64,38]{2,1,3,0:T(2,128)(2,1)S(1)} %pad_maximum_fusion, s32[1024]{0:T(1024)S(1)} %pad_clamp_fusion), kind=kCustom, calls=%fused_computation | custom fusion | bytes 1245440 | tf_op jit(solution)/shard_map/jit(_take)/gather | solution.py:33
  35.1 3.6 %fusion.32 = bf16[64,1,38,2,64]{4,3,2,1,0:T(2,128)(2,1)} fusion(bf16[64,2,64,38]{2,1,3,0:T(2,128)(2,1)} %gather_fusion, pred[64]{0:T(512)(128)(4,1)S(1)} %compare_and_fusion), kind=kLoop, calls=%fused_computation.58 | loop fusion | flops 311296 | bytes 1245248
  38.7 4.2 %reshape.208 = bf16[64,2,2432]{2,1,0:T(2,128)(2,1)} reshape(bf16[64,1,38,2,64]{4,3,2,1,0:T(2,128)(2,1)} %fusion.32) | data formatting | bytes 1245184
  42.9 7.0 %all-to-all-start = ((bf16[64,2,2432]{2,1,0:T(2,128)(2,1)}), bf16[64,2,2432]{2,1,0:T(2,128)(2,1)}, u32[]{:S(2)}, u32[]{:S(2)}) async-start(bf16[64,2,2432]{2,1,0:T(2,128)(2,1)} %reshape.208), calls=%async_computation | async-start | bytes 1245184 | tf_op jit(solution)/shard_map/all_to_all | solution.py:34
  51.4 11.3 %all-to-all-done = bf16[64,2,2432]{2,1,0:T(2,128)(2,1)} async-done(((bf16[64,2,2432]{2,1,0:T(2,128)(2,1)}), bf16[64,2,2432]{2,1,0:T(2,128)(2,1)}, u32[]{:S(2)}, u32[]{:S(2)}) %all-to-all-start) | async-done | bytes 622624 | tf_op jit(solution)/shard_map/all_to_all | solution.py:34
  62.8 4.2 %reshape.209 = bf16[64,1,38,2,64]{4,3,2,1,0:T(2,128)(2,1)} reshape(bf16[64,2,2432]{2,1,0:T(2,128)(2,1)} %all-to-all-done) | data formatting | bytes 1245184
  66.9 5.0 %fusion.30 = (bf16[1,1,64,2432]{2,1,3,0:T(2,128)(2,1)}, bf16[1,1,64,2432]{2,1,3,0:T(2,128)(2,1)}) fusion(bf16[1,2,64,2432]{2,1,3,0:T(2,128)(2,1)} %bitcast.106), kind=kLoop, calls=%fused_computation.55 | loop fusion | bytes 1245184 | tf_op jit(solution)/shard_map/slice | solution.py:39
  71.9 3.5 %copy.102 = bf16[1,1,64,2432]{3,2,1,0:T(8,128)(2,1)} copy(bf16[1,1,64,2432]{2,1,3,0:T(2,128)(2,1)} %get-tuple-element.19) | data formatting | bytes 622592
  75.4 2.5 %copy.103 = bf16[1,1,64,2432]{3,2,1,0:T(8,128)(2,1)S(1)} copy(bf16[1,1,64,2432]{2,1,3,0:T(2,128)(2,1)} %get-tuple-element.18) | data formatting | bytes 622592
  78.0 1.0 convolution_bitcast_fusion
  78.9 21.4 %all-gather.1 = f32[4,608,64]{1,2,0:T(8,128)S(1)} all-gather(f32[1,608,64]{1,2,0:T(8,128)S(1)} %convolution_bitcast_fusion), channel_id=2, replica_groups=mesh['dp'=64,'fsdp'=4] {'fsdp'}, dimensions={0}, use_global_device_ids=true | all-gather | bytes 778240 | tf_op jit(solution)/shard_map/all_gather | solution.py:49
  100.3 1.3 copy.84
  101.6 2.2 reshape.203
  103.8 1.7 fusion.8
  105.5 1.3 fusion.11
  106.9 3.1 %reshape.180 = f32[1,2,64,4,608]{4,3,2,1,0:T(4,128)} reshape(f32[2,64,2432]{2,1,0:T(8,128)} %fusion.11) | data formatting | bytes 2490368 | tf_op jit(solution)/shard_map/reshape | solution.py:52
  110.0 2.5 copy.106
  113.0 2.3 fusion.14
  115.9 12.2 %psum.7 = f32[1,2]{1,0:T(1,128)S(1)} all-reduce(f32[1,2]{1,0:T(1,128)S(1)} %bitcast.112), channel_id=1, replica_groups=mesh['dp'=64,'fsdp'=4] {'fsdp'}, use_global_device_ids=true, to_apply=%region_1.2 | all-reduce | flops 2 | bytes 16 | tf_op jit(solution)/shard_map/psum | solution.py:72
  130.7 1.8 fusion.4
  132.6 0.9 broadcast_multiply_fusion.1
  133.4 2.5 %copy.88 = f32[64,2432]{0,1:T(8,128)} copy(f32[64,2432]{1,0:T(8,128)} %broadcast_multiply_fusion.1) | data formatting | bytes 1245184 | tf_op jit(solution)/shard_map/mul | solution.py:91
  136.0 2.4 mul.106
  138.5 6.2 %reduce-scatter.2.cloned.1.call-done = f32[1,1,2,64,608]{4,3,2,1,0:T(8,128)} async-done(((f32[4,1,2,64,608]{4,3,2,1,0:T(8,128)}), f32[1,1,2,64,608]{4,3,2,1,0:T(8,128)}) %reduce-scatter.2.cloned.1.call-update) | async-done | bytes 311312 | tf_op jit(solution)/shard_map/reduce_scatter | solution.py:53
  144.8 2.7 %fusion.2 = f32[2,64,2432]{2,1,0:T(8,128)S(1)} fusion(bf16[608,2432]{1,0:T(8,128)(2,1)S(1)} %copy-done, f32[1,1,2,64,608]{4,3,2,1,0:T(8,128)} %reduce-scatter.2.cloned.1.call-done), kind=kOutput, calls=%fused_computation.6 | convolution fusion | flops 2271215616 | bytes 4513792 | tf_op jit(solution)/shard_map/pkre,ed->pkrd/dot_general | solution.py:85
  148.5 0.9 broadcast_multiply_fusion
  149.4 2.5 %copy.91 = f32[64,2432]{0,1:T(8,128)} copy(f32[64,2432]{1,0:T(8,128)} %broadcast_multiply_fusion) | data formatting | bytes 1245184 | tf_op jit(solution)/shard_map/mul | solution.py:90
  151.9 2.4 mul.111
  154.3 1.9 maximum_bitcast_fusion
  156.2 3.4 %copy.107 = f32[64,1,2,64,38]{3,2,4,1,0:T(2,128)} copy(f32[64,1,2,64,38]{3,4,0,2,1:T(8,128)S(1)} %maximum_bitcast_fusion) | data formatting | bytes 2490368 | tf_op jit(solution)/shard_map/transpose | solution.py:96
  159.6 4.7 %reshape.210 = f32[64,1,4864]{2,1,0:T(1,128)} reshape(f32[64,1,38,2,64]{4,3,2,1,0:T(2,128)} %bitcast.107) | data formatting | bytes 2490368
  164.3 28.0 %all_to_all.10 = f32[64,1,4864]{2,1,0:T(1,128)} all-to-all(f32[64,1,4864]{2,1,0:T(1,128)} %reshape.210), channel_id=1, replica_groups=mesh['dp'=64,'fsdp'=4] {'dp'}, dimensions={0} | all-to-all | bytes 2490368 | tf_op jit(solution)/shard_map/all_to_all | solution.py:97
  192.8 6.0 %reduce.7 = f32[64,4864]{1,0:T(8,128)} reduce(f32[64,1,4864]{2,1,0:T(1,128)} %all_to_all.10, f32[]{:T(128)} %broadcast.108), dimensions={1}, to_apply=%all_to_all.7.reduce_sub_computation | reduce | bytes 2490372 | tf_op jit(solution)/shard_map/all_to_all | solution.py:97
  198.8 3.8 %reshape.211 = f32[64,1,38,2,64]{4,3,2,1,0:T(2,128)} reshape(f32[64,4864]{1,0:T(8,128)} %reduce.7) | data formatting | bytes 2490368
  202.6 5.4 %copy.93 = f32[64,1,2,64,38]{0,4,3,2,1:T(8,128)} copy(f32[64,1,2,64,38]{3,2,4,1,0:T(2,128)} %bitcast.108) | data formatting | bytes 2490368 | tf_op jit(solution)/shard_map/all_to_all | solution.py:97
  208.0 3.4 %reshape.182 = f32[64,4864]{0,1:T(8,128)} reshape(f32[64,1,2,64,38]{0,4,3,2,1:T(8,128)} %copy.93) | data formatting | bytes 2490368 | tf_op jit(solution)/shard_map/reshape | solution.py:97
  211.4 3.0 %fusion.26 = f32[7,4864]{1,0:T(8,128)S(1)} fusion(f32[64,4864]{0,1:T(8,128)} %reshape.182, s32[64]{0:T(128)S(1)} %all-reduce), kind=kOutput, calls=%fused_computation.46 | convolution fusion | flops 26149312 | bytes 1381632 | tf_op jit(solution)/shard_map/dot_general | solution.py:100
  214.4 2.5 %collective-permute-start = (f32[7,4864]{1,0:T(8,128)S(1)}, f32[7,4864]{1,0:T(8,128)S(1)}, u32[]{:S(2)}, u32[]{:S(2)}) collective-permute-start(f32[7,4864]{1,0:T(8,128)S(1)} %fusion.26), channel_id=1, source_target_pairs={{0,1},{1,0},{2,3},{3,2},{4,5},{5,4},{6,7},{7,6},{8,9},{9,8},{10,11... | collective-permute-start | bytes 408584 | tf_op jit(solution)/shard_map/ppermute | solution.py:14
  216.9 5.9 %collective-permute-done = f32[7,4864]{1,0:T(8,128)S(1)} collective-permute-done((f32[7,4864]{1,0:T(8,128)S(1)}, f32[7,4864]{1,0:T(8,128)S(1)}, u32[]{:S(2)}, u32[]{:S(2)}) %collective-permute-start) | collective-permute-done | bytes 136224 | tf_op jit(solution)/shard_map/ppermute | solution.py:14
  222.8 3.4 %collective-permute-start.1 = (f32[7,4864]{1,0:T(8,128)S(1)}, f32[7,4864]{1,0:T(8,128)S(1)}, u32[]{:S(2)}, u32[]{:S(2)}) collective-permute-start(f32[7,4864]{1,0:T(8,128)S(1)} %add.48), channel_id=1, source_target_pairs={{0,3},{3,0},{1,2},{2,1},{4,7},{7,4},{5,6},{6,5},{8,11},{11,8},{9,1... | collective-permute-start | bytes 408584 | tf_op jit(solution)/shard_map/ppermute | solution.py:15
  226.3 7.8 %collective-permute-done.1 = f32[7,4864]{1,0:T(8,128)S(1)} collective-permute-done((f32[7,4864]{1,0:T(8,128)S(1)}, f32[7,4864]{1,0:T(8,128)S(1)}, u32[]{:S(2)}, u32[]{:S(2)}) %collective-permute-start.1) | collective-permute-done | bytes 136224 | tf_op jit(solution)/shard_map/ppermute | solution.py:15
  234.8 1.4 reshape.183
  237.0 1.7 copy.94
  238.8 1.7 copy.95
  (33 shorter events, 6.9 us)
Async XLA Ops:
  7.2 70.8 %copy-start = (bf16[608,2432]{1,0:T(8,128)(2,1)S(1)}, bf16[608,2432]{1,0:T(8,128)(2,1)}, u32[]{:S(2)}) copy-start(bf16[608,2432]{1,0:T(8,128)(2,1)} %param.10) | copy-start | bytes 8871940
  42.9 19.9 %all-to-all-start = ((bf16[64,2,2432]{2,1,0:T(2,128)(2,1)}), bf16[64,2,2432]{2,1,0:T(2,128)(2,1)}, u32[]{:S(2)}, u32[]{:S(2)}) async-start(bf16[64,2,2432]{2,1,0:T(2,128)(2,1)} %reshape.208), calls=%async_computation | async-start | bytes 1245184 | tf_op jit(solution)/shard_map/all_to_all | solution.py:34
  49.8 94.9 %reduce-scatter.2.cloned.1.call-start = ((), (), s32[]{:S(2)}) async-start(), calls=%async_computation.3 | async-start | bytes 1638400 | tf_op jit(solution)/shard_map/reduce_scatter | solution.py:53
  103.8 1.7 copy-start.1
  112.5 2.8 %copy-start.2 = (bf16[1,2,64,2432]{3,2,1,0:T(8,128)(2,1)S(1)}, bf16[1,2,64,2432]{3,2,1,0:T(8,128)(2,1)}, u32[]{:S(2)}) copy-start(bf16[1,2,64,2432]{3,2,1,0:T(8,128)(2,1)} %param.9) | copy-start | bytes 1867780
  113.0 17.7 %copy-start.4 = (f32[2]{0:T(128)S(1)}, f32[2]{0:T(128)}, u32[]{:S(2)}) copy-start(f32[2]{0:T(128)} %constant.43.clone) | copy-start | bytes 28
  144.8 2.7 %copy-start.3 = (bf16[1,2,64,2432]{3,2,1,0:T(8,128)(2,1)S(1)}, bf16[1,2,64,2432]{3,2,1,0:T(8,128)(2,1)}, u32[]{:S(2)}) copy-start(bf16[1,2,64,2432]{3,2,1,0:T(8,128)(2,1)} %param.9) | copy-start | bytes 1867780
  214.4 8.4 %collective-permute-start = (f32[7,4864]{1,0:T(8,128)S(1)}, f32[7,4864]{1,0:T(8,128)S(1)}, u32[]{:S(2)}, u32[]{:S(2)}) collective-permute-start(f32[7,4864]{1,0:T(8,128)S(1)} %fusion.26), channel_id=1, source_target_pairs={{0,1},{1,0},{2,3},{3,2},{4,5},{5,4},{6,7},{7,6},{8,9},{9,8},{10,11... | collective-permute-start | bytes 408584 | tf_op jit(solution)/shard_map/ppermute | solution.py:14
  222.8 11.3 %collective-permute-start.1 = (f32[7,4864]{1,0:T(8,128)S(1)}, f32[7,4864]{1,0:T(8,128)S(1)}, u32[]{:S(2)}, u32[]{:S(2)}) collective-permute-start(f32[7,4864]{1,0:T(8,128)S(1)} %add.48), channel_id=1, source_target_pairs={{0,3},{3,0},{1,2},{2,1},{4,7},{7,4},{5,6},{6,5},{8,11},{11,8},{9,1... | collective-permute-start | bytes 408584 | tf_op jit(solution)/shard_map/ppermute | solution.py:15
Sparse Core Ops, SparseCore 0:
  112.6 32.0 reduce-scatter.1

commit v5 on v4

--- a/solution.py
+++ b/solution.py
@@ -78,29 +78,29 @@
     signs = jnp.array([2.0, -2.0], dtype=jnp.float32)
     coefficient = coef_pair[:, None] * signs[None, :] / sample_rows
 
+    scale_k = (ADAPTER_SCALE * coefficient)[:, :, None, None]
     hidden_gram = jnp.einsum(
         "pktr,pktq->pkrq", hidden_state, hidden_state, preferred_element_type=jnp.float32
     )
-    up_gradient_k = (
-        jnp.einsum("pkre,ed->pkrd", a_k, frozen_weight, precision=highest)
-        - jnp.einsum("pktr,pktd->pkrd", hidden_state, targets, preferred_element_type=jnp.float32)
-        + ADAPTER_SCALE * jnp.einsum("pkrq,pqd->pkrd", hidden_gram, selected_up, precision=highest)
+    a_weighted = jnp.sum(scale_k * a_k, axis=1)
+    gram_weighted = ADAPTER_SCALE * jnp.sum(scale_k * hidden_gram, axis=1)
+    up_t = (
+        jnp.einsum("ed,pre->pdr", frozen_weight, a_weighted, precision=highest)
+        - jnp.einsum("pktd,pktr->pdr", targets, hidden_f * scale_k, precision=highest)
+        + jnp.einsum("pqd,prq->pdr", selected_up, gram_weighted, precision=highest)
     )
-    down_gradient_k = jnp.einsum("pktr,pktd->pkrd", back, latents, precision=highest)
-    pairwise_up = ADAPTER_SCALE * jnp.sum(coefficient[:, :, None, None] * up_gradient_k, axis=1)
-    pairwise_down = ADAPTER_SCALE * jnp.sum(coefficient[:, :, None, None] * down_gradient_k, axis=1)
+    down_t = jnp.einsum("pktd,pktr->pdr", latents, back * scale_k, precision=highest)
+    grads = jnp.concatenate([down_t, up_t], axis=2).reshape(
+        pair_local, dp_size, col_local, 2 * adapter_rank_width
+    )
 
-    grads = jnp.stack([pairwise_down, pairwise_up], axis=1).reshape(
-        pair_local, 2, adapter_rank_width, dp_size, col_local
-    )
-    grads = grads.transpose(3, 0, 1, 2, 4)
-    gathered = lax.all_to_all(grads, "dp", 0, 0, tiled=True).reshape(
-        dp_size * pair_local, 2 * adapter_rank_width * col_local
+    gathered = lax.all_to_all(grads.transpose(1, 0, 2, 3), "dp", 0, 0, tiled=True).reshape(
+        dp_size * pair_local, col_local * 2 * adapter_rank_width
     )
     dense = jnp.dot(onehot_all.T, gathered, precision=lax.Precision.HIGHEST)
-    dense = fsdp_sum(dense, fsdp_size).reshape(class_total, 2, adapter_rank_width, col_local)
-    grad_down = dense[:, 0]
-    grad_up = dense[:, 1]
+    dense = fsdp_sum(dense, fsdp_size).reshape(class_total, col_local, 2, adapter_rank_width)
+    grad_down = dense[:, :, 0].transpose(0, 2, 1)
+    grad_up = dense[:, :, 1].transpose(0, 2, 1)
     return (grad_down, grad_up, losses)
 
 

time: 250 us -> 222 us (0.89)
  blocking collectives: 80.3 us -> 106 us
  local copies, waits for them, and re-layouts: 74 us -> 48.6 us
  waiting for transfers between devices: 31.3 us -> 13.2 us
  starting transfers between devices: 13.1 us -> 5.79 us
    all_to_all x1 -> x2, blocking collectives: 28 us -> 45.7 us  [the longest x1 25.8 us: local(): lax.all_to_all(grads.transpose(1, 0, 2, 3), 'dp', 0, 0, tiled=True)]
    unnamed x22 -> x18, local copies, waits for them, and re-layouts: 30.7 us -> 17.7 us
    all_to_all x1 -> x0, waiting for transfers between devices: 11.3 us -> none  [local(): recv = lax.all_to_all(send, 'dp', 0, 0, tiled=True)]
    all_gather x1, blocking collectives: 21.4 us -> 31.3 us  [local(): v_full = lax.all_gather(v_block, 'fsdp', axis=2, tiled=True)]
    mul x4 -> x0, local copies, waits for them, and re-layouts: 9.9 us -> none  [the longest x2 4.96 us: local(): ADAPTER_SCALE * jnp.sum(coefficient[:, :, None, None] * down_gradient_k,...]
    all_to_all x1 -> x0, starting transfers between devices: 6.95 us -> none  [local(): recv = lax.all_to_all(send, 'dp', 0, 0, tiled=True)]
    reduce_scatter x1, waiting for transfers between devices: 6.22 us -> 0.02 us  [local(): lax.psum_scatter(a_k.transpose(3, 0, 1, 2, 4), 'fsdp', scatter_dimension=...]
    concatenate x0 -> x3, local copies, waits for them, and re-layouts: none -> 6.08 us  [local(): jnp.concatenate([down_t, up_t], axis=2)]
  transfers between devices with their start and end apart: 4 -> 3, of which waited for: 4 -> 2; matrix products, arithmetic and copies ran while one was open for 5% -> 9% of each run, Pallas kernels for 0% -> 0%
where the time goes in v5:
time: 222 us; the launch traced here: 220 us
  blocking collectives  106 us (48%)
  local copies, waits for them, and re-layouts  48.6 us (22%)
  between operations  19.1 us (9%)
  matrix products  15 us (7%)
  other arithmetic  13.2 us (6%)
  waiting for transfers between devices  13.2 us (6%)
  starting transfers between devices  5.79 us (3%)
    all_gather x1, blocking collectives, local(): v_full = lax.all_gather(v_block, 'fsdp', axis=2, tiled=True)  31.3 us
    all_to_all x1, blocking collectives, local(): lax.all_to_all(grads.transpose(1, 0, 2, 3), 'dp', 0, 0, tiled=True)  25.8 us
    all_to_all x1, blocking collectives, local(): recv = lax.all_to_all(send, 'dp', 0, 0, tiled=True)  19.9 us
    unnamed x1, blocking collectives  18.6 us
    unnamed x18, local copies, waits for them, and re-layouts  17.7 us
    psum x1, blocking collectives, local(): errdiff = lax.psum(partial_err, 'fsdp') / sample_rows  9.91 us
    ppermute x1, waiting for transfers between devices, fsdp_sum(): return value + lax.ppermute(value, 'fsdp', [(0, 3), (3, 0), (1, 2), (2, 1)])  7.26 us
    concatenate x3, local copies, waits for them, and re-layouts, local(): jnp.concatenate([down_t, up_t], axis=2)  6.08 us
  transfers between devices with their start and end apart: 3, of which 2 were waited for; matrix products, arithmetic and copies ran while one was open for 9% of the time, Pallas kernels for 0%

profile of v5, /device:TPU:32, one launch (start us, length us, event | category | flops | bytes accessed | tf_op | source)
XLA Modules:
  0.0 220.5 jit_solution(881777718391143724)
XLA Ops:
  8.0 1.3 dynamic-slice
  9.3 0.8 dynamic-update-slice
  10.1 18.6 %all-reduce = s32[64]{0:T(128)S(1)} all-reduce(s32[64]{0:T(128)S(1)} %dynamic-update-slice), channel_id=1, replica_groups=mesh['dp'=64,'fsdp'=4] {'dp'}, use_global_device_ids=true, to_apply=%add | all-reduce | flops 64 | bytes 512
  28.7 1.0 copy.78
  29.7 1.0 copy.77
  30.7 0.4 pad_maximum_fusion.1
  31.1 4.0 %gather_fusion = bf16[64,2,64,38]{2,1,3,0:T(2,128)(2,1)} fusion(bf16[7,2,64,38]{2,1,3,0:T(2,128)(2,1)S(1)} %pad_maximum_fusion.1, s32[1024]{0:T(1024)S(1)} %pad_clamp_fusion), kind=kCustom, calls=%fused_computation | custom fusion | bytes 1245440 | tf_op jit(solution)/shard_map/jit(_take)/gather | solution.py:33
  35.1 3.6 %fusion.39 = bf16[64,1,38,2,64]{4,3,2,1,0:T(2,128)(2,1)} fusion(bf16[64,2,64,38]{2,1,3,0:T(2,128)(2,1)} %gather_fusion, pred[64]{0:T(512)(128)(4,1)S(1)} %compare_and_fusion), kind=kLoop, calls=%fused_computation.66 | loop fusion | flops 311296 | bytes 1245248
  38.7 4.2 %reshape.196 = bf16[64,2,2432]{2,1,0:T(2,128)(2,1)} reshape(bf16[64,1,38,2,64]{4,3,2,1,0:T(2,128)(2,1)} %fusion.39) | data formatting | bytes 1245184
  42.9 19.9 %all_to_all.10 = bf16[64,2,2432]{2,1,0:T(2,128)(2,1)} all-to-all(bf16[64,2,2432]{2,1,0:T(2,128)(2,1)} %reshape.196), channel_id=1, replica_groups=mesh['dp'=64,'fsdp'=4] {'dp'}, dimensions={0} | all-to-all | bytes 1245184 | tf_op jit(solution)/shard_map/all_to_all | solution.py:34
  62.8 4.2 %reshape.197 = bf16[64,1,38,2,64]{4,3,2,1,0:T(2,128)(2,1)} reshape(bf16[64,2,2432]{2,1,0:T(2,128)(2,1)} %all_to_all.10) | data formatting | bytes 1245184
  67.0 5.0 %fusion.36 = (bf16[1,1,64,2432]{2,1,3,0:T(2,128)(2,1)}, bf16[1,1,64,2432]{2,1,3,0:T(2,128)(2,1)}) fusion(bf16[1,2,64,2432]{2,1,3,0:T(2,128)(2,1)} %bitcast.119), kind=kLoop, calls=%fused_computation.63 | loop fusion | bytes 1245184 | tf_op jit(solution)/shard_map/slice | solution.py:39
  72.0 2.5 %copy.103 = bf16[1,1,64,2432]{3,2,1,0:T(8,128)(2,1)S(1)} copy(bf16[1,1,64,2432]{2,1,3,0:T(2,128)(2,1)} %get-tuple-element.4) | data formatting | bytes 622592
  74.5 1.6 fusion.8
  76.1 1.3 fusion.11
  77.4 3.1 %reshape.166 = f32[1,2,64,4,608]{4,3,2,1,0:T(4,128)} reshape(f32[2,64,2432]{2,1,0:T(8,128)} %fusion.11) | data formatting | bytes 2490368 | tf_op jit(solution)/shard_map/reshape | solution.py:52
  80.6 2.5 %copy.114 = f32[1,2,64,4,608]{4,2,1,0,3:T(8,128)} copy(f32[1,2,64,4,608]{4,3,2,1,0:T(4,128)} %reshape.166) | data formatting | bytes 2490368 | tf_op jit(solution)/shard_map/reshape | solution.py:52
  83.9 0.6 fusion.33
  84.5 2.5 %copy.102 = bf16[1,1,64,2432]{3,2,1,0:T(8,128)(2,1)S(1)} copy(bf16[1,1,64,2432]{2,1,3,0:T(2,128)(2,1)} %get-tuple-element.3) | data formatting | bytes 622592
  87.0 1.0 convolution_bitcast_fusion.4
  88.0 31.3 %all-gather.1 = f32[4,608,64]{1,2,0:T(8,128)S(1)} all-gather(f32[1,608,64]{1,2,0:T(8,128)S(1)} %convolution_bitcast_fusion.4), channel_id=2, replica_groups=mesh['dp'=64,'fsdp'=4] {'fsdp'}, dimensions={0}, use_global_device_ids=true | all-gather | bytes 778240 | tf_op jit(solution)/shard_map/all_gather | solution.py:49
  119.3 1.3 copy.82
  120.6 2.2 %reshape.188 = f32[2432,64,1]{0,1,2:T(8,128)} reshape(f32[4,608,64]{1,0,2:T(4,128)} %copy.82) | data formatting | bytes 1245184
  122.8 0.2 convolution_bitcast_fusion.5
  123.1 0.2 fusion.40
  123.3 2.3 %fusion.15 = f32[64,2,64]{2,0,1:T(8,128)S(1)} fusion(f32[2432,64,1]{0,1,2:T(8,128)} %reshape.188, bf16[1,2,64,2432]{3,2,1,0:T(8,128)(2,1)} %param.8), kind=kOutput, calls=%fused_computation.28 | convolution fusion | flops 239075328 | bytes 1277952 | tf_op jit(solution)/shard_map/pktd,prd->pktr/dot_general | solution.py:56
  125.7 0.5 fusion.23
  126.2 9.9 %psum.7 = f32[1,2]{1,0:T(1,128)S(1)} all-reduce(f32[1,2]{1,0:T(1,128)S(1)} %bitcast.124), channel_id=1, replica_groups=mesh['dp'=64,'fsdp'=4] {'fsdp'}, use_global_device_ids=true, to_apply=%region_1.2 | all-reduce | flops 2 | bytes 16 | tf_op jit(solution)/shard_map/psum | solution.py:72
  136.1 0.6 fusion.38
  138.8 2.5 %convolution_bitcast_fusion.2 = f32[2432,64]{0,1:T(8,128)} fusion(bf16[1,2,64,2432]{3,2,1,0:T(8,128)(2,1)} %param.8, f32[2,64,64]{1,2,0:T(8,128)S(1)} %get-tuple-element.10, f32[2,64,64]{1,2,0:T(8,128)S(1)} %fusion.40, f32[2]{0:T(128)S(1)} %multiply_multiply_fusion), kind=kOutput, calls=%fused_computation.5 | convolution fusion | flops 239099904 | bytes 1310728 | tf_op jit(solution)/shard_map/pktd,pktr->pdr/dot_general | solution.py:92
  141.3 2.5 %copy.87 = f32[2432,64]{1,0:T(8,128)} copy(f32[2432,64]{0,1:T(8,128)} %convolution_bitcast_fusion.2) | data formatting | bytes 1245184 | tf_op jit(solution)/shard_map/pktd,pktr->pdr/dot_general | solution.py:92
  143.8 2.4 %concatenate.8 = f32[64,1,38,64]{3,2,0,1:T(8,128)} reshape(f32[2432,64]{1,0:T(8,128)} %copy.87) | data formatting | bytes 1245184 | tf_op jit(solution)/shard_map/concatenate | solution.py:93
  146.4 1.1 fusion.17
  147.5 1.5 convolution_bitcast_fusion.3
  149.0 0.6 fusion.1
  149.6 1.3 fusion
  150.9 2.5 %copy.91 = f32[1,2432,64]{2,1,0:T(8,128)} copy(f32[1,2432,64]{1,2,0:T(8,128)} %fusion) | data formatting | bytes 1245184 | tf_op jit(solution)/shard_map/add | solution.py:88
  153.4 2.4 %concatenate.9 = f32[64,1,38,64]{3,2,0,1:T(8,128)} reshape(f32[1,2432,64]{2,1,0:T(8,128)} %copy.91) | data formatting | bytes 1245184 | tf_op jit(solution)/shard_map/concatenate | solution.py:93
  155.8 2.1 pad_maximum_fusion
  157.9 1.3 copy.92
  159.2 25.8 %all_to_all.11 = f32[64,1,38,128]{3,1,2,0:T(1,128)} all-to-all(f32[64,1,38,128]{3,1,2,0:T(1,128)S(1)} %copy.92), channel_id=1, replica_groups=mesh['dp'=64,'fsdp'=4] {'dp'}, dimensions={0} | all-to-all | bytes 2490368 | tf_op jit(solution)/shard_map/all_to_all | solution.py:97
  185.0 5.3 %reduce.6 = f32[64,38,128]{2,1,0:T(8,128)} reduce(f32[64,1,38,128]{3,1,2,0:T(1,128)} %all_to_all.11, f32[]{:T(128)} %constant.58), dimensions={1}, to_apply=%all_to_all.7.reduce_sub_computation | reduce | bytes 2490372 | tf_op jit(solution)/shard_map/all_to_all | solution.py:97
  190.3 1.9 fusion.2
  192.3 1.1 collective-permute-start
  193.3 5.9 %collective-permute-done = f32[7,4864]{1,0:T(8,128)S(1)} collective-permute-done((f32[7,4864]{1,0:T(8,128)S(1)}, f32[7,4864]{1,0:T(8,128)S(1)}, u32[]{:S(2)}, u32[]{:S(2)}) %collective-permute-start) | collective-permute-done | bytes 136224 | tf_op jit(solution)/shard_map/ppermute | solution.py:14
  199.3 4.7 %collective-permute-start.1 = (f32[7,4864]{1,0:T(8,128)S(1)}, f32[7,4864]{1,0:T(8,128)S(1)}, u32[]{:S(2)}, u32[]{:S(2)}) collective-permute-start(f32[7,4864]{1,0:T(8,128)S(1)} %add.47), channel_id=1, source_target_pairs={{0,3},{3,0},{1,2},{2,1},{4,7},{7,4},{5,6},{6,5},{8,11},{11,8},{9,1... | collective-permute-start | bytes 408584 | tf_op jit(solution)/shard_map/ppermute | solution.py:15
  204.0 7.3 %collective-permute-done.1 = f32[7,4864]{1,0:T(8,128)S(1)} collective-permute-done((f32[7,4864]{1,0:T(8,128)S(1)}, f32[7,4864]{1,0:T(8,128)S(1)}, u32[]{:S(2)}, u32[]{:S(2)}) %collective-permute-start.1) | collective-permute-done | bytes 136224 | tf_op jit(solution)/shard_map/ppermute | solution.py:15
  211.8 0.7 copy_bitcast_fusion.1
  (25 shorter events, 0.8 us)
Async XLA Ops:
  7.2 79.8 %copy-start = (bf16[608,2432]{1,0:T(8,128)(2,1)S(1)}, bf16[608,2432]{1,0:T(8,128)(2,1)}, u32[]{:S(2)}) copy-start(bf16[608,2432]{1,0:T(8,128)(2,1)} %param.10) | copy-start | bytes 8871940
  7.2 139.2 %reduce-scatter.2.cloned.1.call-start = ((), (), s32[]{:S(2)}) async-start(), calls=%async_computation.3 | async-start | bytes 1638400 | tf_op jit(solution)/shard_map/reduce_scatter | solution.py:53
  74.5 1.6 copy-start.1
  122.8 2.8 %copy-start.2 = (bf16[1,2,64,2432]{3,2,1,0:T(8,128)(2,1)S(1)}, bf16[1,2,64,2432]{3,2,1,0:T(8,128)(2,1)}, u32[]{:S(2)}) copy-start(bf16[1,2,64,2432]{3,2,1,0:T(8,128)(2,1)} %param.9) | copy-start | bytes 1867780
  123.1 15.7 %copy-start.4 = (f32[2]{0:T(128)S(1)}, f32[2]{0:T(128)}, u32[]{:S(2)}) copy-start(f32[2]{0:T(128)} %constant.45.clone) | copy-start | bytes 28
  147.5 1.5 copy-start.3
  192.3 7.0 %collective-permute-start = (f32[7,4864]{1,0:T(8,128)S(1)}, f32[7,4864]{1,0:T(8,128)S(1)}, u32[]{:S(2)}, u32[]{:S(2)}) collective-permute-start(f32[7,4864]{1,0:T(8,128)S(1)} %fusion.2), channel_id=1, source_target_pairs={{0,1},{1,0},{2,3},{3,2},{4,5},{5,4},{6,7},{7,6},{8,9},{9,8},{10,11... | collective-permute-start | bytes 408584 | tf_op jit(solution)/shard_map/ppermute | solution.py:14
  199.3 12.0 %collective-permute-start.1 = (f32[7,4864]{1,0:T(8,128)S(1)}, f32[7,4864]{1,0:T(8,128)S(1)}, u32[]{:S(2)}, u32[]{:S(2)}) collective-permute-start(f32[7,4864]{1,0:T(8,128)S(1)} %add.47), channel_id=1, source_target_pairs={{0,3},{3,0},{1,2},{2,1},{4,7},{7,4},{5,6},{6,5},{8,11},{11,8},{9,1... | collective-permute-start | bytes 408584 | tf_op jit(solution)/shard_map/ppermute | solution.py:15
Sparse Core Ops, SparseCore 0:
  83.2 44.7 reduce-scatter.1

commit v6 on v5

--- a/solution.py
+++ b/solution.py
@@ -29,41 +29,47 @@
     )
     counts = jnp.sum(onehot_all, axis=0)
 
-    both = jnp.stack([adapter_down, adapter_up], axis=1)
+    both = jnp.stack([adapter_down, adapter_up], axis=1).transpose(0, 3, 1, 2)
     send = jnp.take(both, cats_all.reshape(dp_size, pair_local), axis=0)
     recv = lax.all_to_all(send, "dp", 0, 0, tiled=True)
-    selected = recv.transpose(1, 2, 3, 0, 4).reshape(
-        pair_local, 2, adapter_rank_width, dp_size * col_local
+    selected = recv.transpose(1, 0, 2, 3, 4).reshape(
+        pair_local, dp_size * col_local, 2, adapter_rank_width
     )
-    selected_down = selected[:, 0]
-    selected_up = selected[:, 1]
+    down_t = selected[:, :, 0]
+    up_t = selected[:, :, 1]
 
     highest = lax.Precision.HIGHEST
     hidden_state = jnp.einsum(
-        "pktd,prd->pktr", latents, selected_down, preferred_element_type=jnp.float32
+        "pktd,pdr->pktr", latents, down_t, preferred_element_type=jnp.float32
     ).astype(jnp.bfloat16)
     hidden_f = hidden_state.astype(jnp.float32)
-    v_block = jnp.einsum(
-        "prd,ed->pre", selected_up, frozen_weight, preferred_element_type=jnp.float32
-    )
-    v_full = lax.all_gather(v_block, "fsdp", axis=2, tiled=True)
+    v_block = jnp.einsum("ed,pdr->per", frozen_weight, up_t, preferred_element_type=jnp.float32)
+    shifted = [v_block] + [
+        lax.ppermute(
+            v_block, "fsdp", [((dst + shift) % fsdp_size, dst) for dst in range(fsdp_size)]
+        )
+        for shift in range(1, fsdp_size)
+    ]
+    stacked = jnp.stack(shifted + shifted, axis=0)
+    own = lax.axis_index("fsdp")
+    v_by_source = lax.dynamic_slice_in_dim(stacked, (fsdp_size - own) % fsdp_size, fsdp_size, 0)
+    latents_blocks = latents.reshape(pair_local, 2, row_local, fsdp_size, in_local)
     a_k = jnp.einsum(
         "pktr,pktd->pkrd", hidden_state, latents, preferred_element_type=jnp.float32
     ).reshape(pair_local, 2, adapter_rank_width, fsdp_size, in_local)
     a_k = lax.psum_scatter(
         a_k.transpose(3, 0, 1, 2, 4), "fsdp", scatter_dimension=0, tiled=True
     ).reshape(pair_local, 2, adapter_rank_width, in_local)
-    base_up = jnp.einsum("pktd,prd->pktr", latents, v_full, precision=highest)
     target_up = jnp.einsum(
-        "pktd,prd->pktr", targets, selected_up, preferred_element_type=jnp.float32
+        "pktd,pdr->pktr", targets, up_t, preferred_element_type=jnp.float32
     )
-    up_gram = jnp.einsum(
-        "prd,pqd->prq", selected_up, selected_up, preferred_element_type=jnp.float32
-    )
+    up_gram = jnp.einsum("pdr,pdq->prq", up_t, up_t, preferred_element_type=jnp.float32)
     delta_up = ADAPTER_SCALE * jnp.einsum("pktr,prq->pktq", hidden_f, up_gram, precision=highest)
-    partial_err = jnp.sum(
-        hidden_f * (base_up - target_up + 0.5 * delta_up), axis=(2, 3)
+    base_term = jnp.sum(a_k * v_block[:, None].transpose(0, 1, 3, 2), axis=(2, 3))
+    partial_err = (
+        jnp.sum(hidden_f * (0.5 * delta_up - target_up), axis=(2, 3)) + base_term
     ) * (2.0 * ADAPTER_SCALE)
+    base_up = jnp.einsum("pktfe,fper->pktr", latents_blocks, v_by_source, precision=highest)
     back = base_up - target_up + delta_up
 
     onehot = (categories[:, None] == jnp.arange(class_total, dtype=jnp.int32)[None, :]).astype(
@@ -87,7 +93,7 @@
     up_t = (
         jnp.einsum("ed,pre->pdr", frozen_weight, a_weighted, precision=highest)
         - jnp.einsum("pktd,pktr->pdr", targets, hidden_f * scale_k, precision=highest)
-        + jnp.einsum("pqd,prq->pdr", selected_up, gram_weighted, precision=highest)
+        + jnp.einsum("pdq,prq->pdr", up_t, gram_weighted, precision=highest)
     )
     down_t = jnp.einsum("pktd,pktr->pdr", latents, back * scale_k, precision=highest)
     grads = jnp.concatenate([down_t, up_t], axis=2).reshape(

time: 222 us -> 234 us (1.054)
  blocking collectives: 106 us -> 57 us
  waiting for transfers between devices: 13.2 us -> 52.2 us
  starting transfers between devices: 5.79 us -> 20.7 us
  local copies, waits for them, and re-layouts: 48.6 us -> 54.1 us
    all_gather x1 -> x0, blocking collectives: 31.3 us -> none  [local(): v_full = lax.all_gather(v_block, 'fsdp', axis=2, tiled=True)]
    ppermute x0 -> x3, waiting for transfers between devices: none -> 24.5 us  [local(): lax.ppermute(v_block, 'fsdp', [((dst + shift) % fsdp_size, dst) for dst i...]
    all_to_all x1 -> x0, blocking collectives: 19.9 us -> none  [local(): recv = lax.all_to_all(send, 'dp', 0, 0, tiled=True)]
    all_to_all x0 -> x1, waiting for transfers between devices: none -> 9.25 us  [local(): recv = lax.all_to_all(send, 'dp', 0, 0, tiled=True)]
    ppermute x0 -> x3, starting transfers between devices: none -> 9.21 us  [local(): lax.ppermute(v_block, 'fsdp', [((dst + shift) % fsdp_size, dst) for dst i...]
    all_to_all x0 -> x1, starting transfers between devices: none -> 6.95 us  [local(): recv = lax.all_to_all(send, 'dp', 0, 0, tiled=True)]
    reduce_scatter x1, waiting for transfers between devices: 0.02 us -> 4.96 us  [local(): lax.psum_scatter(a_k.transpose(3, 0, 1, 2, 4), 'fsdp', scatter_dimension=...]
    another operation x2 -> x4, local copies, waits for them, and re-layouts: 1.98 us -> 6.37 us  [local(): both = jnp.stack([adapter_down, adapter_up], axis=1)]
  transfers between devices with their start and end apart: 3 -> 7, of which waited for: 2 -> 6; matrix products, arithmetic and copies ran while one was open for 9% -> 6% of each run, Pallas kernels for 0% -> 0%
where the time goes in v6:
time: 234 us; the launch traced here: 233 us
  blocking collectives  57 us (24%)
  local copies, waits for them, and re-layouts  54.1 us (23%)
  waiting for transfers between devices  52.2 us (22%)
  starting transfers between devices  20.7 us (9%)
  between operations  19.1 us (8%)
  matrix products  15.1 us (6%)
  other arithmetic  14.4 us (6%)
    all_to_all x1, blocking collectives, local(): lax.all_to_all(grads.transpose(1, 0, 2, 3), 'dp', 0, 0, tiled=True)  27.3 us
    ppermute x3, waiting for transfers between devices, local(): lax.ppermute(v_block, 'fsdp', [((dst + shift) % fsdp_size, dst) for dst i...  24.5 us
    unnamed x27, local copies, waits for them, and re-layouts  20.2 us
    unnamed x1, blocking collectives  18.6 us
    psum x1, blocking collectives, local(): errdiff = lax.psum(partial_err, 'fsdp') / sample_rows  11 us
    all_to_all x1, waiting for transfers between devices, local(): recv = lax.all_to_all(send, 'dp', 0, 0, tiled=True)  9.25 us
    ppermute x3, starting transfers between devices, local(): lax.ppermute(v_block, 'fsdp', [((dst + shift) % fsdp_size, dst) for dst i...  9.21 us
    ppermute x1, waiting for transfers between devices, fsdp_sum(): return value + lax.ppermute(value, 'fsdp', [(0, 3), (3, 0), (1, 2), (2, 1)])  7.26 us
  transfers between devices with their start and end apart: 7, of which 6 were waited for; matrix products, arithmetic and copies ran while one was open for 6% of the time, Pallas kernels for 0%

profile of v6, /device:TPU:32, one launch (start us, length us, event | category | flops | bytes accessed | tf_op | source)
XLA Modules:
  0.0 232.6 jit_solution(1856845356287794336)
XLA Ops:
  8.0 1.4 dynamic-slice
  9.3 0.8 dynamic-update-slice
  10.1 18.6 %all-reduce = s32[64]{0:T(128)S(1)} all-reduce(s32[64]{0:T(128)S(1)} %dynamic-update-slice), channel_id=1, replica_groups=mesh['dp'=64,'fsdp'=4] {'dp'}, use_global_device_ids=true, to_apply=%add | all-reduce | flops 64 | bytes 512
  28.7 1.0 copy.76
  29.7 1.0 copy.77
  31.1 4.0 %gather_fusion = bf16[64,38,2,64]{3,2,1,0:T(2,128)(2,1)} fusion(bf16[7,38,2,64]{3,2,1,0:T(2,128)(2,1)S(1)} %maximum_bitcast_fusion, s32[1024]{0:T(1024)S(1)} %pad_clamp_fusion), kind=kCustom, calls=%fused_computation | custom fusion | bytes 1245440 | tf_op jit(solution)/shard_map/jit(_take)/gather | solution.py:33
  35.1 3.6 %fusion.5 = bf16[64,1,38,2,64]{4,3,2,1,0:T(2,128)(2,1)} fusion(bf16[64,38,2,64]{3,2,1,0:T(2,128)(2,1)} %gather_fusion, pred[64]{0:T(512)(128)(4,1)S(1)} %compare_and_fusion), kind=kLoop, calls=%fused_computation.13 | loop fusion | flops 311296 | bytes 1245248 | tf_op jit(solution)/shard_map/jit(_take)/select_n | solution.py:33
  38.7 4.2 %reshape.221 = bf16[64,2,2432]{2,1,0:T(2,128)(2,1)} reshape(bf16[64,1,38,2,64]{4,3,2,1,0:T(2,128)(2,1)} %fusion.5) | data formatting | bytes 1245184
  42.9 7.0 %all-to-all-start = ((bf16[64,2,2432]{2,1,0:T(2,128)(2,1)}), bf16[64,2,2432]{2,1,0:T(2,128)(2,1)}, u32[]{:S(2)}, u32[]{:S(2)}) async-start(bf16[64,2,2432]{2,1,0:T(2,128)(2,1)} %reshape.221), calls=%async_computation | async-start | bytes 1245184 | tf_op jit(solution)/shard_map/all_to_all | solution.py:34
  50.7 2.8 %reshape.191 = bf16[2,64,4,608]{3,2,1,0:T(4,128)(2,1)} reshape(bf16[1,2,64,2432]{3,2,1,0:T(8,128)(2,1)} %param.8) | data formatting | bytes 1245184 | tf_op jit(solution)/shard_map/reshape.4
  53.5 9.2 %all-to-all-done = bf16[64,2,2432]{2,1,0:T(2,128)(2,1)} async-done(((bf16[64,2,2432]{2,1,0:T(2,128)(2,1)}), bf16[64,2,2432]{2,1,0:T(2,128)(2,1)}, u32[]{:S(2)}, u32[]{:S(2)}) %all-to-all-start) | async-done | bytes 622624 | tf_op jit(solution)/shard_map/all_to_all | solution.py:34
  62.8 4.2 %reshape.222 = bf16[64,1,38,2,64]{4,3,2,1,0:T(2,128)(2,1)} reshape(bf16[64,2,2432]{2,1,0:T(2,128)(2,1)} %all-to-all-done) | data formatting | bytes 1245184
  66.9 5.0 %fusion.36 = (bf16[1,2432,1,64]{3,2,1,0:T(2,128)(2,1)}, bf16[1,2432,1,64]{3,2,1,0:T(2,128)(2,1)}) fusion(bf16[1,2432,2,64]{3,2,1,0:T(2,128)(2,1)} %bitcast.147), kind=kLoop, calls=%fused_computation.73 | loop fusion | bytes 1245184 | tf_op jit(solution)/shard_map/slice | solution.py:39
  71.9 2.5 %copy.103 = bf16[1,2432,1,64]{1,3,2,0:T(8,128)(2,1)S(1)} copy(bf16[1,2432,1,64]{3,2,1,0:T(2,128)(2,1)} %get-tuple-element.4) | data formatting | bytes 622592
  74.5 1.6 fusion.10
  76.1 1.3 fusion.15
  77.4 3.1 %reshape.195 = f32[1,2,64,4,608]{4,3,2,1,0:T(4,128)} reshape(f32[2,64,2432]{2,1,0:T(8,128)} %fusion.15) | data formatting | bytes 2490368 | tf_op jit(solution)/shard_map/reshape | solution.py:59
  80.5 2.5 %copy.116 = f32[1,2,64,4,608]{4,2,1,0,3:T(8,128)} copy(f32[1,2,64,4,608]{4,3,2,1,0:T(4,128)} %reshape.195) | data formatting | bytes 2490368 | tf_op jit(solution)/shard_map/reshape | solution.py:59
  83.8 2.5 %copy.102 = bf16[1,2432,1,64]{1,3,2,0:T(8,128)(2,1)S(1)} copy(bf16[1,2432,1,64]{3,2,1,0:T(2,128)(2,1)} %get-tuple-element.3) | data formatting | bytes 622592
  86.4 1.6 bitcast_dynamic-update-slice_fusion
  88.0 5.4 %collective-permute-start = (f32[1,608,64]{1,2,0:T(8,128)S(1)}, f32[1,608,64]{1,2,0:T(8,128)S(1)}, u32[]{:S(2)}, u32[]{:S(2)}) collective-permute-start(f32[1,608,64]{1,2,0:T(8,128)S(1)} %bitcast.150), channel_id=1, source_target_pairs={{1,0},{2,1},{3,2},{0,3},{5,4},{6,5},{7,6},{4,7},{9,8},{10,9},{11,1... | collective-permute-start | bytes 466952 | tf_op jit(solution)/shard_map/ppermute | solution.py:48
  93.4 1.4 collective-permute-start.1
  94.9 2.4 %collective-permute-start.2 = (f32[1,608,64]{1,2,0:T(8,128)S(1)}, f32[1,608,64]{1,2,0:T(8,128)S(1)}, u32[]{:S(2)}, u32[]{:S(2)}) collective-permute-start(f32[1,608,64]{1,2,0:T(8,128)S(1)} %bitcast.152), channel_id=1, source_target_pairs={{3,0},{0,1},{1,2},{2,3},{7,4},{4,5},{5,6},{6,7},{11,8},{8,9},{9,10... | collective-permute-start | bytes 466952 | tf_op jit(solution)/shard_map/ppermute | solution.py:48
  97.7 1.1 fusion.28
  98.8 11.9 %collective-permute-done = f32[1,608,64]{1,2,0:T(8,128)S(1)} collective-permute-done((f32[1,608,64]{1,2,0:T(8,128)S(1)}, f32[1,608,64]{1,2,0:T(8,128)S(1)}, u32[]{:S(2)}, u32[]{:S(2)}) %collective-permute-start) | collective-permute-done | bytes 155680 | tf_op jit(solution)/shard_map/ppermute | solution.py:48
  111.4 12.6 %collective-permute-done.1 = f32[1,608,64]{1,2,0:T(8,128)S(1)} collective-permute-done((f32[1,608,64]{1,2,0:T(8,128)S(1)}, f32[1,608,64]{1,2,0:T(8,128)S(1)}, u32[]{:S(2)}, u32[]{:S(2)}) %collective-permute-start.1) | collective-permute-done | bytes 155680 | tf_op jit(solution)/shard_map/ppermute | solution.py:48
  128.0 5.0 %reduce-scatter.2.cloned.1.call-done = f32[1,1,2,64,608]{4,3,2,1,0:T(8,128)} async-done(((f32[4,1,2,64,608]{4,3,2,1,0:T(8,128)}), f32[1,1,2,64,608]{4,3,2,1,0:T(8,128)}) %reduce-scatter.2.cloned.1.call-update) | async-done | bytes 311312 | tf_op jit(solution)/shard_map/reduce_scatter | solution.py:60
  133.0 1.1 fusion.20
  134.1 1.6 bitcast_dynamic-update-slice_fusion.3
  135.7 11.0 %psum.7 = f32[1,2]{1,0:T(1,128)S(1)} all-reduce(f32[1,2]{1,0:T(1,128)S(1)} %add_bitcast_fusion), channel_id=1, replica_groups=mesh['dp'=64,'fsdp'=4] {'fsdp'}, use_global_device_ids=true, to_apply=%region_3.4 | all-reduce | flops 2 | bytes 16 | tf_op jit(solution)/shard_map/psum | solution.py:78
  149.5 2.4 %fusion.8 = f32[2,64,64]{1,2,0:T(8,128)S(1)} fusion(f32[2,64,64]{1,2,0:T(8,128)} %get-tuple-element.10, bf16[2,64,4,608]{3,2,1,0:T(4,128)(2,1)} %reshape.191, f32[8,1,608,64]{2,3,1,0:T(8,128)} %bitcast_dynamic-update-slice_fusion.3, s32[]{:T(128)S(6)} %select_n.35, f32[2,64,64]{1,2,0:T(8,128)S(1)} %fusion.39, f32[2]{0:T(128)S(1)} %multiply_multiply_fusion), kind=kOutput, calls=%fused_computation.19 | convolution fusion | flops 239108096 | bytes 1441804 | tf_op jit(solution)/shard_map/pktfe,fper->pktr/dot_general | solution.py:72
  151.9 1.3 convolution_bitcast_fusion.2
  153.2 2.5 %copy.87 = f32[2432,64]{1,0:T(8,128)} copy(f32[2432,64]{0,1:T(8,128)} %convolution_bitcast_fusion.2) | data formatting | bytes 1245184 | tf_op jit(solution)/shard_map/pktd,pktr->pdr/dot_general | solution.py:98
  155.7 2.4 %concatenate.8 = f32[64,1,38,64]{3,2,0,1:T(8,128)} reshape(f32[2432,64]{1,0:T(8,128)} %copy.87) | data formatting | bytes 1245184 | tf_op jit(solution)/shard_map/concatenate | solution.py:99
  158.1 1.1 fusion.21
  159.2 1.5 convolution_bitcast_fusion.3
  161.3 1.3 fusion
  162.6 2.5 %copy.90 = f32[1,2432,64]{2,1,0:T(8,128)} copy(f32[1,2432,64]{1,2,0:T(8,128)} %fusion) | data formatting | bytes 1245184 | tf_op jit(solution)/shard_map/add | solution.py:94
  165.2 2.4 %concatenate.9 = f32[64,1,38,64]{3,2,0,1:T(8,128)} reshape(f32[1,2432,64]{2,1,0:T(8,128)} %copy.90) | data formatting | bytes 1245184 | tf_op jit(solution)/shard_map/concatenate | solution.py:99
  167.6 2.1 pad_maximum_fusion
  169.7 1.3 copy.91
  171.0 27.3 %all_to_all.10 = f32[64,1,38,128]{3,1,2,0:T(1,128)} all-to-all(f32[64,1,38,128]{3,1,2,0:T(1,128)S(1)} %copy.91), channel_id=1, replica_groups=mesh['dp'=64,'fsdp'=4] {'dp'}, dimensions={0} | all-to-all | bytes 2490368 | tf_op jit(solution)/shard_map/all_to_all | solution.py:103
  198.3 5.3 %reduce.7 = f32[64,38,128]{2,1,0:T(8,128)} reduce(f32[64,1,38,128]{3,1,2,0:T(1,128)} %all_to_all.10, f32[]{:T(128)} %constant.77), dimensions={1}, to_apply=%all_to_all.7.reduce_sub_computation | reduce | bytes 2490372 | tf_op jit(solution)/shard_map/all_to_all | solution.py:103
  203.7 1.9 fusion.2
  205.7 6.2 %collective-permute-done.3 = f32[7,4864]{1,0:T(8,128)S(1)} collective-permute-done((f32[7,4864]{1,0:T(8,128)S(1)}, f32[7,4864]{1,0:T(8,128)S(1)}, u32[]{:S(2)}, u32[]{:S(2)}) %collective-permute-start.3) | collective-permute-done | bytes 136224 | tf_op jit(solution)/shard_map/ppermute | solution.py:14
  211.9 4.2 %collective-permute-start.4 = (f32[7,4864]{1,0:T(8,128)S(1)}, f32[7,4864]{1,0:T(8,128)S(1)}, u32[]{:S(2)}, u32[]{:S(2)}) collective-permute-start(f32[7,4864]{1,0:T(8,128)S(1)} %add.67), channel_id=1, source_target_pairs={{0,3},{3,0},{1,2},{2,1},{4,7},{7,4},{5,6},{6,5},{8,11},{11,8},{9,1... | collective-permute-start | bytes 408584 | tf_op jit(solution)/shard_map/ppermute | solution.py:15
  216.2 7.3 %collective-permute-done.4 = f32[7,4864]{1,0:T(8,128)S(1)} collective-permute-done((f32[7,4864]{1,0:T(8,128)S(1)}, f32[7,4864]{1,0:T(8,128)S(1)}, u32[]{:S(2)}, u32[]{:S(2)}) %collective-permute-start.4) | collective-permute-done | bytes 136224 | tf_op jit(solution)/shard_map/ppermute | solution.py:15
  223.9 0.7 copy_bitcast_fusion.1
  (43 shorter events, 8.4 us)
Async XLA Ops:
  7.2 79.2 %copy-start = (bf16[608,2432]{1,0:T(8,128)(2,1)S(1)}, bf16[608,2432]{1,0:T(8,128)(2,1)}, u32[]{:S(2)}) copy-start(bf16[608,2432]{1,0:T(8,128)(2,1)} %param.10) | copy-start | bytes 8871940
  42.9 19.9 %all-to-all-start = ((bf16[64,2,2432]{2,1,0:T(2,128)(2,1)}), bf16[64,2,2432]{2,1,0:T(2,128)(2,1)}, u32[]{:S(2)}, u32[]{:S(2)}) async-start(bf16[64,2,2432]{2,1,0:T(2,128)(2,1)} %reshape.221), calls=%async_computation | async-start | bytes 1245184 | tf_op jit(solution)/shard_map/all_to_all | solution.py:34
  49.8 83.1 %reduce-scatter.2.cloned.1.call-start = ((), (), s32[]{:S(2)}) async-start(), calls=%async_computation.3 | async-start | bytes 1638400 | tf_op jit(solution)/shard_map/reduce_scatter | solution.py:60
  74.5 1.6 copy-start.1
  86.4 11.3 %copy-start.3 = (bf16[1,2,64,2432]{3,2,1,0:T(8,128)(2,1)S(1)}, bf16[1,2,64,2432]{3,2,1,0:T(8,128)(2,1)}, u32[]{:S(2)}) copy-start(bf16[1,2,64,2432]{3,2,1,0:T(8,128)(2,1)} %param.9) | copy-start | bytes 1867780
  88.0 22.7 %collective-permute-start = (f32[1,608,64]{1,2,0:T(8,128)S(1)}, f32[1,608,64]{1,2,0:T(8,128)S(1)}, u32[]{:S(2)}, u32[]{:S(2)}) collective-permute-start(f32[1,608,64]{1,2,0:T(8,128)S(1)} %bitcast.150), channel_id=1, source_target_pairs={{1,0},{2,1},{3,2},{0,3},{5,4},{6,5},{7,6},{4,7},{9,8},{10,9},{11,1... | collective-permute-start | bytes 466952 | tf_op jit(solution)/shard_map/ppermute | solution.py:48
  93.4 30.6 %collective-permute-start.1 = (f32[1,608,64]{1,2,0:T(8,128)S(1)}, f32[1,608,64]{1,2,0:T(8,128)S(1)}, u32[]{:S(2)}, u32[]{:S(2)}) collective-permute-start(f32[1,608,64]{1,2,0:T(8,128)S(1)} %bitcast.151), channel_id=1, source_target_pairs={{2,0},{3,1},{0,2},{1,3},{6,4},{7,5},{4,6},{5,7},{10,8},{11,9},{8,1... | collective-permute-start | bytes 466952 | tf_op jit(solution)/shard_map/ppermute | solution.py:48
  94.9 29.8 %collective-permute-start.2 = (f32[1,608,64]{1,2,0:T(8,128)S(1)}, f32[1,608,64]{1,2,0:T(8,128)S(1)}, u32[]{:S(2)}, u32[]{:S(2)}) collective-permute-start(f32[1,608,64]{1,2,0:T(8,128)S(1)} %bitcast.152), channel_id=1, source_target_pairs={{3,0},{0,1},{1,2},{2,3},{7,4},{4,5},{5,6},{6,7},{11,8},{8,9},{9,10... | collective-permute-start | bytes 466952 | tf_op jit(solution)/shard_map/ppermute | solution.py:48
  111.4 38.0 %copy-start.6 = (f32[2]{0:T(128)S(1)}, f32[2]{0:T(128)}, u32[]{:S(2)}) copy-start(f32[2]{0:T(128)} %constant.64.clone) | copy-start | bytes 28
  124.7 0.7 copy-start.5
  146.7 5.2 %copy-start.2 = (bf16[1,2,64,2432]{3,2,1,0:T(8,128)(2,1)S(1)}, bf16[1,2,64,2432]{3,2,1,0:T(8,128)(2,1)}, u32[]{:S(2)}) copy-start(bf16[1,2,64,2432]{3,2,1,0:T(8,128)(2,1)} %param.8) | copy-start | bytes 1867780
  159.2 1.5 copy-start.4
  205.6 6.3 %collective-permute-start.3 = (f32[7,4864]{1,0:T(8,128)S(1)}, f32[7,4864]{1,0:T(8,128)S(1)}, u32[]{:S(2)}, u32[]{:S(2)}) collective-permute-start(f32[7,4864]{1,0:T(8,128)S(1)} %fusion.2), channel_id=1, source_target_pairs={{0,1},{1,0},{2,3},{3,2},{4,5},{5,4},{6,7},{7,6},{8,9},{9,8},{10,11... | collective-permute-start | bytes 408584 | tf_op jit(solution)/shard_map/ppermute | solution.py:14
  211.9 11.6 %collective-permute-start.4 = (f32[7,4864]{1,0:T(8,128)S(1)}, f32[7,4864]{1,0:T(8,128)S(1)}, u32[]{:S(2)}, u32[]{:S(2)}) collective-permute-start(f32[7,4864]{1,0:T(8,128)S(1)} %add.67), channel_id=1, source_target_pairs={{0,3},{3,0},{1,2},{2,1},{4,7},{7,4},{5,6},{6,5},{8,11},{11,8},{9,1... | collective-permute-start | bytes 408584 | tf_op jit(solution)/shard_map/ppermute | solution.py:15
Sparse Core Ops, SparseCore 0:
  83.2 49.7 reduce-scatter.1

commit v7 on v5

--- a/solution.py
+++ b/solution.py
@@ -29,22 +29,28 @@
     )
     counts = jnp.sum(onehot_all, axis=0)
 
-    both = jnp.stack([adapter_down, adapter_up], axis=1)
-    send = jnp.take(both, cats_all.reshape(dp_size, pair_local), axis=0)
-    recv = lax.all_to_all(send, "dp", 0, 0, tiled=True)
-    selected = recv.transpose(1, 2, 3, 0, 4).reshape(
-        pair_local, 2, adapter_rank_width, dp_size * col_local
+    both = jnp.stack(
+        [adapter_down.transpose(0, 2, 1), adapter_up.transpose(0, 2, 1)], axis=2
+    ).reshape(class_total, col_local * 2 * adapter_rank_width)
+    send = jnp.dot(
+        onehot_all.astype(jnp.bfloat16), both, preferred_element_type=jnp.float32
+    ).astype(jnp.bfloat16)
+    recv = lax.all_to_all(
+        send.reshape(dp_size, pair_local, col_local * 2 * adapter_rank_width), "dp", 0, 0, tiled=True
     )
-    selected_down = selected[:, 0]
-    selected_up = selected[:, 1]
+    selected = recv.reshape(dp_size, pair_local, col_local, 2, adapter_rank_width).transpose(
+        1, 0, 2, 3, 4
+    ).reshape(pair_local, dp_size * col_local, 2, adapter_rank_width)
+    down_t = selected[:, :, 0]
+    up_t = selected[:, :, 1]
 
     highest = lax.Precision.HIGHEST
     hidden_state = jnp.einsum(
-        "pktd,prd->pktr", latents, selected_down, preferred_element_type=jnp.float32
+        "pktd,pdr->pktr", latents, down_t, preferred_element_type=jnp.float32
     ).astype(jnp.bfloat16)
     hidden_f = hidden_state.astype(jnp.float32)
     v_block = jnp.einsum(
-        "prd,ed->pre", selected_up, frozen_weight, preferred_element_type=jnp.float32
+        "pdr,ed->pre", up_t, frozen_weight, preferred_element_type=jnp.float32
     )
     v_full = lax.all_gather(v_block, "fsdp", axis=2, tiled=True)
     a_k = jnp.einsum(
@@ -55,10 +61,10 @@
     ).reshape(pair_local, 2, adapter_rank_width, in_local)
     base_up = jnp.einsum("pktd,prd->pktr", latents, v_full, precision=highest)
     target_up = jnp.einsum(
-        "pktd,prd->pktr", targets, selected_up, preferred_element_type=jnp.float32
+        "pktd,pdr->pktr", targets, up_t, preferred_element_type=jnp.float32
     )
     up_gram = jnp.einsum(
-        "prd,pqd->prq", selected_up, selected_up, preferred_element_type=jnp.float32
+        "pdr,pdq->prq", up_t, up_t, preferred_element_type=jnp.float32
     )
     delta_up = ADAPTER_SCALE * jnp.einsum("pktr,prq->pktq", hidden_f, up_gram, precision=highest)
     partial_err = jnp.sum(
@@ -87,7 +93,7 @@
     up_t = (
         jnp.einsum("ed,pre->pdr", frozen_weight, a_weighted, precision=highest)
         - jnp.einsum("pktd,pktr->pdr", targets, hidden_f * scale_k, precision=highest)
-        + jnp.einsum("pqd,prq->pdr", selected_up, gram_weighted, precision=highest)
+        + jnp.einsum("pdq,prq->pdr", up_t, gram_weighted, precision=highest)
     )
     down_t = jnp.einsum("pktd,pktr->pdr", latents, back * scale_k, precision=highest)
     grads = jnp.concatenate([down_t, up_t], axis=2).reshape(

time: 222 us -> 226 us (1.018)
  other arithmetic: 13.2 us -> 18.8 us
  local copies, waits for them, and re-layouts: 48.6 us -> 46.1 us
    all_to_all x0 -> x1, other arithmetic: none -> 5.59 us  [local(): lax.all_to_all(send.reshape(dp_size, pair_local, col_local * 2 * adapter_...]
    gather x1 -> x0, local copies, waits for them, and re-layouts: 4.02 us -> none  [local(): send = jnp.take(both, cats_all.reshape(dp_size, pair_local), axis=0)]
    unnamed x1 -> x0, other arithmetic: 3.56 us -> none
    reshape x0 -> x1, other arithmetic: none -> 2.81 us  [local(): send.reshape(dp_size, pair_local, col_local * 2 * adapter_rank_width)]
    dot_general x5 -> x6, matrix products: 4.61 us -> 5.81 us  [the longest x1 1.58 us: local(): jnp.einsum('pktd,pdr->pktr', latents, down_t, preferred_element_type=jnp....]
where the time goes in v7:
time: 226 us; the launch traced here: 225 us
  blocking collectives  106 us (47%)
  local copies, waits for them, and re-layouts  46.1 us (20%)
  between operations  18.9 us (8%)
  other arithmetic  18.8 us (8%)
  matrix products  16.2 us (7%)
  waiting for transfers between devices  13.2 us (6%)
  starting transfers between devices  5.82 us (3%)
    all_gather x1, blocking collectives, local(): v_full = lax.all_gather(v_block, 'fsdp', axis=2, tiled=True)  31.2 us
    all_to_all x1, blocking collectives, local(): lax.all_to_all(grads.transpose(1, 0, 2, 3), 'dp', 0, 0, tiled=True)  25.9 us
    all_to_all x1, blocking collectives, local(): lax.all_to_all(send.reshape(dp_size, pair_local, col_local * 2 * adapter_...  19.9 us
    unnamed x1, blocking collectives  18.6 us
    unnamed x18, local copies, waits for them, and re-layouts  16.8 us
    psum x1, blocking collectives, local(): errdiff = lax.psum(partial_err, 'fsdp') / sample_rows  9.9 us
    ppermute x1, waiting for transfers between devices, fsdp_sum(): return value + lax.ppermute(value, 'fsdp', [(0, 3), (3, 0), (1, 2), (2, 1)])  7.26 us
    concatenate x3, local copies, waits for them, and re-layouts, local(): jnp.concatenate([down_t, up_t], axis=2)  6.08 us
  transfers between devices with their start and end apart: 3, of which 2 were waited for; matrix products, arithmetic and copies ran while one was open for 9% of the time, Pallas kernels for 0%

profile of v7, /device:TPU:32, one launch (start us, length us, event | category | flops | bytes accessed | tf_op | source)
XLA Modules:
  0.0 224.6 jit_solution(7438588306196324028)
XLA Ops:
  7.2 1.1 pad_maximum_fusion.1
  9.3 1.3 dynamic-slice
  10.6 0.8 dynamic-update-slice
  11.4 18.6 %all-reduce = s32[64]{0:T(128)S(1)} all-reduce(s32[64]{0:T(128)S(1)} %dynamic-update-slice), channel_id=1, replica_groups=mesh['dp'=64,'fsdp'=4] {'dp'}, use_global_device_ids=true, to_apply=%add | all-reduce | flops 64 | bytes 512
  30.0 1.2 fusion
  31.2 0.5 broadcast.61
  31.7 2.8 %reduce.8 = bf16[64,4864]{1,0:T(8,128)(2,1)} reduce(bf16[64,1,4864]{2,0,1:T(8,128)(2,1)} %fusion, bf16[]{:T(256)} %broadcast.61), dimensions={1}, to_apply=%copy.46.reduce_sub_computation | reduce | bytes 1245186 | tf_op jit(solution)/shard_map/reshape | solution.py:39
  34.5 2.6 %reshape.170 = bf16[64,2,2432]{2,1,0:T(2,128)(2,1)} reshape(bf16[64,4864]{1,0:T(8,128)(2,1)} %reduce.8) | data formatting | bytes 1245184
  37.1 19.9 %all_to_all.10 = bf16[64,2,2432]{2,1,0:T(2,128)(2,1)} all-to-all(bf16[64,2,2432]{2,1,0:T(2,128)(2,1)} %reshape.170), channel_id=1, replica_groups=mesh['dp'=64,'fsdp'=4] {'dp'}, dimensions={0} | all-to-all | bytes 1245184 | tf_op jit(solution)/shard_map/all_to_all | solution.py:38
  57.1 4.9 %reshape.171 = bf16[64,1,4864]{2,1,0:T(2,128)(2,1)} reshape(bf16[64,2,2432]{2,1,0:T(2,128)(2,1)} %all_to_all.10) | data formatting | bytes 1245184
  61.9 5.6 %reduce.6 = bf16[64,4864]{1,0:T(8,128)(2,1)} reduce(bf16[64,1,4864]{2,1,0:T(2,128)(2,1)} %reshape.171, bf16[]{:T(256)} %constant.42), dimensions={1}, to_apply=%all_to_all.6.reduce_sub_computation | reduce | bytes 1245186 | tf_op jit(solution)/shard_map/all_to_all | solution.py:38
  67.5 3.6 %reshape_transpose_reshape.3 = bf16[1,2432,2,64]{3,2,1,0:T(2,128)(2,1)} reshape(bf16[64,4864]{1,0:T(8,128)(2,1)} %reduce.6) | data formatting | bytes 1245184 | tf_op jit(solution)/shard_map/reshape;transpose;reshape | solution.py:43
  71.1 5.0 %fusion.37 = (bf16[1,2432,1,64]{3,2,1,0:T(2,128)(2,1)}, bf16[1,2432,1,64]{3,2,1,0:T(2,128)(2,1)}) fusion(bf16[1,2432,2,64]{3,2,1,0:T(2,128)(2,1)} %reshape_transpose_reshape.3), kind=kLoop, calls=%fused_computation.61 | loop fusion | bytes 1245184 | tf_op jit(solution)/shard_map/slice | solution.py:45
  76.1 2.5 %copy.66 = bf16[1,2432,1,64]{1,3,2,0:T(8,128)(2,1)S(1)} copy(bf16[1,2432,1,64]{3,2,1,0:T(2,128)(2,1)} %get-tuple-element.4) | data formatting | bytes 622592
  78.7 1.6 fusion.8
  80.3 1.3 fusion.11
  81.6 3.1 %reshape.148 = f32[1,2,64,4,608]{4,3,2,1,0:T(4,128)} reshape(f32[2,64,2432]{2,1,0:T(8,128)} %fusion.11) | data formatting | bytes 2490368 | tf_op jit(solution)/shard_map/reshape | solution.py:58
  84.7 2.5 %copy.77 = f32[1,2,64,4,608]{4,2,1,0,3:T(8,128)} copy(f32[1,2,64,4,608]{4,3,2,1,0:T(4,128)} %reshape.148) | data formatting | bytes 2490368 | tf_op jit(solution)/shard_map/reshape | solution.py:58
  88.0 0.6 fusion.34
  88.6 2.5 %copy.65 = bf16[1,2432,1,64]{1,3,2,0:T(8,128)(2,1)S(1)} copy(bf16[1,2432,1,64]{3,2,1,0:T(2,128)(2,1)} %get-tuple-element.3) | data formatting | bytes 622592
  91.2 1.0 convolution_bitcast_fusion.4
  92.1 31.2 %all-gather.1 = f32[4,608,64]{1,2,0:T(8,128)S(1)} all-gather(f32[1,608,64]{1,2,0:T(8,128)S(1)} %convolution_bitcast_fusion.4), channel_id=2, replica_groups=mesh['dp'=64,'fsdp'=4] {'fsdp'}, dimensions={0}, use_global_device_ids=true | all-gather | bytes 778240 | tf_op jit(solution)/shard_map/all_gather | solution.py:55
  123.3 1.3 copy.48
  124.6 2.2 reshape.161
  126.8 0.2 convolution_bitcast_fusion.5
  127.3 2.3 %fusion.15 = f32[64,2,64]{2,0,1:T(8,128)S(1)} fusion(f32[2432,64,1]{0,1,2:T(8,128)} %reshape.161, bf16[1,2,64,2432]{3,2,1,0:T(8,128)(2,1)} %param.8), kind=kOutput, calls=%fused_computation.27 | convolution fusion | flops 239075328 | bytes 1277952 | tf_op jit(solution)/shard_map/pktd,prd->pktr/dot_general | solution.py:62
  129.7 0.5 fusion.23
  130.2 9.9 %psum.7 = f32[1,2]{1,0:T(1,128)S(1)} all-reduce(f32[1,2]{1,0:T(1,128)S(1)} %bitcast.114), channel_id=1, replica_groups=mesh['dp'=64,'fsdp'=4] {'fsdp'}, use_global_device_ids=true, to_apply=%region_1.0 | all-reduce | flops 2 | bytes 16 | tf_op jit(solution)/shard_map/psum | solution.py:78
  140.1 0.6 fusion.39
  142.8 2.5 %convolution_bitcast_fusion.2 = f32[2432,64]{0,1:T(8,128)} fusion(bf16[1,2,64,2432]{3,2,1,0:T(8,128)(2,1)} %param.8, f32[2,64,64]{1,2,0:T(8,128)S(1)} %get-tuple-element.10, f32[2,64,64]{1,2,0:T(8,128)S(1)} %fusion.40, f32[2]{0:T(128)S(1)} %multiply_multiply_fusion), kind=kOutput, calls=%fused_computation.6 | convolution fusion | flops 239099904 | bytes 1310728 | tf_op jit(solution)/shard_map/pktd,pktr->pdr/dot_general | solution.py:98
  145.3 2.5 %copy.53 = f32[2432,64]{1,0:T(8,128)} copy(f32[2432,64]{0,1:T(8,128)} %convolution_bitcast_fusion.2) | data formatting | bytes 1245184 | tf_op jit(solution)/shard_map/pktd,pktr->pdr/dot_general | solution.py:98
  147.8 2.4 %concatenate.8 = f32[64,1,38,64]{3,2,0,1:T(8,128)} reshape(f32[2432,64]{1,0:T(8,128)} %copy.53) | data formatting | bytes 1245184 | tf_op jit(solution)/shard_map/concatenate | solution.py:99
  150.4 1.1 fusion.17
  151.5 1.5 convolution_bitcast_fusion.3
  153.0 0.6 fusion.2
  153.6 1.3 fusion.1
  154.9 2.5 %copy.57 = f32[1,2432,64]{2,1,0:T(8,128)} copy(f32[1,2432,64]{1,2,0:T(8,128)} %fusion.1) | data formatting | bytes 1245184 | tf_op jit(solution)/shard_map/add | solution.py:94
  157.4 2.4 %concatenate.9 = f32[64,1,38,64]{3,2,0,1:T(8,128)} reshape(f32[1,2432,64]{2,1,0:T(8,128)} %copy.57) | data formatting | bytes 1245184 | tf_op jit(solution)/shard_map/concatenate | solution.py:99
  159.8 2.1 pad_maximum_fusion
  161.9 1.3 copy.58
  163.2 25.9 %all_to_all.11 = f32[64,1,38,128]{3,1,2,0:T(1,128)} all-to-all(f32[64,1,38,128]{3,1,2,0:T(1,128)S(1)} %copy.58), channel_id=1, replica_groups=mesh['dp'=64,'fsdp'=4] {'dp'}, dimensions={0} | all-to-all | bytes 2490368 | tf_op jit(solution)/shard_map/all_to_all | solution.py:103
  189.1 5.3 %reduce.7 = f32[64,38,128]{2,1,0:T(8,128)} reduce(f32[64,1,38,128]{3,1,2,0:T(1,128)} %all_to_all.11, f32[]{:T(128)} %constant.43), dimensions={1}, to_apply=%all_to_all.7.reduce_sub_computation | reduce | bytes 2490372 | tf_op jit(solution)/shard_map/all_to_all | solution.py:103
  194.4 1.9 fusion.3
  196.4 1.1 collective-permute-start
  197.5 5.9 %collective-permute-done = f32[7,4864]{1,0:T(8,128)S(1)} collective-permute-done((f32[7,4864]{1,0:T(8,128)S(1)}, f32[7,4864]{1,0:T(8,128)S(1)}, u32[]{:S(2)}, u32[]{:S(2)}) %collective-permute-start) | collective-permute-done | bytes 136224 | tf_op jit(solution)/shard_map/ppermute | solution.py:14
  203.4 4.7 %collective-permute-start.1 = (f32[7,4864]{1,0:T(8,128)S(1)}, f32[7,4864]{1,0:T(8,128)S(1)}, u32[]{:S(2)}, u32[]{:S(2)}) collective-permute-start(f32[7,4864]{1,0:T(8,128)S(1)} %add.36), channel_id=1, source_target_pairs={{0,3},{3,0},{1,2},{2,1},{4,7},{7,4},{5,6},{6,5},{8,11},{11,8},{9,1... | collective-permute-start | bytes 408584 | tf_op jit(solution)/shard_map/ppermute | solution.py:15
  208.2 7.3 %collective-permute-done.1 = f32[7,4864]{1,0:T(8,128)S(1)} collective-permute-done((f32[7,4864]{1,0:T(8,128)S(1)}, f32[7,4864]{1,0:T(8,128)S(1)}, u32[]{:S(2)}, u32[]{:S(2)}) %collective-permute-start.1) | collective-permute-done | bytes 136224 | tf_op jit(solution)/shard_map/ppermute | solution.py:15
  215.9 0.7 copy_bitcast_fusion.1
  (25 shorter events, 1.3 us)
Async XLA Ops:
  7.2 84.0 %copy-start = (bf16[608,2432]{1,0:T(8,128)(2,1)S(1)}, bf16[608,2432]{1,0:T(8,128)(2,1)}, u32[]{:S(2)}) copy-start(bf16[608,2432]{1,0:T(8,128)(2,1)} %param.10) | copy-start | bytes 8871940
  7.2 143.2 %reduce-scatter.2.cloned.1.call-start = ((), (), s32[]{:S(2)}) async-start(), calls=%async_computation.3 | async-start | bytes 1638400 | tf_op jit(solution)/shard_map/reduce_scatter | solution.py:59
  78.7 1.6 copy-start.1
  126.8 2.8 %copy-start.2 = (bf16[1,2,64,2432]{3,2,1,0:T(8,128)(2,1)S(1)}, bf16[1,2,64,2432]{3,2,1,0:T(8,128)(2,1)}, u32[]{:S(2)}) copy-start(bf16[1,2,64,2432]{3,2,1,0:T(8,128)(2,1)} %param.9) | copy-start | bytes 1867780
  127.1 15.7 %copy-start.4 = (f32[2]{0:T(128)S(1)}, f32[2]{0:T(128)}, u32[]{:S(2)}) copy-start(f32[2]{0:T(128)} %constant.29.clone) | copy-start | bytes 28
  151.5 1.5 copy-start.3
  196.4 7.0 %collective-permute-start = (f32[7,4864]{1,0:T(8,128)S(1)}, f32[7,4864]{1,0:T(8,128)S(1)}, u32[]{:S(2)}, u32[]{:S(2)}) collective-permute-start(f32[7,4864]{1,0:T(8,128)S(1)} %fusion.3), channel_id=1, source_target_pairs={{0,1},{1,0},{2,3},{3,2},{4,5},{5,4},{6,7},{7,6},{8,9},{9,8},{10,11... | collective-permute-start | bytes 408584 | tf_op jit(solution)/shard_map/ppermute | solution.py:14
  203.4 12.0 %collective-permute-start.1 = (f32[7,4864]{1,0:T(8,128)S(1)}, f32[7,4864]{1,0:T(8,128)S(1)}, u32[]{:S(2)}, u32[]{:S(2)}) collective-permute-start(f32[7,4864]{1,0:T(8,128)S(1)} %add.36), channel_id=1, source_target_pairs={{0,3},{3,0},{1,2},{2,1},{4,7},{7,4},{5,6},{6,5},{8,11},{11,8},{9,1... | collective-permute-start | bytes 408584 | tf_op jit(solution)/shard_map/ppermute | solution.py:15
Sparse Core Ops, SparseCore 0:
  87.4 44.6 reduce-scatter.1

commit v8 on v5

--- a/solution.py
+++ b/solution.py
@@ -50,6 +50,7 @@
     a_k = jnp.einsum(
         "pktr,pktd->pkrd", hidden_state, latents, preferred_element_type=jnp.float32
     ).reshape(pair_local, 2, adapter_rank_width, fsdp_size, in_local)
+    a_k, v_full = lax.optimization_barrier((a_k, v_full))
     a_k = lax.psum_scatter(
         a_k.transpose(3, 0, 1, 2, 4), "fsdp", scatter_dimension=0, tiled=True
     ).reshape(pair_local, 2, adapter_rank_width, in_local)

time: 222 us -> 222 us (level)
  blocking collectives: 106 us -> 103 us
  waiting for transfers between devices: 13.2 us -> 16 us
    all_gather x1, blocking collectives: 31.3 us -> 21.4 us  [local(): v_full = lax.all_gather(v_block, 'fsdp', axis=2, tiled=True)]
    all_to_all x1, blocking collectives: 25.8 us -> 29.9 us  [local(): lax.all_to_all(grads.transpose(1, 0, 2, 3), 'dp', 0, 0, tiled=True)]
    psum x1, blocking collectives: 9.91 us -> 12.7 us  [local(): errdiff = lax.psum(partial_err, 'fsdp') / sample_rows]
    reshape x2 -> x1, local copies, waits for them, and re-layouts: 5.63 us -> 3.15 us  [local(): a_k = jnp.einsum('pktr,pktd->pkrd', hidden_state, latents, preferred_elem...]
    optimization_barrier x0 -> x1, local copies, waits for them, and re-layouts: none -> 2.48 us  [local(): a_k, v_full = lax.optimization_barrier((a_k, v_full))]
    reduce_scatter x1, waiting for transfers between devices: 0.02 us -> 2.31 us  [local(): lax.psum_scatter(a_k.transpose(3, 0, 1, 2, 4), 'fsdp', scatter_dimension=...]
  transfers between devices with their start and end apart: 3 -> 3, of which waited for: 2 -> 3; matrix products, arithmetic and copies ran while one was open for 9% -> 6% of each run, Pallas kernels for 0% -> 0%
where the time goes in v8:
time: 222 us; the launch traced here: 221 us
  blocking collectives  103 us (46%)
  local copies, waits for them, and re-layouts  48.7 us (22%)
  between operations  19.1 us (9%)
  waiting for transfers between devices  16 us (7%)
  matrix products  15 us (7%)
  other arithmetic  13.2 us (6%)
  starting transfers between devices  5.9 us (3%)
    all_to_all x1, blocking collectives, local(): lax.all_to_all(grads.transpose(1, 0, 2, 3), 'dp', 0, 0, tiled=True)  29.9 us
    all_gather x1, blocking collectives, local(): v_full = lax.all_gather(v_block, 'fsdp', axis=2, tiled=True)  21.4 us
    all_to_all x1, blocking collectives, local(): recv = lax.all_to_all(send, 'dp', 0, 0, tiled=True)  19.9 us
    unnamed x1, blocking collectives  18.6 us
    unnamed x18, local copies, waits for them, and re-layouts  17.8 us
    psum x1, blocking collectives, local(): errdiff = lax.psum(partial_err, 'fsdp') / sample_rows  12.7 us
    ppermute x1, waiting for transfers between devices, fsdp_sum(): return value + lax.ppermute(value, 'fsdp', [(0, 3), (3, 0), (1, 2), (2, 1)])  7.81 us
    concatenate x3, local copies, waits for them, and re-layouts, local(): jnp.concatenate([down_t, up_t], axis=2)  6.08 us
  transfers between devices with their start and end apart: 3, of which 3 were waited for; matrix products, arithmetic and copies ran while one was open for 6% of the time, Pallas kernels for 0%

profile of v8, /device:TPU:32, one launch (start us, length us, event | category | flops | bytes accessed | tf_op | source)
XLA Modules:
  0.0 220.6 jit_solution(993729971146466486)
XLA Ops:
  8.0 1.3 dynamic-slice
  9.3 0.8 dynamic-update-slice
  10.1 18.6 %all-reduce = s32[64]{0:T(128)S(1)} all-reduce(s32[64]{0:T(128)S(1)} %dynamic-update-slice), channel_id=1, replica_groups=mesh['dp'=64,'fsdp'=4] {'dp'}, use_global_device_ids=true, to_apply=%add | all-reduce | flops 64 | bytes 512
  28.7 1.0 copy.78
  29.7 1.0 copy.77
  30.7 0.4 pad_maximum_fusion.1
  31.1 4.0 %gather_fusion = bf16[64,2,64,38]{2,1,3,0:T(2,128)(2,1)} fusion(bf16[7,2,64,38]{2,1,3,0:T(2,128)(2,1)S(1)} %pad_maximum_fusion.1, s32[1024]{0:T(1024)S(1)} %pad_clamp_fusion), kind=kCustom, calls=%fused_computation | custom fusion | bytes 1245440 | tf_op jit(solution)/shard_map/jit(_take)/gather | solution.py:33
  35.1 3.6 %fusion.40 = bf16[64,1,38,2,64]{4,3,2,1,0:T(2,128)(2,1)} fusion(bf16[64,2,64,38]{2,1,3,0:T(2,128)(2,1)} %gather_fusion, pred[64]{0:T(512)(128)(4,1)S(1)} %compare_and_fusion), kind=kLoop, calls=%fused_computation.67 | loop fusion | flops 311296 | bytes 1245248
  38.7 4.2 %reshape.194 = bf16[64,2,2432]{2,1,0:T(2,128)(2,1)} reshape(bf16[64,1,38,2,64]{4,3,2,1,0:T(2,128)(2,1)} %fusion.40) | data formatting | bytes 1245184
  42.9 19.9 %all_to_all.10 = bf16[64,2,2432]{2,1,0:T(2,128)(2,1)} all-to-all(bf16[64,2,2432]{2,1,0:T(2,128)(2,1)} %reshape.194), channel_id=1, replica_groups=mesh['dp'=64,'fsdp'=4] {'dp'}, dimensions={0} | all-to-all | bytes 1245184 | tf_op jit(solution)/shard_map/all_to_all | solution.py:34
  62.8 4.2 %reshape.195 = bf16[64,1,38,2,64]{4,3,2,1,0:T(2,128)(2,1)} reshape(bf16[64,2,2432]{2,1,0:T(2,128)(2,1)} %all_to_all.10) | data formatting | bytes 1245184
  67.0 5.1 %fusion.37 = (bf16[1,1,64,2432]{2,1,3,0:T(2,128)(2,1)}, bf16[1,1,64,2432]{2,1,3,0:T(2,128)(2,1)}) fusion(bf16[1,2,64,2432]{2,1,3,0:T(2,128)(2,1)} %bitcast.125), kind=kLoop, calls=%fused_computation.64 | loop fusion | bytes 1245184 | tf_op jit(solution)/shard_map/slice | solution.py:39
  72.1 2.5 %copy.102 = bf16[1,1,64,2432]{3,2,1,0:T(8,128)(2,1)S(1)} copy(bf16[1,1,64,2432]{2,1,3,0:T(2,128)(2,1)} %get-tuple-element.8) | data formatting | bytes 622592
  74.6 1.6 fusion.8
  76.2 1.4 fusion.15
  77.6 3.1 %reshape.163 = f32[1,2,64,4,608]{4,3,2,1,0:T(4,128)} reshape(f32[2,64,2432]{2,1,0:T(8,128)} %fusion.15) | data formatting | bytes 2490368 | tf_op jit(solution)/shard_map/reshape | solution.py:52
  80.7 2.5 %copy.103 = bf16[1,1,64,2432]{3,2,1,0:T(8,128)(2,1)S(1)} copy(bf16[1,1,64,2432]{2,1,3,0:T(2,128)(2,1)} %get-tuple-element.7) | data formatting | bytes 622592
  83.3 1.0 convolution_bitcast_fusion.4
  84.2 21.4 %all-gather.1 = f32[4,608,64]{1,2,0:T(8,128)S(1)} all-gather(f32[1,608,64]{1,2,0:T(8,128)S(1)} %convolution_bitcast_fusion.4), channel_id=2, replica_groups=mesh['dp'=64,'fsdp'=4] {'fsdp'}, dimensions={0}, use_global_device_ids=true | all-gather | bytes 778240 | tf_op jit(solution)/shard_map/all_gather | solution.py:49
  105.7 1.3 copy.83
  106.9 2.2 %reshape.184 = f32[2432,64]{0,1:T(8,128)} reshape(f32[4,608,64]{1,0,2:T(4,128)} %copy.83) | data formatting | bytes 1245184
  109.2 2.5 %copy.114 = f32[1,2,64,4,608]{4,2,1,0,3:T(8,128)} copy(f32[1,2,64,4,608]{4,3,2,1,0:T(4,128)} %reshape.163) | data formatting | bytes 2490368 | tf_op jit(solution)/shard_map/optimization_barrier | solution.py:53
  112.5 0.6 fusion.34
  113.4 0.2 fusion.41
  113.6 2.3 %fusion.11 = f32[64,2,64]{2,0,1:T(8,128)S(1)} fusion(f32[1,64,2432]{2,1,0:T(8,128)} %bitcast.128, bf16[1,2,64,2432]{3,2,1,0:T(8,128)(2,1)} %param.8), kind=kOutput, calls=%fused_computation.24 | convolution fusion | flops 239075328 | bytes 1277952 | tf_op jit(solution)/shard_map/pktd,prd->pktr/dot_general | solution.py:57
  116.0 0.5 fusion.24
  116.5 12.7 %psum.7 = f32[1,2]{1,0:T(1,128)S(1)} all-reduce(f32[1,2]{1,0:T(1,128)S(1)} %bitcast.131), channel_id=1, replica_groups=mesh['dp'=64,'fsdp'=4] {'fsdp'}, use_global_device_ids=true, to_apply=%region_1.2 | all-reduce | flops 2 | bytes 16 | tf_op jit(solution)/shard_map/psum | solution.py:73
  129.2 0.6 fusion.39
  131.9 2.5 %convolution_bitcast_fusion.2 = f32[2432,64]{0,1:T(8,128)} fusion(bf16[1,2,64,2432]{3,2,1,0:T(8,128)(2,1)} %param.8, f32[2,64,64]{1,2,0:T(8,128)S(1)} %get-tuple-element.14, f32[2,64,64]{1,2,0:T(8,128)S(1)} %fusion.41, f32[2]{0:T(128)S(1)} %multiply_multiply_fusion), kind=kOutput, calls=%fused_computation.5 | convolution fusion | flops 239099904 | bytes 1310728 | tf_op jit(solution)/shard_map/pktd,pktr->pdr/dot_general | solution.py:93
  134.3 2.6 %copy.87 = f32[2432,64]{1,0:T(8,128)} copy(f32[2432,64]{0,1:T(8,128)} %convolution_bitcast_fusion.2) | data formatting | bytes 1245184 | tf_op jit(solution)/shard_map/pktd,pktr->pdr/dot_general | solution.py:93
  136.9 2.4 %concatenate.8 = f32[64,1,38,64]{3,2,0,1:T(8,128)} reshape(f32[2432,64]{1,0:T(8,128)} %copy.87) | data formatting | bytes 1245184 | tf_op jit(solution)/shard_map/concatenate | solution.py:94
  139.4 2.3 %reduce-scatter.2.cloned.1.call-done = f32[1,1,2,64,608]{4,3,2,1,0:T(8,128)} async-done(((f32[4,1,2,64,608]{4,3,2,1,0:T(8,128)}), f32[1,1,2,64,608]{4,3,2,1,0:T(8,128)}) %reduce-scatter.2.cloned.1.call-update) | async-done | bytes 311312 | tf_op jit(solution)/shard_map/reduce_scatter | solution.py:54
  141.7 1.1 fusion.18
  142.8 1.5 convolution_bitcast_fusion.3
  144.4 0.6 fusion.1
  144.9 1.3 fusion
  146.2 2.5 %copy.91 = f32[1,2432,64]{2,1,0:T(8,128)} copy(f32[1,2432,64]{1,2,0:T(8,128)} %fusion) | data formatting | bytes 1245184 | tf_op jit(solution)/shard_map/add | solution.py:89
  148.8 2.4 %concatenate.9 = f32[64,1,38,64]{3,2,0,1:T(8,128)} reshape(f32[1,2432,64]{2,1,0:T(8,128)} %copy.91) | data formatting | bytes 1245184 | tf_op jit(solution)/shard_map/concatenate | solution.py:94
  151.2 2.1 pad_maximum_fusion
  153.3 1.3 copy.92
  154.6 29.9 %all_to_all.11 = f32[64,1,38,128]{3,1,2,0:T(1,128)} all-to-all(f32[64,1,38,128]{3,1,2,0:T(1,128)S(1)} %copy.92), channel_id=1, replica_groups=mesh['dp'=64,'fsdp'=4] {'dp'}, dimensions={0} | all-to-all | bytes 2490368 | tf_op jit(solution)/shard_map/all_to_all | solution.py:98
  184.5 5.3 %reduce.6 = f32[64,38,128]{2,1,0:T(8,128)} reduce(f32[64,1,38,128]{3,1,2,0:T(1,128)} %all_to_all.11, f32[]{:T(128)} %constant.58), dimensions={1}, to_apply=%all_to_all.7.reduce_sub_computation | reduce | bytes 2490372 | tf_op jit(solution)/shard_map/all_to_all | solution.py:98
  189.8 1.9 fusion.2
  191.7 2.5 %collective-permute-start = (f32[7,4864]{1,0:T(8,128)S(1)}, f32[7,4864]{1,0:T(8,128)S(1)}, u32[]{:S(2)}, u32[]{:S(2)}) collective-permute-start(f32[7,4864]{1,0:T(8,128)S(1)} %fusion.2), channel_id=1, source_target_pairs={{0,1},{1,0},{2,3},{3,2},{4,5},{5,4},{6,7},{7,6},{8,9},{9,8},{10,11... | collective-permute-start | bytes 408584 | tf_op jit(solution)/shard_map/ppermute | solution.py:14
  194.2 5.9 %collective-permute-done = f32[7,4864]{1,0:T(8,128)S(1)} collective-permute-done((f32[7,4864]{1,0:T(8,128)S(1)}, f32[7,4864]{1,0:T(8,128)S(1)}, u32[]{:S(2)}, u32[]{:S(2)}) %collective-permute-start) | collective-permute-done | bytes 136224 | tf_op jit(solution)/shard_map/ppermute | solution.py:14
  200.1 3.4 %collective-permute-start.1 = (f32[7,4864]{1,0:T(8,128)S(1)}, f32[7,4864]{1,0:T(8,128)S(1)}, u32[]{:S(2)}, u32[]{:S(2)}) collective-permute-start(f32[7,4864]{1,0:T(8,128)S(1)} %add.47), channel_id=1, source_target_pairs={{0,3},{3,0},{1,2},{2,1},{4,7},{7,4},{5,6},{6,5},{8,11},{11,8},{9,1... | collective-permute-start | bytes 408584 | tf_op jit(solution)/shard_map/ppermute | solution.py:15
  203.6 7.8 %collective-permute-done.1 = f32[7,4864]{1,0:T(8,128)S(1)} collective-permute-done((f32[7,4864]{1,0:T(8,128)S(1)}, f32[7,4864]{1,0:T(8,128)S(1)}, u32[]{:S(2)}, u32[]{:S(2)}) %collective-permute-start.1) | collective-permute-done | bytes 136224 | tf_op jit(solution)/shard_map/ppermute | solution.py:15
  211.9 0.7 copy_bitcast_fusion.1
  (25 shorter events, 1.0 us)
Async XLA Ops:
  7.2 76.1 %copy-start = (bf16[608,2432]{1,0:T(8,128)(2,1)S(1)}, bf16[608,2432]{1,0:T(8,128)(2,1)}, u32[]{:S(2)}) copy-start(bf16[608,2432]{1,0:T(8,128)(2,1)} %param.10) | copy-start | bytes 8871940
  7.2 134.6 %reduce-scatter.2.cloned.1.call-start = ((), (), s32[]{:S(2)}) async-start(), calls=%async_computation.3 | async-start | bytes 1638400 | tf_op jit(solution)/shard_map/reduce_scatter | solution.py:54
  74.6 1.6 copy-start.1
  111.7 4.3 %copy-start.2 = (bf16[1,2,64,2432]{3,2,1,0:T(8,128)(2,1)S(1)}, bf16[1,2,64,2432]{3,2,1,0:T(8,128)(2,1)}, u32[]{:S(2)}) copy-start(bf16[1,2,64,2432]{3,2,1,0:T(8,128)(2,1)} %param.9) | copy-start | bytes 1867780
  113.4 18.5 %copy-start.4 = (f32[2]{0:T(128)S(1)}, f32[2]{0:T(128)}, u32[]{:S(2)}) copy-start(f32[2]{0:T(128)} %constant.45.clone) | copy-start | bytes 28
  142.8 1.5 copy-start.3
  191.7 8.4 %collective-permute-start = (f32[7,4864]{1,0:T(8,128)S(1)}, f32[7,4864]{1,0:T(8,128)S(1)}, u32[]{:S(2)}, u32[]{:S(2)}) collective-permute-start(f32[7,4864]{1,0:T(8,128)S(1)} %fusion.2), channel_id=1, source_target_pairs={{0,1},{1,0},{2,3},{3,2},{4,5},{5,4},{6,7},{7,6},{8,9},{9,8},{10,11... | collective-permute-start | bytes 408584 | tf_op jit(solution)/shard_map/ppermute | solution.py:14
  200.1 11.3 %collective-permute-start.1 = (f32[7,4864]{1,0:T(8,128)S(1)}, f32[7,4864]{1,0:T(8,128)S(1)}, u32[]{:S(2)}, u32[]{:S(2)}) collective-permute-start(f32[7,4864]{1,0:T(8,128)S(1)} %add.47), channel_id=1, source_target_pairs={{0,3},{3,0},{1,2},{2,1},{4,7},{7,4},{5,6},{6,5},{8,11},{11,8},{9,1... | collective-permute-start | bytes 408584 | tf_op jit(solution)/shard_map/ppermute | solution.py:15
Sparse Core Ops, SparseCore 0:
  111.8 29.8 reduce-scatter.1

commit v9 on v5

--- a/solution.py
+++ b/solution.py
@@ -23,6 +23,25 @@
     in_local = frozen_weight.shape[0]
     sample_rows = row_local * fsdp_size
 
+    own = lax.axis_index("fsdp")
+    shift_ids = jnp.arange(fsdp_size, dtype=jnp.int32)
+    latents_split = latents.reshape(pair_local, 2, row_local, fsdp_size, in_local)
+    blocks_by_shift = jnp.stack(
+        [
+            lax.ppermute(
+                lax.dynamic_index_in_dim(
+                    latents_split, (own + shift) % fsdp_size, axis=3, keepdims=False
+                ),
+                "fsdp",
+                [(src, (src + shift) % fsdp_size) for src in range(fsdp_size)],
+            )
+            if shift
+            else lax.dynamic_index_in_dim(latents_split, own, axis=3, keepdims=False)
+            for shift in range(fsdp_size)
+        ],
+        axis=0,
+    )
+
     cats_all = lax.all_gather(categories, "dp", tiled=True)
     onehot_all = (cats_all[:, None] == jnp.arange(class_total, dtype=jnp.int32)[None, :]).astype(
         jnp.float32
@@ -46,13 +65,20 @@
     v_block = jnp.einsum(
         "prd,ed->pre", selected_up, frozen_weight, preferred_element_type=jnp.float32
     )
-    v_full = lax.all_gather(v_block, "fsdp", axis=2, tiled=True)
+    hidden_cols = hidden_f.transpose(0, 3, 1, 2).reshape(pair_local, adapter_rank_width, 2 * row_local)
+    packed = lax.all_gather(
+        jnp.concatenate([v_block, hidden_cols], axis=2), "fsdp", axis=2, tiled=True
+    ).reshape(pair_local, adapter_rank_width, fsdp_size, in_local + 2 * row_local)
+    v_full = packed[:, :, :, :in_local].reshape(pair_local, adapter_rank_width, fsdp_size * in_local)
+    hidden_all = packed[:, :, :, in_local:].reshape(
+        pair_local, adapter_rank_width, fsdp_size, 2, row_local
+    )
+    hidden_by_shift = jnp.take(hidden_all, (own - shift_ids) % fsdp_size, axis=2).astype(
+        jnp.bfloat16
+    )
     a_k = jnp.einsum(
-        "pktr,pktd->pkrd", hidden_state, latents, preferred_element_type=jnp.float32
-    ).reshape(pair_local, 2, adapter_rank_width, fsdp_size, in_local)
-    a_k = lax.psum_scatter(
-        a_k.transpose(3, 0, 1, 2, 4), "fsdp", scatter_dimension=0, tiled=True
-    ).reshape(pair_local, 2, adapter_rank_width, in_local)
+        "prskt,spkte->pkre", hidden_by_shift, blocks_by_shift, preferred_element_type=jnp.float32
+    )
     base_up = jnp.einsum("pktd,prd->pktr", latents, v_full, precision=highest)
     target_up = jnp.einsum(
         "pktd,prd->pktr", targets, selected_up, preferred_element_type=jnp.float32

time: 222 us -> 211 us (0.950)
  blocking collectives: 106 us -> 87.5 us
  starting transfers between devices: 5.79 us -> 21.7 us
  between operations: 19.1 us -> 5.66 us
  local copies, waits for them, and re-layouts: 48.6 us -> 54.7 us
    all_to_all x1 -> x0, blocking collectives: 19.9 us -> none  [local(): recv = lax.all_to_all(send, 'dp', 0, 0, tiled=True)]
    ppermute x0 -> x3, starting transfers between devices: none -> 9.22 us  [local(): lax.ppermute(lax.dynamic_index_in_dim(latents_split, (own + shift) % fsdp...]
    all_to_all x0 -> x1, starting transfers between devices: none -> 6.95 us  [local(): recv = lax.all_to_all(send, 'dp', 0, 0, tiled=True)]
    dynamic_slice x0 -> x1, local copies, waits for them, and re-layouts: none -> 3.24 us  [local(): lax.dynamic_index_in_dim(latents_split, own, axis=3, keepdims=False)]
    all_to_all x1, blocking collectives: 25.8 us -> 28.7 us  [local(): lax.all_to_all(grads.transpose(1, 0, 2, 3), 'dp', 0, 0, tiled=True)]
    unnamed x18 -> x27, local copies, waits for them, and re-layouts: 17.7 us -> 19.7 us
    reshape x2 -> x3, local copies, waits for them, and re-layouts: 5.63 us -> 3.91 us  [the longest x1 2.79 us: local(): latents.reshape(pair_local, 2, row_local, fsdp_size, in_local)]
  transfers between devices with their start and end apart: 3 -> 6, of which waited for: 2 -> 2; matrix products, arithmetic and copies ran while one was open for 9% -> 17% of each run, Pallas kernels for 0% -> 0%
where the time goes in v9:
time: 211 us; the launch traced here: 210 us
  blocking collectives  87.5 us (41%)
  local copies, waits for them, and re-layouts  54.7 us (26%)
  starting transfers between devices  21.7 us (10%)
  matrix products  15.2 us (7%)
  waiting for transfers between devices  13.2 us (6%)
  other arithmetic  12.3 us (6%)
  between operations  5.66 us (3%)
    all_gather x1, blocking collectives, local(): lax.all_gather(jnp.concatenate([v_block, hidden_cols], axis=2), 'fsdp', a...  29.2 us
    all_to_all x1, blocking collectives, local(): lax.all_to_all(grads.transpose(1, 0, 2, 3), 'dp', 0, 0, tiled=True)  28.7 us
    unnamed x27, local copies, waits for them, and re-layouts  19.7 us
    unnamed x1, blocking collectives  18.6 us
    psum x1, blocking collectives, local(): errdiff = lax.psum(partial_err, 'fsdp') / sample_rows  11 us
    ppermute x3, starting transfers between devices, local(): lax.ppermute(lax.dynamic_index_in_dim(latents_split, (own + shift) % fsdp...  9.22 us
    ppermute x1, waiting for transfers between devices, fsdp_sum(): return value + lax.ppermute(value, 'fsdp', [(0, 3), (3, 0), (1, 2), (2, 1)])  7.26 us
    all_to_all x1, starting transfers between devices, local(): recv = lax.all_to_all(send, 'dp', 0, 0, tiled=True)  6.95 us
  transfers between devices with their start and end apart: 6, of which 2 were waited for; matrix products, arithmetic and copies ran while one was open for 17% of the time, Pallas kernels for 0%

profile of v9, /device:TPU:32, one launch (start us, length us, event | category | flops | bytes accessed | tf_op | source)
XLA Modules:
  0.0 210.1 jit_solution(400880475197987528)
XLA Ops:
  1.4 1.4 dynamic-slice
  2.8 0.8 dynamic-update-slice
  3.6 18.6 %all-reduce = s32[64]{0:T(128)S(1)} all-reduce(s32[64]{0:T(128)S(1)} %dynamic-update-slice), channel_id=1, replica_groups=mesh['dp'=64,'fsdp'=4] {'dp'}, use_global_device_ids=true, to_apply=%add | all-reduce | flops 64 | bytes 512
  22.2 1.0 copy.136
  23.2 1.0 copy.135
  24.6 4.0 %gather_fusion = bf16[64,2,64,38]{2,1,3,0:T(2,128)(2,1)} fusion(bf16[7,2,64,38]{2,1,3,0:T(2,128)(2,1)S(1)} %pad_maximum_fusion.2, s32[1024]{0:T(1024)S(1)} %pad_clamp_fusion.1), kind=kCustom, calls=%fused_computation | custom fusion | bytes 1245440 | tf_op jit(solution)/shard_map/jit(_take)/gather | solution.py:52
  28.6 3.6 %fusion.53 = bf16[64,1,38,2,64]{4,3,2,1,0:T(2,128)(2,1)} fusion(bf16[64,2,64,38]{2,1,3,0:T(2,128)(2,1)} %gather_fusion, pred[64]{0:T(512)(128)(4,1)S(1)} %compare_and_fusion.1), kind=kLoop, calls=%fused_computation.101 | loop fusion | flops 311296 | bytes 1245248
  32.2 4.2 %reshape.264 = bf16[64,2,2432]{2,1,0:T(2,128)(2,1)} reshape(bf16[64,1,38,2,64]{4,3,2,1,0:T(2,128)(2,1)} %fusion.53) | data formatting | bytes 1245184
  36.3 7.0 %all-to-all-start = ((bf16[64,2,2432]{2,1,0:T(2,128)(2,1)}), bf16[64,2,2432]{2,1,0:T(2,128)(2,1)}, u32[]{:S(2)}, u32[]{:S(2)}) async-start(bf16[64,2,2432]{2,1,0:T(2,128)(2,1)} %reshape.264), calls=%async_computation | async-start | bytes 1245184 | tf_op jit(solution)/shard_map/all_to_all | solution.py:53
  43.3 2.8 %reshape.225 = bf16[1,2,64,4,608]{4,3,2,1,0:T(4,128)(2,1)} reshape(bf16[1,2,64,2432]{3,2,1,0:T(8,128)(2,1)} %param.8) | data formatting | bytes 1245184 | tf_op jit(solution)/shard_map/reshape | solution.py:28
  46.1 3.2 %constant_dynamic-slice_fusion.3 = (bf16[1,2,64,1,608]{4,3,2,1,0:T(2,128)(2,1)S(1)}, bf16[1,2,64,1,608]{4,3,2,1,0:T(2,128)(2,1)S(1)}, bf16[1,2,64,1,608]{4,3,2,1,0:T(2,128)(2,1)S(1)}, bf16[1,2,64,1,608]{4,3,2,1,0:T(2,128)(2,1)S(1)}) fusion(bf16[1,2,64,4,608]{4,3,2,1,0:T(4,128)(2,1)} %reshape.225, s32[]{:T(128)S(6)} %select_n.97, s32[]{:T(128)S(6)} %select_n.103, ...), kind=kLoop, calls=%fused_computation.87 | loop fusion | bytes 1245200 | tf_op jit(solution)/shard_map/jit(dynamic_index_in_dim)/dynamic_slice | solution.py:39
  50.0 5.4 %collective-permute-start.2 = (bf16[1,2,64,608]{3,2,1,0:T(8,128)(2,1)}, bf16[1,2,64,608]{3,2,1,0:T(8,128)(2,1)}, u32[]{:S(2)}, u32[]{:S(2)}) collective-permute-start(bf16[1,2,64,608]{3,2,1,0:T(8,128)(2,1)} %bitcast.140), channel_id=1, source_target_pairs={{0,3},{1,0},{2,1},{3,2},{4,7},{5,4},{6,5},{7,6},{8,11},{9,8},{10,9... | collective-permute-start | bytes 466952 | tf_op jit(solution)/shard_map/ppermute | solution.py:31
  56.1 1.4 collective-permute-start.1
  58.3 2.4 %collective-permute-start = (bf16[1,2,64,608]{3,2,1,0:T(8,128)(2,1)}, bf16[1,2,64,608]{3,2,1,0:T(8,128)(2,1)}, u32[]{:S(2)}, u32[]{:S(2)}) collective-permute-start(bf16[1,2,64,608]{3,2,1,0:T(8,128)(2,1)} %bitcast.142), channel_id=1, source_target_pairs={{0,1},{1,2},{2,3},{3,0},{4,5},{5,6},{6,7},{7,4},{8,9},{9,10},{10,1... | collective-permute-start | bytes 466952 | tf_op jit(solution)/shard_map/ppermute | solution.py:31
  62.7 4.2 %reshape.265 = bf16[64,1,38,2,64]{4,3,2,1,0:T(2,128)(2,1)} reshape(bf16[64,2,2432]{2,1,0:T(2,128)(2,1)} %all-to-all-done) | data formatting | bytes 1245184
  66.9 5.0 %fusion.50 = (bf16[1,1,64,2432]{2,1,3,0:T(2,128)(2,1)}, bf16[1,1,64,2432]{2,1,3,0:T(2,128)(2,1)}) fusion(bf16[1,2,64,2432]{2,1,3,0:T(2,128)(2,1)} %bitcast.145), kind=kLoop, calls=%fused_computation.98 | loop fusion | bytes 1245184 | tf_op jit(solution)/shard_map/slice | solution.py:58
  71.9 2.5 %copy.169 = bf16[1,1,64,2432]{3,2,1,0:T(8,128)(2,1)S(1)} copy(bf16[1,1,64,2432]{2,1,3,0:T(2,128)(2,1)} %get-tuple-element.4) | data formatting | bytes 622592
  74.4 1.5 fusion.10
  75.9 2.5 %copy.168 = bf16[1,1,64,2432]{3,2,1,0:T(8,128)(2,1)S(1)} copy(bf16[1,1,64,2432]{2,1,3,0:T(2,128)(2,1)} %get-tuple-element.3) | data formatting | bytes 622592
  78.7 0.9 fusion.54
  79.7 0.9 convolution_bitcast_fusion.5
  80.8 1.0 copy.142
  81.7 29.2 %all_gather.7 = f32[1,64,2944]{1,0,2:T(1,128)S(1)} all-gather(f32[1,64,736]{1,0,2:T(1,128)} %copy.142), channel_id=1, replica_groups=mesh['dp'=64,'fsdp'=4] {'fsdp'}, dimensions={2}, use_global_device_ids=true | all-gather | bytes 942080 | tf_op jit(solution)/shard_map/all_gather | solution.py:69
  111.0 1.1 copy-done.2
  112.4 1.2 fusion.20
  113.6 1.1 fusion.32
  114.7 11.0 %psum.7 = f32[1,2]{1,0:T(1,128)S(1)} all-reduce(f32[1,2]{1,0:T(1,128)S(1)} %bitcast.154), channel_id=1, replica_groups=mesh['dp'=64,'fsdp'=4] {'fsdp'}, use_global_device_ids=true, to_apply=%region_1.2 | all-reduce | flops 2 | bytes 16 | tf_op jit(solution)/shard_map/psum | solution.py:98
  128.3 1.6 slice.39
  130.0 1.0 copy.149
  131.0 1.2 gather_fusion.1
  132.4 1.6 fusion.7
  134.0 1.5 convolution_bitcast_fusion.3
  136.0 1.3 fusion
  137.4 2.5 %copy.153 = f32[1,2432,64]{2,1,0:T(8,128)} copy(f32[1,2432,64]{1,2,0:T(8,128)} %fusion) | data formatting | bytes 1245184 | tf_op jit(solution)/shard_map/add | solution.py:114
  139.9 2.4 %concatenate.13 = f32[64,1,38,64]{3,2,0,1:T(8,128)} reshape(f32[1,2432,64]{2,1,0:T(8,128)} %copy.153) | data formatting | bytes 1245184 | tf_op jit(solution)/shard_map/concatenate | solution.py:119
  142.3 2.5 %convolution_bitcast_fusion.2 = f32[2432,64]{0,1:T(8,128)} fusion(bf16[1,2,64,2432]{3,2,1,0:T(8,128)(2,1)} %param.8, f32[2,64,64]{1,2,0:T(8,128)S(1)} %copy-done.6, f32[2,64,64]{1,2,0:T(8,128)S(1)} %copy-done.5, f32[2]{0:T(128)S(1)} %multiply_multiply_fusion), kind=kOutput, calls=%fused_computation.6 | convolution fusion | flops 239099904 | bytes 1310728 | tf_op jit(solution)/shard_map/pktd,pktr->pdr/dot_general | solution.py:118
  144.8 2.5 %copy.147 = f32[2432,64]{1,0:T(8,128)} copy(f32[2432,64]{0,1:T(8,128)} %convolution_bitcast_fusion.2) | data formatting | bytes 1245184 | tf_op jit(solution)/shard_map/pktd,pktr->pdr/dot_general | solution.py:118
  147.3 2.4 %concatenate.12 = f32[64,1,38,64]{3,2,0,1:T(8,128)} reshape(f32[2432,64]{1,0:T(8,128)} %copy.147) | data formatting | bytes 1245184 | tf_op jit(solution)/shard_map/concatenate | solution.py:119
  149.7 2.1 %pad_maximum_fusion = f32[64,1,38,128]{3,2,0,1:T(8,128)S(1)} fusion(f32[64,1,38,64]{3,2,0,1:T(8,128)} %concatenate.13, f32[64,1,38,64]{3,2,0,1:T(8,128)} %concatenate.12), kind=kLoop, calls=%fused_computation.9 | loop fusion | flops 311296 | bytes 2490368 | tf_op jit(solution)/shard_map/concatenate | solution.py:119
  151.9 1.3 copy.154
  153.1 28.7 %all_to_all.10 = f32[64,1,38,128]{3,1,2,0:T(1,128)} all-to-all(f32[64,1,38,128]{3,1,2,0:T(1,128)S(1)} %copy.154), channel_id=1, replica_groups=mesh['dp'=64,'fsdp'=4] {'dp'}, dimensions={0} | all-to-all | bytes 2490368 | tf_op jit(solution)/shard_map/all_to_all | solution.py:123
  181.8 5.3 %reduce.7 = f32[64,38,128]{2,1,0:T(8,128)} reduce(f32[64,1,38,128]{3,1,2,0:T(1,128)} %all_to_all.10, f32[]{:T(128)} %constant.120), dimensions={1}, to_apply=%all_to_all.7.reduce_sub_computation | reduce | bytes 2490372 | tf_op jit(solution)/shard_map/all_to_all | solution.py:123
  187.1 1.9 fusion.2
  189.0 0.8 collective-permute-start.3
  189.9 5.9 %collective-permute-done.3 = f32[7,4864]{1,0:T(8,128)S(1)} collective-permute-done((f32[7,4864]{1,0:T(8,128)S(1)}, f32[7,4864]{1,0:T(8,128)S(1)}, u32[]{:S(2)}, u32[]{:S(2)}) %collective-permute-start.3) | collective-permute-done | bytes 136224 | tf_op jit(solution)/shard_map/ppermute | solution.py:14
  195.8 4.7 %collective-permute-start.4 = (f32[7,4864]{1,0:T(8,128)S(1)}, f32[7,4864]{1,0:T(8,128)S(1)}, u32[]{:S(2)}, u32[]{:S(2)}) collective-permute-start(f32[7,4864]{1,0:T(8,128)S(1)} %add.123), channel_id=1, source_target_pairs={{0,3},{3,0},{1,2},{2,1},{4,7},{7,4},{5,6},{6,5},{8,11},{11,8},{9,1... | collective-permute-start | bytes 408584 | tf_op jit(solution)/shard_map/ppermute | solution.py:15
  200.6 7.3 %collective-permute-done.4 = f32[7,4864]{1,0:T(8,128)S(1)} collective-permute-done((f32[7,4864]{1,0:T(8,128)S(1)}, f32[7,4864]{1,0:T(8,128)S(1)}, u32[]{:S(2)}, u32[]{:S(2)}) %collective-permute-start.4) | collective-permute-done | bytes 136224 | tf_op jit(solution)/shard_map/ppermute | solution.py:15
  208.3 0.7 copy_bitcast_fusion.4
  (48 shorter events, 6.5 us)
Async XLA Ops:
  0.6 79.1 %copy-start = (bf16[608,2432]{1,0:T(8,128)(2,1)S(1)}, bf16[608,2432]{1,0:T(8,128)(2,1)}, u32[]{:S(2)}) copy-start(bf16[608,2432]{1,0:T(8,128)(2,1)} %param.10) | copy-start | bytes 8871940
  36.3 26.4 %all-to-all-start = ((bf16[64,2,2432]{2,1,0:T(2,128)(2,1)}), bf16[64,2,2432]{2,1,0:T(2,128)(2,1)}, u32[]{:S(2)}, u32[]{:S(2)}) async-start(bf16[64,2,2432]{2,1,0:T(2,128)(2,1)} %reshape.264), calls=%async_computation | async-start | bytes 1245184 | tf_op jit(solution)/shard_map/all_to_all | solution.py:53
  50.0 82.3 %collective-permute-start.2 = (bf16[1,2,64,608]{3,2,1,0:T(8,128)(2,1)}, bf16[1,2,64,608]{3,2,1,0:T(8,128)(2,1)}, u32[]{:S(2)}, u32[]{:S(2)}) collective-permute-start(bf16[1,2,64,608]{3,2,1,0:T(8,128)(2,1)} %bitcast.140), channel_id=1, source_target_pairs={{0,3},{1,0},{2,1},{3,2},{4,7},{5,4},{6,5},{7,6},{8,11},{9,8},{10,9... | collective-permute-start | bytes 466952 | tf_op jit(solution)/shard_map/ppermute | solution.py:31
  56.1 76.2 %collective-permute-start.1 = (bf16[1,2,64,608]{3,2,1,0:T(8,128)(2,1)}, bf16[1,2,64,608]{3,2,1,0:T(8,128)(2,1)}, u32[]{:S(2)}, u32[]{:S(2)}) collective-permute-start(bf16[1,2,64,608]{3,2,1,0:T(8,128)(2,1)} %bitcast.141), channel_id=1, source_target_pairs={{0,2},{1,3},{2,0},{3,1},{4,6},{5,7},{6,4},{7,5},{8,10},{9,11},{10,... | collective-permute-start | bytes 466952 | tf_op jit(solution)/shard_map/ppermute | solution.py:31
  58.3 74.1 %collective-permute-start = (bf16[1,2,64,608]{3,2,1,0:T(8,128)(2,1)}, bf16[1,2,64,608]{3,2,1,0:T(8,128)(2,1)}, u32[]{:S(2)}, u32[]{:S(2)}) collective-permute-start(bf16[1,2,64,608]{3,2,1,0:T(8,128)(2,1)} %bitcast.142), channel_id=1, source_target_pairs={{0,1},{1,2},{2,3},{3,0},{4,5},{5,6},{6,7},{7,4},{8,9},{9,10},{10,1... | collective-permute-start | bytes 466952 | tf_op jit(solution)/shard_map/ppermute | solution.py:31
  110.9 1.2 copy-start.2
  110.9 1.5 copy-start.1
  112.1 1.5 copy-start.3
  112.1 1.6 copy-start.5
  112.4 15.9 %copy-start.7 = (f32[2]{0:T(128)S(1)}, f32[2]{0:T(128)}, u32[]{:S(2)}) copy-start(f32[2]{0:T(128)} %constant.107.clone) | copy-start | bytes 28
  133.9 1.5 copy-start.4
  139.9 2.4 %copy-start.6 = (f32[2,64,64]{1,2,0:T(8,128)S(1)}, f32[2,64,64]{1,2,0:T(8,128)}, u32[]{:S(2)}) copy-start(f32[2,64,64]{1,2,0:T(8,128)} %get-tuple-element.14) | copy-start | bytes 98308
  189.0 6.7 %collective-permute-start.3 = (f32[7,4864]{1,0:T(8,128)S(1)}, f32[7,4864]{1,0:T(8,128)S(1)}, u32[]{:S(2)}, u32[]{:S(2)}) collective-permute-start(f32[7,4864]{1,0:T(8,128)S(1)} %fusion.2), channel_id=1, source_target_pairs={{0,1},{1,0},{2,3},{3,2},{4,5},{5,4},{6,7},{7,6},{8,9},{9,8},{10,11... | collective-permute-start | bytes 408584 | tf_op jit(solution)/shard_map/ppermute | solution.py:14
  195.8 12.0 %collective-permute-start.4 = (f32[7,4864]{1,0:T(8,128)S(1)}, f32[7,4864]{1,0:T(8,128)S(1)}, u32[]{:S(2)}, u32[]{:S(2)}) collective-permute-start(f32[7,4864]{1,0:T(8,128)S(1)} %add.123), channel_id=1, source_target_pairs={{0,3},{3,0},{1,2},{2,1},{4,7},{7,4},{5,6},{6,5},{8,11},{11,8},{9,1... | collective-permute-start | bytes 408584 | tf_op jit(solution)/shard_map/ppermute | solution.py:15

commit v10 on v9

--- a/solution.py
+++ b/solution.py
@@ -110,13 +110,29 @@
     )
     a_weighted = jnp.sum(scale_k * a_k, axis=1)
     gram_weighted = ADAPTER_SCALE * jnp.sum(scale_k * hidden_gram, axis=1)
-    up_t = (
-        jnp.einsum("ed,pre->pdr", frozen_weight, a_weighted, precision=highest)
-        - jnp.einsum("pktd,pktr->pdr", targets, hidden_f * scale_k, precision=highest)
-        + jnp.einsum("pqd,prq->pdr", selected_up, gram_weighted, precision=highest)
+    token_rows = 2 * row_local
+    lhs = jnp.concatenate(
+        [
+            latents.reshape(pair_local, token_rows, feat_width),
+            targets.reshape(pair_local, token_rows, feat_width),
+            jnp.broadcast_to(frozen_weight[None], (pair_local, in_local, feat_width)),
+            selected_up,
+        ],
+        axis=1,
     )
-    down_t = jnp.einsum("pktd,pktr->pdr", latents, back * scale_k, precision=highest)
-    grads = jnp.concatenate([down_t, up_t], axis=2).reshape(
+    zero_tok = jnp.zeros((pair_local, token_rows, adapter_rank_width), jnp.float32)
+    zero_in = jnp.zeros((pair_local, in_local, adapter_rank_width), jnp.float32)
+    zero_rank = jnp.zeros((pair_local, adapter_rank_width, adapter_rank_width), jnp.float32)
+    rhs = jnp.concatenate(
+        [
+            jnp.concatenate([(back * scale_k).reshape(pair_local, token_rows, -1), zero_tok], axis=2),
+            jnp.concatenate([zero_tok, -(hidden_f * scale_k).reshape(pair_local, token_rows, -1)], axis=2),
+            jnp.concatenate([zero_in, a_weighted.transpose(0, 2, 1)], axis=2),
+            jnp.concatenate([zero_rank, gram_weighted.transpose(0, 2, 1)], axis=2),
+        ],
+        axis=1,
+    )
+    grads = jnp.einsum("pjd,pjc->pdc", lhs, rhs, precision=highest).reshape(
         pair_local, dp_size, col_local, 2 * adapter_rank_width
     )
 

time: 211 us -> 203 us (0.962)
  local copies, waits for them, and re-layouts: 54.7 us -> 46.9 us
    unnamed x27, local copies, waits for them, and re-layouts: 19.7 us -> 10.9 us
    another operation x0 -> x1, local copies, waits for them, and re-layouts: none -> 7.61 us
    all_gather x1, blocking collectives: 29.2 us -> 22 us  [local(): lax.all_gather(jnp.concatenate([v_block, hidden_cols], axis=2), 'fsdp', a...]
    dot_general x1 -> x2, local copies, waits for them, and re-layouts: 2.55 us -> 8.7 us  [local(): jnp.einsum('pjd,pjc->pdc', lhs, rhs, precision=highest)]
    concatenate x3 -> x0, local copies, waits for them, and re-layouts: 6.12 us -> none  [local(): jnp.concatenate([down_t, up_t], axis=2)]
    all_to_all x1, blocking collectives: 28.7 us -> 33.4 us  [local(): lax.all_to_all(grads.transpose(1, 0, 2, 3), 'dp', 0, 0, tiled=True)]
    dot_general x0 -> x1, other arithmetic: none -> 3.66 us  [local(): jnp.einsum('pjd,pjc->pdc', lhs, rhs, precision=highest)]
    add x1 -> x0, local copies, waits for them, and re-layouts: 2.53 us -> none  [local(): jnp.einsum('ed,pre->pdr', frozen_weight, a_weighted, precision=highest)]
  transfers between devices with their start and end apart: 6 -> 6, of which waited for: 2 -> 2; matrix products, arithmetic and copies ran while one was open for 17% -> 15% of each run, Pallas kernels for 0% -> 0%
where the time goes in v10:
time: 203 us; the launch traced here: 202 us
  blocking collectives  87.3 us (43%)
  local copies, waits for them, and re-layouts  46.9 us (23%)
  starting transfers between devices  21.6 us (11%)
  matrix products  16.2 us (8%)
  waiting for transfers between devices  13.2 us (7%)
  other arithmetic  10.8 us (5%)
  between operations  5.65 us (3%)
    all_to_all x1, blocking collectives, local(): lax.all_to_all(grads.transpose(1, 0, 2, 3), 'dp', 0, 0, tiled=True)  33.4 us
    all_gather x1, blocking collectives, local(): lax.all_gather(jnp.concatenate([v_block, hidden_cols], axis=2), 'fsdp', a...  22 us
    unnamed x1, blocking collectives  18.6 us
    psum x1, blocking collectives, local(): errdiff = lax.psum(partial_err, 'fsdp') / sample_rows  13.3 us
    unnamed x27, local copies, waits for them, and re-layouts  10.9 us
    ppermute x3, starting transfers between devices, local(): lax.ppermute(lax.dynamic_index_in_dim(latents_split, (own + shift) % fsdp...  9.21 us
    dot_general x2, local copies, waits for them, and re-layouts, local(): jnp.einsum('pjd,pjc->pdc', lhs, rhs, precision=highest)  8.7 us
    another operation x1, local copies, waits for them, and re-layouts  7.61 us
  transfers between devices with their start and end apart: 6, of which 2 were waited for; matrix products, arithmetic and copies ran while one was open for 15% of the time, Pallas kernels for 0%

profile of v10, /device:TPU:32, one launch (start us, length us, event | category | flops | bytes accessed | tf_op | source)
XLA Modules:
  0.0 201.6 jit_solution(10919405610830477413)
XLA Ops:
  1.3 1.3 dynamic-slice
  2.5 0.8 dynamic-update-slice
  3.3 18.6 %all-reduce.4 = s32[64]{0:T(128)S(1)} all-reduce(s32[64]{0:T(128)S(1)} %dynamic-update-slice), channel_id=1, replica_groups=mesh['dp'=64,'fsdp'=4] {'dp'}, use_global_device_ids=true, to_apply=%add.4 | all-reduce | flops 64 | bytes 512
  22.0 1.0 copy.151
  23.0 1.0 copy.152
  24.3 3.1 %gather_fusion = bf16[64,2,64,38]{2,1,3,0:T(2,128)(2,1)S(1)} fusion(bf16[7,2,64,38]{2,1,3,0:T(2,128)(2,1)S(1)} %pad_maximum_fusion.1, s32[1024]{0:T(1024)S(1)} %pad_clamp_fusion.1), kind=kCustom, calls=%fused_computation | custom fusion | bytes 1245440 | tf_op jit(solution)/shard_map/jit(_take)/gather | solution.py:52
  27.4 1.2 fusion.59
  28.6 1.6 reshape.294
  30.2 6.2 %all-to-all-start = ((bf16[64,2,2432]{2,1,0:T(2,128)(2,1)}), bf16[64,2,2432]{2,1,0:T(2,128)(2,1)S(1)}, u32[]{:S(2)}, u32[]{:S(2)}) async-start(bf16[64,2,2432]{2,1,0:T(2,128)(2,1)} %reshape.294), calls=%async_computation | async-start | bytes 1245184 | tf_op jit(solution)/shard_map/all_to_all | solution.py:53
  36.5 0.7 reshape.255
  37.2 1.4 constant_dynamic-slice_fusion.3
  38.6 0.7 copy.215
  39.3 5.4 %collective-permute-start.2 = (bf16[1,2,64,608]{3,2,1,0:T(8,128)(2,1)}, bf16[1,2,64,608]{3,2,1,0:T(8,128)(2,1)}, u32[]{:S(2)}, u32[]{:S(2)}) collective-permute-start(bf16[1,2,64,608]{3,2,1,0:T(8,128)(2,1)} %bitcast.134), channel_id=1, source_target_pairs={{0,3},{1,0},{2,1},{3,2},{4,7},{5,4},{6,5},{7,6},{8,11},{9,8},{10,9... | collective-permute-start | bytes 466952 | tf_op jit(solution)/shard_map/ppermute | solution.py:31
  44.7 0.7 copy.217
  45.4 0.7 copy.216
  46.1 3.8 %collective-permute-start.1 = (bf16[1,2,64,608]{3,2,1,0:T(8,128)(2,1)}, bf16[1,2,64,608]{3,2,1,0:T(8,128)(2,1)}, u32[]{:S(2)}, u32[]{:S(2)}) collective-permute-start(bf16[1,2,64,608]{3,2,1,0:T(8,128)(2,1)} %bitcast.135), channel_id=1, source_target_pairs={{0,2},{1,3},{2,0},{3,1},{4,6},{5,7},{6,4},{7,5},{8,10},{9,11},{10,... | collective-permute-start | bytes 466952 | tf_op jit(solution)/shard_map/ppermute | solution.py:31
  50.5 0.7 copy.218
  52.0 0.7 reshape.295
  52.8 2.7 %fusion.56 = (bf16[1,1,64,2432]{2,1,3,0:T(2,128)(2,1)S(1)}, bf16[1,1,64,2432]{2,1,3,0:T(2,128)(2,1)}) fusion(bf16[1,2,64,2432]{2,1,3,0:T(2,128)(2,1)S(1)} %bitcast.140), kind=kLoop, calls=%fused_computation.109 | loop fusion | bytes 1245184 | tf_op jit(solution)/shard_map/slice | solution.py:57
  55.5 1.2 copy.192
  56.6 1.7 fusion.8
  58.5 2.5 %copy.191 = bf16[1,1,64,2432]{3,2,1,0:T(8,128)(2,1)S(1)} copy(bf16[1,1,64,2432]{2,1,3,0:T(2,128)(2,1)} %get-tuple-element.4) | data formatting | bytes 622592
  61.0 0.9 convolution_bitcast_fusion.3
  61.9 0.9 convolution_bitcast_fusion.2
  62.9 1.0 copy.159
  63.9 22.0 %all_gather.7 = f32[1,64,2944]{1,0,2:T(1,128)S(1)} all-gather(f32[1,64,736]{1,0,2:T(1,128)} %copy.159), channel_id=1, replica_groups=mesh['dp'=64,'fsdp'=4] {'fsdp'}, dimensions={2}, use_global_device_ids=true | all-gather | bytes 942080 | tf_op jit(solution)/shard_map/all_gather | solution.py:69
  87.1 1.8 fusion.16
  88.9 1.0 copy.169
  89.9 2.2 %fusion.42 = (f32[2]{0:T(128)S(1)}, f32[2,64,64]{1,2,0:T(8,128)}) fusion(bf16[2,64,64]{1,2,0:T(8,128)(2,1)S(1)} %fusion.8, f32[2,64,64]{1,2,0:T(8,128)S(1)} %fusion.60, f32[64,2,64]{2,0,1:T(8,128)} %fusion.16, bf16[1,2,64,2432]{3,2,1,0:T(8,128)(2,1)} %param.9, bf16[1,1,64,2432]{3,2,1,0:T(8,128)(2,1)S(1)} %copy.191), kind=kOutput, calls=%fused_computation.71 | convolution fusion | flops 39895040 | bytes 1048584 | tf_op jit(solution)/shard_map/pktd,prd->pktr/dot_general | solution.py:83
  92.1 13.3 %psum.7 = f32[1,2]{1,0:T(1,128)S(1)} all-reduce(f32[1,2]{1,0:T(1,128)S(1)} %bitcast.155), channel_id=1, replica_groups=mesh['dp'=64,'fsdp'=4] {'fsdp'}, use_global_device_ids=true, to_apply=%region_1.2 | all-reduce | flops 2 | bytes 16 | tf_op jit(solution)/shard_map/psum | solution.py:98
  108.2 1.6 add_multiply_fusion
  109.8 1.6 copy.187
  111.3 1.6 copy.188
  112.9 1.2 gather_fusion.1
  114.1 1.6 fusion.5
  115.7 0.9 copy.174
  116.6 3.7 %maximum_bitcast_fusion = bf16[2432,928]{0,1:T(8,128)(2,1)} fusion(bf16[1,64,2432]{2,1,0:T(8,128)(2,1)S(1)} %bitcast.145, bf16[1,608,2432]{2,1,0:T(8,128)(2,1)S(1)} %bitcast.139, bf16[1,128,2432]{2,1,0:T(8,128)(2,1)} %bitcast.147, bf16[1,128,2432]{2,1,0:T(8,128)(2,1)} %bitcast.141), kind=kLoop, calls=%fused_computation.2 | loop fusion | flops 18055168 | bytes 9027584 | tf_op jit(solution)/shard_map/pjd,pjc->pdc/dot_general | solution.py:135
  120.3 7.4 %copy.156 = bf16[2432,928]{1,0:T(8,128)(2,1)} copy(bf16[2432,928]{0,1:T(8,128)(2,1)} %maximum_bitcast_fusion) | data formatting | bytes 9027584 | tf_op jit(solution)/shard_map/pjd,pjc->pdc/dot_general | solution.py:135
  127.7 7.6 %reshape.245 = bf16[64,38,928]{2,1,0:T(8,128)(2,1)} reshape(bf16[2432,928]{1,0:T(8,128)(2,1)} %copy.156) | data formatting | bytes 9027584 | tf_op jit(solution)/shard_map/reshape.124
  135.3 6.3 %convolution_bitcast_fusion = f32[64,1,38,128]{3,2,0,1:T(8,128)S(1)} fusion(bf16[64,38,928]{2,1,0:T(8,128)(2,1)} %reshape.245, f32[1,64,64]{2,1,0:T(8,128)S(1)} %multiply_bitcast_fusion, f32[1,608,64]{2,1,0:T(8,128)S(1)} %bitcast.149, f32[1,128,64]{2,1,0:T(8,128)S(1)} %bitcast.154, f32[1,128,64]{2,1,0:T(8,128)S(1)} %bitcast.153), kind=kOutput, calls=%fused_computation.4 | convolution fusion | flops 3468374016 | bytes 5996544 | tf_op jit(solution)/shard_map/pjd,pjc->pdc/dot_general | solution.py:135
  141.6 1.3 copy.177
  142.9 33.4 %all_to_all.10 = f32[64,1,38,128]{3,1,2,0:T(1,128)S(1)} all-to-all(f32[64,1,38,128]{3,1,2,0:T(1,128)S(1)} %copy.177), channel_id=1, replica_groups=mesh['dp'=64,'fsdp'=4] {'dp'}, dimensions={0} | all-to-all | bytes 2490368 | tf_op jit(solution)/shard_map/all_to_all | solution.py:139
  176.3 3.0 %reduce.7 = f32[64,38,128]{2,1,0:T(8,128)S(1)} reduce(f32[64,1,38,128]{3,1,2,0:T(1,128)S(1)} %all_to_all.10, f32[]{:T(128)} %constant.131), dimensions={1}, to_apply=%all_to_all.7.reduce_sub_computation | reduce | bytes 2490372 | tf_op jit(solution)/shard_map/all_to_all | solution.py:139
  179.9 1.5 collective-permute-start.3
  181.4 5.9 %collective-permute-done.3 = f32[7,4864]{1,0:T(8,128)S(1)} collective-permute-done((f32[7,4864]{1,0:T(8,128)S(1)}, f32[7,4864]{1,0:T(8,128)S(1)}, u32[]{:S(2)}, u32[]{:S(2)}) %collective-permute-start.3) | collective-permute-done | bytes 136224 | tf_op jit(solution)/shard_map/ppermute | solution.py:14
  187.3 4.7 %collective-permute-start.4 = (f32[7,4864]{1,0:T(8,128)S(1)}, f32[7,4864]{1,0:T(8,128)S(1)}, u32[]{:S(2)}, u32[]{:S(2)}) collective-permute-start(f32[7,4864]{1,0:T(8,128)S(1)} %add.127), channel_id=1, source_target_pairs={{0,3},{3,0},{1,2},{2,1},{4,7},{7,4},{5,6},{6,5},{8,11},{11,8},{9,1... | collective-permute-start | bytes 408584 | tf_op jit(solution)/shard_map/ppermute | solution.py:15
  192.1 7.3 %collective-permute-done.4 = f32[7,4864]{1,0:T(8,128)S(1)} collective-permute-done((f32[7,4864]{1,0:T(8,128)S(1)}, f32[7,4864]{1,0:T(8,128)S(1)}, u32[]{:S(2)}, u32[]{:S(2)}) %collective-permute-start.4) | collective-permute-done | bytes 136224 | tf_op jit(solution)/shard_map/ppermute | solution.py:15
  199.8 0.7 copy_bitcast_fusion.4
  (48 shorter events, 4.4 us)
Async XLA Ops:
  28.6 7.8 %copy-start.1 = (bf16[1,2,64,2432]{3,2,1,0:T(8,128)(2,1)S(1)}, bf16[1,2,64,2432]{3,2,1,0:T(8,128)(2,1)}, u32[]{:S(2)}) copy-start(bf16[1,2,64,2432]{3,2,1,0:T(8,128)(2,1)} %param.8) | copy-start | bytes 1867780
  30.2 21.8 %all-to-all-start = ((bf16[64,2,2432]{2,1,0:T(2,128)(2,1)}), bf16[64,2,2432]{2,1,0:T(2,128)(2,1)S(1)}, u32[]{:S(2)}, u32[]{:S(2)}) async-start(bf16[64,2,2432]{2,1,0:T(2,128)(2,1)} %reshape.294), calls=%async_computation | async-start | bytes 1245184 | tf_op jit(solution)/shard_map/all_to_all | solution.py:53
  39.3 74.8 %collective-permute-start.2 = (bf16[1,2,64,608]{3,2,1,0:T(8,128)(2,1)}, bf16[1,2,64,608]{3,2,1,0:T(8,128)(2,1)}, u32[]{:S(2)}, u32[]{:S(2)}) collective-permute-start(bf16[1,2,64,608]{3,2,1,0:T(8,128)(2,1)} %bitcast.134), channel_id=1, source_target_pairs={{0,3},{1,0},{2,1},{3,2},{4,7},{5,4},{6,5},{7,6},{8,11},{9,8},{10,9... | collective-permute-start | bytes 466952 | tf_op jit(solution)/shard_map/ppermute | solution.py:31
  45.4 68.8 %collective-permute-start = (bf16[1,2,64,608]{3,2,1,0:T(8,128)(2,1)}, bf16[1,2,64,608]{3,2,1,0:T(8,128)(2,1)}, u32[]{:S(2)}, u32[]{:S(2)}) collective-permute-start(bf16[1,2,64,608]{3,2,1,0:T(8,128)(2,1)} %bitcast.136), channel_id=1, source_target_pairs={{0,1},{1,2},{2,3},{3,0},{4,5},{5,6},{6,7},{7,4},{8,9},{9,10},{10,1... | collective-permute-start | bytes 466952 | tf_op jit(solution)/shard_map/ppermute | solution.py:31
  46.1 68.1 %collective-permute-start.1 = (bf16[1,2,64,608]{3,2,1,0:T(8,128)(2,1)}, bf16[1,2,64,608]{3,2,1,0:T(8,128)(2,1)}, u32[]{:S(2)}, u32[]{:S(2)}) collective-permute-start(bf16[1,2,64,608]{3,2,1,0:T(8,128)(2,1)} %bitcast.135), channel_id=1, source_target_pairs={{0,2},{1,3},{2,0},{3,1},{4,6},{5,7},{6,4},{7,5},{8,10},{9,11},{10,... | collective-permute-start | bytes 466952 | tf_op jit(solution)/shard_map/ppermute | solution.py:31
  56.6 5.2 %copy-start = (bf16[608,2432]{1,0:T(8,128)(2,1)S(1)}, bf16[608,2432]{1,0:T(8,128)(2,1)}, u32[]{:S(2)}) copy-start(bf16[608,2432]{1,0:T(8,128)(2,1)} %param.10) | copy-start | bytes 8871940
  85.9 0.8 copy-start.6
  85.9 1.1 copy-start.2
  87.1 21.0 %copy-start.7 = (f32[2]{0:T(128)S(1)}, f32[2]{0:T(128)}, u32[]{:S(2)}) copy-start(f32[2]{0:T(128)} %constant.110.clone) | copy-start | bytes 28
  127.7 7.6 %copy-start.3 = (f32[64,608]{0,1:T(8,128)S(1)}, f32[64,608]{0,1:T(8,128)}, u32[]{:S(2)}) copy-start(f32[64,608]{0,1:T(8,128)} %copy.174) | copy-start | bytes 466948
  127.7 7.6 %copy-start.4 = (f32[2,64,64]{2,1,0:T(8,128)S(1)}, f32[2,64,64]{2,1,0:T(8,128)}, u32[]{:S(2)}) copy-start(f32[2,64,64]{2,1,0:T(8,128)} %copy.187) | copy-start | bytes 98308
  127.7 7.6 %copy-start.5 = (f32[2,64,64]{2,1,0:T(8,128)S(1)}, f32[2,64,64]{2,1,0:T(8,128)}, u32[]{:S(2)}) copy-start(f32[2,64,64]{2,1,0:T(8,128)} %copy.188) | copy-start | bytes 98308
  179.9 7.4 %collective-permute-start.3 = (f32[7,4864]{1,0:T(8,128)S(1)}, f32[7,4864]{1,0:T(8,128)S(1)}, u32[]{:S(2)}, u32[]{:S(2)}) collective-permute-start(f32[7,4864]{1,0:T(8,128)S(1)} %fusion), channel_id=1, source_target_pairs={{0,1},{1,0},{2,3},{3,2},{4,5},{5,4},{6,7},{7,6},{8,9},{9,8},{10,11... | collective-permute-start | bytes 408584 | tf_op jit(solution)/shard_map/ppermute | solution.py:14
  187.3 12.0 %collective-permute-start.4 = (f32[7,4864]{1,0:T(8,128)S(1)}, f32[7,4864]{1,0:T(8,128)S(1)}, u32[]{:S(2)}, u32[]{:S(2)}) collective-permute-start(f32[7,4864]{1,0:T(8,128)S(1)} %add.127), channel_id=1, source_target_pairs={{0,3},{3,0},{1,2},{2,1},{4,7},{7,4},{5,6},{6,5},{8,11},{11,8},{9,1... | collective-permute-start | bytes 408584 | tf_op jit(solution)/shard_map/ppermute | solution.py:15

commit v11 on v10

--- a/solution.py
+++ b/solution.py
@@ -132,9 +132,8 @@
         ],
         axis=1,
     )
-    grads = jnp.einsum("pjd,pjc->pdc", lhs, rhs, precision=highest).reshape(
-        pair_local, dp_size, col_local, 2 * adapter_rank_width
-    )
+    grads = lax.optimization_barrier(jnp.einsum("pjc,pjd->pcd", rhs, lhs, precision=highest))
+    grads = grads.reshape(pair_local, 2 * adapter_rank_width, dp_size, col_local).transpose(0, 2, 3, 1)
 
     gathered = lax.all_to_all(grads.transpose(1, 0, 2, 3), "dp", 0, 0, tiled=True).reshape(
         dp_size * pair_local, col_local * 2 * adapter_rank_width

time: 203 us -> 176 us (0.87)
  local copies, waits for them, and re-layouts: 46.9 us -> 30.2 us
  other arithmetic: 10.8 us -> 5.56 us
  matrix products: 16.2 us -> 12.6 us
    dot_general x2 -> x0, local copies, waits for them, and re-layouts: 8.7 us -> none  [local(): jnp.einsum('pjd,pjc->pdc', lhs, rhs, precision=highest)]
    all_gather x1, blocking collectives: 22 us -> 30 us  [local(): lax.all_gather(jnp.concatenate([v_block, hidden_cols], axis=2), 'fsdp', a...]
    all_to_all x1, blocking collectives: 33.4 us -> 26.7 us  [local(): lax.all_to_all(grads.transpose(1, 0, 2, 3), 'dp', 0, 0, tiled=True)]
    another operation x1, local copies, waits for them, and re-layouts: 7.61 us -> 1.28 us  [local(): grads.transpose(1, 0, 2, 3)]
    dot_general x1 -> x0, other arithmetic: 3.66 us -> none  [local(): jnp.einsum('pjd,pjc->pdc', lhs, rhs, precision=highest)]
    unnamed x27 -> x20, local copies, waits for them, and re-layouts: 10.9 us -> 13.5 us
    psum x1, blocking collectives: 13.3 us -> 10.7 us  [local(): errdiff = lax.psum(partial_err, 'fsdp') / sample_rows]
  transfers between devices with their start and end apart: 6 -> 6, of which waited for: 2 -> 2; matrix products, arithmetic and copies ran while one was open for 15% -> 14% of each run, Pallas kernels for 0% -> 0%
where the time goes in v11:
time: 176 us
  blocking collectives  86.1 us (49%)
  local copies, waits for them, and re-layouts  30.2 us (17%)
  starting transfers between devices  22 us (12%)
  waiting for transfers between devices  13.6 us (8%)
  matrix products  12.6 us (7%)
  between operations  5.7 us (3%)
  other arithmetic  5.56 us (3%)
    all_gather x1, blocking collectives, local(): lax.all_gather(jnp.concatenate([v_block, hidden_cols], axis=2), 'fsdp', a...  30 us
    all_to_all x1, blocking collectives, local(): lax.all_to_all(grads.transpose(1, 0, 2, 3), 'dp', 0, 0, tiled=True)  26.7 us
    unnamed x1, blocking collectives  18.6 us
    unnamed x20, local copies, waits for them, and re-layouts  13.5 us
    psum x1, blocking collectives, local(): errdiff = lax.psum(partial_err, 'fsdp') / sample_rows  10.7 us
    ppermute x3, starting transfers between devices, local(): lax.ppermute(lax.dynamic_index_in_dim(latents_split, (own + shift) % fsdp...  10.4 us
    ppermute x1, waiting for transfers between devices, fsdp_sum(): return value + lax.ppermute(value, 'fsdp', [(0, 3), (3, 0), (1, 2), (2, 1)])  7.66 us
    all_to_all x1, starting transfers between devices, local(): recv = lax.all_to_all(send, 'dp', 0, 0, tiled=True)  6.95 us
  transfers between devices with their start and end apart: 6, of which 2 were waited for; matrix products, arithmetic and copies ran while one was open for 14% of the time, Pallas kernels for 0%

profile of v11, /device:TPU:32, one launch (start us, length us, event | category | flops | bytes accessed | tf_op | source)
XLA Modules:
  0.0 175.8 jit_solution(8131214407249722329)
XLA Ops:
  1.3 1.3 dynamic-slice
  2.5 0.8 dynamic-update-slice
  3.3 18.6 %all-reduce.4 = s32[64]{0:T(128)S(1)} all-reduce(s32[64]{0:T(128)S(1)} %dynamic-update-slice), channel_id=1, replica_groups=mesh['dp'=64,'fsdp'=4] {'dp'}, use_global_device_ids=true, to_apply=%add.4 | all-reduce | flops 64 | bytes 512
  22.0 1.0 copy.141
  23.0 1.0 copy.142
  24.0 0.4 pad_maximum_fusion.1
  24.3 3.1 %gather_fusion = bf16[64,2,64,38]{2,1,3,0:T(2,128)(2,1)S(1)} fusion(bf16[7,2,64,38]{2,1,3,0:T(2,128)(2,1)S(1)} %pad_maximum_fusion.1, s32[1024]{0:T(1024)S(1)} %pad_clamp_fusion.1), kind=kCustom, calls=%fused_computation | custom fusion | bytes 1245440 | tf_op jit(solution)/shard_map/jit(_take)/gather | solution.py:52
  27.4 1.2 fusion.68
  28.6 1.6 reshape.289
  30.2 7.0 %all-to-all-start = ((bf16[64,2,2432]{2,1,0:T(2,128)(2,1)}), bf16[64,2,2432]{2,1,0:T(2,128)(2,1)}, u32[]{:S(2)}, u32[]{:S(2)}) async-start(bf16[64,2,2432]{2,1,0:T(2,128)(2,1)} %reshape.289), calls=%async_computation | async-start | bytes 1245184 | tf_op jit(solution)/shard_map/all_to_all | solution.py:53
  37.2 0.7 reshape.247
  38.0 1.4 constant_dynamic-slice_fusion.3
  39.3 0.7 copy.202
  40.0 3.3 %collective-permute-start = (bf16[1,2,64,608]{3,2,1,0:T(8,128)(2,1)}, bf16[1,2,64,608]{3,2,1,0:T(8,128)(2,1)}, u32[]{:S(2)}, u32[]{:S(2)}) collective-permute-start(bf16[1,2,64,608]{3,2,1,0:T(8,128)(2,1)} %bitcast.140), channel_id=1, source_target_pairs={{0,1},{1,2},{2,3},{3,0},{4,5},{5,6},{6,7},{7,4},{8,9},{9,10},{10,1... | collective-permute-start | bytes 466952 | tf_op jit(solution)/shard_map/ppermute | solution.py:31
  43.3 0.7 copy.201
  44.0 4.5 %collective-permute-start.1 = (bf16[1,2,64,608]{3,2,1,0:T(8,128)(2,1)}, bf16[1,2,64,608]{3,2,1,0:T(8,128)(2,1)}, u32[]{:S(2)}, u32[]{:S(2)}) collective-permute-start(bf16[1,2,64,608]{3,2,1,0:T(8,128)(2,1)} %bitcast.139), channel_id=1, source_target_pairs={{0,2},{1,3},{2,0},{3,1},{4,6},{5,7},{6,4},{7,5},{8,10},{9,11},{10,... | collective-permute-start | bytes 466952 | tf_op jit(solution)/shard_map/ppermute | solution.py:31
  48.5 0.7 copy.200
  49.2 2.7 %collective-permute-start.2 = (bf16[1,2,64,608]{3,2,1,0:T(8,128)(2,1)}, bf16[1,2,64,608]{3,2,1,0:T(8,128)(2,1)}, u32[]{:S(2)}, u32[]{:S(2)}) collective-permute-start(bf16[1,2,64,608]{3,2,1,0:T(8,128)(2,1)} %bitcast.138), channel_id=1, source_target_pairs={{0,3},{1,0},{2,1},{3,2},{4,7},{5,4},{6,5},{7,6},{8,11},{9,8},{10,9... | collective-permute-start | bytes 466952 | tf_op jit(solution)/shard_map/ppermute | solution.py:31
  52.5 0.7 copy.203
  53.3 0.6 fusion.53
  54.0 3.4 %reshape.290 = bf16[64,1,38,2,64]{4,3,2,1,0:T(2,128)(2,1)S(1)} reshape(bf16[64,2,2432]{2,1,0:T(2,128)(2,1)} %all-to-all-done) | data formatting | bytes 1245184
  57.3 2.7 %fusion.65 = (bf16[1,1,64,2432]{2,1,3,0:T(2,128)(2,1)}, bf16[1,1,64,2432]{2,1,3,0:T(2,128)(2,1)S(1)}) fusion(bf16[1,2,64,2432]{2,1,3,0:T(2,128)(2,1)S(1)} %bitcast.143), kind=kLoop, calls=%fused_computation.117 | loop fusion | bytes 1245184 | tf_op jit(solution)/shard_map/slice | solution.py:57
  60.0 2.5 %copy.176 = bf16[1,1,64,2432]{3,2,1,0:T(8,128)(2,1)S(1)} copy(bf16[1,1,64,2432]{2,1,3,0:T(2,128)(2,1)} %get-tuple-element.3) | data formatting | bytes 622592
  62.5 0.4 fusion.16
  63.1 1.2 copy.175
  64.3 0.2 convolution_bitcast_fusion.2
  64.6 2.8 %convolution_bitcast_fusion.1 = f32[1,64,608]{2,1,0:T(8,128)S(1)} fusion(bf16[608,2432]{1,0:T(8,128)(2,1)} %param.10, bf16[1,1,64,2432]{3,2,1,0:T(8,128)(2,1)S(1)} %copy.175), kind=kOutput, calls=%fused_computation.19 | convolution fusion | flops 189267968 | bytes 3424256 | tf_op jit(solution)/shard_map/prd,ed->pre/dot_general | solution.py:65
  67.4 0.8 copy.148
  68.3 30.0 %all_gather.7 = f32[1,64,2944]{1,0,2:T(1,128)S(1)} all-gather(f32[1,64,736]{1,0,2:T(1,128)S(1)} %copy.148), channel_id=1, replica_groups=mesh['dp'=64,'fsdp'=4] {'fsdp'}, dimensions={2}, use_global_device_ids=true | all-gather | bytes 942080 | tf_op jit(solution)/shard_map/all_gather | solution.py:69
  98.4 1.2 fusion.24
  99.6 0.2 fusion.69
  99.9 0.5 fusion.50
  100.4 10.7 %psum.7 = f32[1,2]{1,0:T(1,128)S(1)} all-reduce(f32[1,2]{1,0:T(1,128)S(1)} %bitcast.157), channel_id=1, replica_groups=mesh['dp'=64,'fsdp'=4] {'fsdp'}, use_global_device_ids=true, to_apply=%region_1.2 | all-reduce | flops 2 | bytes 16 | tf_op jit(solution)/shard_map/psum | solution.py:98
  111.1 0.6 fusion.67
  114.6 0.6 gather_fusion.1
  115.2 1.4 fusion.13
  116.6 5.1 %fusion.7 = f32[1,128,2432]{2,1,0:T(8,128)} fusion(bf16[1,64,2432]{2,1,0:T(8,128)(2,1)S(1)} %bitcast.151, bf16[1,608,2432]{2,1,0:T(8,128)(2,1)} %bitcast.150, bf16[1,128,2432]{2,1,0:T(8,128)(2,1)S(1)} %bitcast.152, bf16[1,128,2432]{2,1,0:T(8,128)(2,1)S(1)} %bitcast.144, f32[1,64,64]{1,2,0:T(8,128)S(1)} %copy.185, f32[1,608,64]{1,2,0:T(8,128)S(1)} %bitcast.158, ...), kind=kOutput, calls=%fused_computation.10 | convolution fusion | flops 3486429184 | bytes 5996544 | tf_op jit(solution)/shard_map/pjc,pjd->pcd/dot_general | solution.py:135
  121.7 1.7 copy.164
  123.5 1.3 copy.165
  124.8 26.7 %all_to_all.10 = f32[64,1,38,128]{3,1,2,0:T(1,128)S(1)} all-to-all(f32[64,1,38,128]{3,1,2,0:T(1,128)S(1)} %copy.165), channel_id=1, replica_groups=mesh['dp'=64,'fsdp'=4] {'dp'}, dimensions={0} | all-to-all | bytes 2490368 | tf_op jit(solution)/shard_map/all_to_all | solution.py:138
  151.6 3.0 %reduce.7 = f32[64,38,128]{2,1,0:T(8,128)S(1)} reduce(f32[64,1,38,128]{3,1,2,0:T(1,128)S(1)} %all_to_all.10, f32[]{:T(128)} %constant.131), dimensions={1}, to_apply=%all_to_all.7.reduce_sub_computation | reduce | bytes 2490372 | tf_op jit(solution)/shard_map/all_to_all | solution.py:138
  154.5 0.6 fusion.8
  155.1 1.1 collective-permute-start.3
  156.2 5.9 %collective-permute-done.3 = f32[7,4864]{1,0:T(8,128)S(1)} collective-permute-done((f32[7,4864]{1,0:T(8,128)S(1)}, f32[7,4864]{1,0:T(8,128)S(1)}, u32[]{:S(2)}, u32[]{:S(2)}) %collective-permute-start.3) | collective-permute-done | bytes 136224 | tf_op jit(solution)/shard_map/ppermute | solution.py:14
  162.2 3.5 %collective-permute-start.4 = (f32[7,4864]{1,0:T(8,128)S(1)}, f32[7,4864]{1,0:T(8,128)S(1)}, u32[]{:S(2)}, u32[]{:S(2)}) collective-permute-start(f32[7,4864]{1,0:T(8,128)S(1)} %add.127), channel_id=1, source_target_pairs={{0,3},{3,0},{1,2},{2,1},{4,7},{7,4},{5,6},{6,5},{8,11},{11,8},{9,1... | collective-permute-start | bytes 408584 | tf_op jit(solution)/shard_map/ppermute | solution.py:15
  165.8 7.7 %collective-permute-done.4 = f32[7,4864]{1,0:T(8,128)S(1)} collective-permute-done((f32[7,4864]{1,0:T(8,128)S(1)}, f32[7,4864]{1,0:T(8,128)S(1)}, u32[]{:S(2)}, u32[]{:S(2)}) %collective-permute-start.4) | collective-permute-done | bytes 136224 | tf_op jit(solution)/shard_map/ppermute | solution.py:15
  173.7 0.2 fusion.66
  173.9 0.7 copy_bitcast_fusion.4
  (41 shorter events, 1.6 us)
Async XLA Ops:
  28.6 8.6 %copy-start = (bf16[1,2,64,2432]{3,2,1,0:T(8,128)(2,1)S(1)}, bf16[1,2,64,2432]{3,2,1,0:T(8,128)(2,1)}, u32[]{:S(2)}) copy-start(bf16[1,2,64,2432]{3,2,1,0:T(8,128)(2,1)} %param.8) | copy-start | bytes 1867780
  30.2 23.7 %all-to-all-start = ((bf16[64,2,2432]{2,1,0:T(2,128)(2,1)}), bf16[64,2,2432]{2,1,0:T(2,128)(2,1)}, u32[]{:S(2)}, u32[]{:S(2)}) async-start(bf16[64,2,2432]{2,1,0:T(2,128)(2,1)} %reshape.289), calls=%async_computation | async-start | bytes 1245184 | tf_op jit(solution)/shard_map/all_to_all | solution.py:53
  40.0 75.1 %collective-permute-start = (bf16[1,2,64,608]{3,2,1,0:T(8,128)(2,1)}, bf16[1,2,64,608]{3,2,1,0:T(8,128)(2,1)}, u32[]{:S(2)}, u32[]{:S(2)}) collective-permute-start(bf16[1,2,64,608]{3,2,1,0:T(8,128)(2,1)} %bitcast.140), channel_id=1, source_target_pairs={{0,1},{1,2},{2,3},{3,0},{4,5},{5,6},{6,7},{7,4},{8,9},{9,10},{10,1... | collective-permute-start | bytes 466952 | tf_op jit(solution)/shard_map/ppermute | solution.py:31
  44.0 71.2 %collective-permute-start.1 = (bf16[1,2,64,608]{3,2,1,0:T(8,128)(2,1)}, bf16[1,2,64,608]{3,2,1,0:T(8,128)(2,1)}, u32[]{:S(2)}, u32[]{:S(2)}) collective-permute-start(bf16[1,2,64,608]{3,2,1,0:T(8,128)(2,1)} %bitcast.139), channel_id=1, source_target_pairs={{0,2},{1,3},{2,0},{3,1},{4,6},{5,7},{6,4},{7,5},{8,10},{9,11},{10,... | collective-permute-start | bytes 466952 | tf_op jit(solution)/shard_map/ppermute | solution.py:31
  49.2 66.0 %collective-permute-start.2 = (bf16[1,2,64,608]{3,2,1,0:T(8,128)(2,1)}, bf16[1,2,64,608]{3,2,1,0:T(8,128)(2,1)}, u32[]{:S(2)}, u32[]{:S(2)}) collective-permute-start(bf16[1,2,64,608]{3,2,1,0:T(8,128)(2,1)} %bitcast.138), channel_id=1, source_target_pairs={{0,3},{1,0},{2,1},{3,2},{4,7},{5,4},{6,5},{7,6},{8,11},{9,8},{10,9... | collective-permute-start | bytes 466952 | tf_op jit(solution)/shard_map/ppermute | solution.py:31
  98.4 1.5 copy-start.1
  98.4 15.4 %copy-start.3 = (f32[2]{0:T(128)S(1)}, f32[2]{0:T(128)}, u32[]{:S(2)}) copy-start(f32[2]{0:T(128)} %constant.110.clone) | copy-start | bytes 28
  99.9 15.3 %copy-start.2 = (bf16[1,2,64,1,608]{4,2,1,3,0:T(8,128)(2,1)S(1)}, bf16[1,2,64,1,608]{4,2,1,3,0:T(8,128)(2,1)}, u32[]{:S(2)}) copy-start(bf16[1,2,64,1,608]{4,2,1,3,0:T(8,128)(2,1)} %copy.203) | copy-start | bytes 466948
  155.1 7.0 %collective-permute-start.3 = (f32[7,4864]{1,0:T(8,128)S(1)}, f32[7,4864]{1,0:T(8,128)S(1)}, u32[]{:S(2)}, u32[]{:S(2)}) collective-permute-start(f32[7,4864]{1,0:T(8,128)S(1)} %fusion.8), channel_id=1, source_target_pairs={{0,1},{1,0},{2,3},{3,2},{4,5},{5,4},{6,7},{7,6},{8,9},{9,8},{10,11... | collective-permute-start | bytes 408584 | tf_op jit(solution)/shard_map/ppermute | solution.py:14
  162.2 11.3 %collective-permute-start.4 = (f32[7,4864]{1,0:T(8,128)S(1)}, f32[7,4864]{1,0:T(8,128)S(1)}, u32[]{:S(2)}, u32[]{:S(2)}) collective-permute-start(f32[7,4864]{1,0:T(8,128)S(1)} %add.127), channel_id=1, source_target_pairs={{0,3},{3,0},{1,2},{2,1},{4,7},{7,4},{5,6},{6,5},{8,11},{11,8},{9,1... | collective-permute-start | bytes 408584 | tf_op jit(solution)/shard_map/ppermute | solution.py:15

commit v12 on v11

--- a/solution.py
+++ b/solution.py
@@ -9,10 +9,17 @@
 
 
 def fsdp_sum(value, fsdp_size):
-    if fsdp_size != 4:
-        return lax.psum(value, "fsdp")
-    value = value + lax.ppermute(value, "fsdp", [(0, 1), (1, 0), (2, 3), (3, 2)])
-    return value + lax.ppermute(value, "fsdp", [(0, 3), (3, 0), (1, 2), (2, 1)])
+    shifted = [value] + [
+        lax.ppermute(value, "fsdp", [(src, (src + shift) % fsdp_size) for src in range(fsdp_size)])
+        for shift in range(1, fsdp_size)
+    ]
+    own = lax.axis_index("fsdp")
+    doubled = jnp.stack(shifted[::-1] + shifted[::-1], axis=0)
+    by_source = lax.dynamic_slice_in_dim(doubled, (fsdp_size - 1 - own) % fsdp_size, fsdp_size, 0)
+    total = by_source[0]
+    for index in range(1, fsdp_size):
+        total = total + by_source[index]
+    return total
 
 
 def local(latents, targets, frozen_weight, adapter_down, adapter_up, categories, timesteps):

time: 176 us -> 174 us (0.989)
  local copies, waits for them, and re-layouts: 30.2 us -> 27.7 us
  starting transfers between devices: 22 us -> 24.2 us
    ppermute x2 -> x3, starting transfers between devices: 4.64 us -> 6.62 us  [fsdp_sum(): lax.ppermute(value, 'fsdp', [(src, (src + shift) % fsdp_size) for src in...]
    unnamed x20 -> x27, local copies, waits for them, and re-layouts: 13.5 us -> 12.3 us
    ppermute x2 -> x3, waiting for transfers between devices: 13.6 us -> 12.9 us  [fsdp_sum(): lax.ppermute(value, 'fsdp', [(src, (src + shift) % fsdp_size) for src in...]
  transfers between devices with their start and end apart: 6 -> 7, of which waited for: 2 -> 3; matrix products, arithmetic and copies ran while one was open for 14% -> 13% of each run, Pallas kernels for 0% -> 0%
where the time goes in v12:
time: 174 us; the launch traced here: 173 us
  blocking collectives  85.8 us (49%)
  local copies, waits for them, and re-layouts  27.7 us (16%)
  starting transfers between devices  24.2 us (14%)
  waiting for transfers between devices  13 us (7%)
  matrix products  11.5 us (7%)
  between operations  5.77 us (3%)
  other arithmetic  5.57 us (3%)
    all_gather x1, blocking collectives, local(): lax.all_gather(jnp.concatenate([v_block, hidden_cols], axis=2), 'fsdp', a...  30.4 us
    all_to_all x1, blocking collectives, local(): lax.all_to_all(grads.transpose(1, 0, 2, 3), 'dp', 0, 0, tiled=True)  25.9 us
    unnamed x1, blocking collectives  18.6 us
    ppermute x3, waiting for transfers between devices, fsdp_sum(): lax.ppermute(value, 'fsdp', [(src, (src + shift) % fsdp_size) for src in...  12.9 us
    unnamed x27, local copies, waits for them, and re-layouts  12.3 us
    psum x1, blocking collectives, local(): errdiff = lax.psum(partial_err, 'fsdp') / sample_rows  10.8 us
    ppermute x3, starting transfers between devices, local(): lax.ppermute(lax.dynamic_index_in_dim(latents_split, (own + shift) % fsdp...  10.6 us
    all_to_all x1, starting transfers between devices, local(): recv = lax.all_to_all(send, 'dp', 0, 0, tiled=True)  6.95 us
  transfers between devices with their start and end apart: 7, of which 3 were waited for; matrix products, arithmetic and copies ran while one was open for 13% of the time, Pallas kernels for 0%

profile of v12, /device:TPU:32, one launch (start us, length us, event | category | flops | bytes accessed | tf_op | source)
XLA Modules:
  0.0 173.5 jit_solution(15713543620936959970)
XLA Ops:
  1.3 1.3 dynamic-slice
  2.5 0.8 dynamic-update-slice
  3.3 18.6 %all-reduce.4 = s32[64]{0:T(128)S(1)} all-reduce(s32[64]{0:T(128)S(1)} %dynamic-update-slice), channel_id=1, replica_groups=mesh['dp'=64,'fsdp'=4] {'dp'}, use_global_device_ids=true, to_apply=%add.4 | all-reduce | flops 64 | bytes 512
  22.0 1.0 copy.131
  23.0 1.0 copy.132
  24.0 0.4 pad_maximum_fusion.1
  24.3 3.1 %gather_fusion = bf16[64,2,64,38]{2,1,3,0:T(2,128)(2,1)S(1)} fusion(bf16[7,2,64,38]{2,1,3,0:T(2,128)(2,1)S(1)} %pad_maximum_fusion.1, s32[1024]{0:T(1024)S(1)} %pad_clamp_fusion.1), kind=kCustom, calls=%fused_computation | custom fusion | bytes 1245440 | tf_op jit(solution)/shard_map/jit(_take)/gather | solution.py:59
  27.4 1.2 fusion.68
  28.6 1.6 reshape.293
  30.2 7.0 %all-to-all-start = ((bf16[64,2,2432]{2,1,0:T(2,128)(2,1)}), bf16[64,2,2432]{2,1,0:T(2,128)(2,1)}, u32[]{:S(2)}, u32[]{:S(2)}) async-start(bf16[64,2,2432]{2,1,0:T(2,128)(2,1)} %reshape.293), calls=%async_computation | async-start | bytes 1245184 | tf_op jit(solution)/shard_map/all_to_all | solution.py:60
  37.2 0.7 reshape.252
  38.0 1.4 constant_dynamic-slice_fusion.3
  39.4 3.3 %collective-permute-start = (bf16[1,2,64,608]{3,2,1,0:T(8,128)(2,1)S(1)}, bf16[1,2,64,608]{3,2,1,0:T(8,128)(2,1)}, u32[]{:S(2)}, u32[]{:S(2)}) collective-permute-start(bf16[1,2,64,608]{3,2,1,0:T(8,128)(2,1)S(1)} %bitcast.166), channel_id=1, source_target_pairs={{0,1},{1,2},{2,3},{3,0},{4,5},{5,6},{6,7},{7,4},{8,9},{9,10},{10,1... | collective-permute-start | bytes 466952 | tf_op jit(solution)/shard_map/ppermute | solution.py:38
  42.8 4.6 %collective-permute-start.1 = (bf16[1,2,64,608]{3,2,1,0:T(8,128)(2,1)S(1)}, bf16[1,2,64,608]{3,2,1,0:T(8,128)(2,1)}, u32[]{:S(2)}, u32[]{:S(2)}) collective-permute-start(bf16[1,2,64,608]{3,2,1,0:T(8,128)(2,1)S(1)} %bitcast.167), channel_id=1, source_target_pairs={{0,2},{1,3},{2,0},{3,1},{4,6},{5,7},{6,4},{7,5},{8,10},{9,11},{10,... | collective-permute-start | bytes 466952 | tf_op jit(solution)/shard_map/ppermute | solution.py:38
  47.3 0.7 copy.188
  48.0 2.7 %collective-permute-start.2 = (bf16[1,2,64,608]{3,2,1,0:T(8,128)(2,1)}, bf16[1,2,64,608]{3,2,1,0:T(8,128)(2,1)}, u32[]{:S(2)}, u32[]{:S(2)}) collective-permute-start(bf16[1,2,64,608]{3,2,1,0:T(8,128)(2,1)} %bitcast.150), channel_id=1, source_target_pairs={{0,3},{1,0},{2,1},{3,2},{4,7},{5,4},{6,5},{7,6},{8,11},{9,8},{10,9... | collective-permute-start | bytes 466952 | tf_op jit(solution)/shard_map/ppermute | solution.py:38
  51.3 0.7 copy.191
  52.2 0.6 fusion.53
  52.8 3.4 %reshape.294 = bf16[64,1,38,2,64]{4,3,2,1,0:T(2,128)(2,1)S(1)} reshape(bf16[64,2,2432]{2,1,0:T(2,128)(2,1)} %all-to-all-done) | data formatting | bytes 1245184
  56.2 2.7 %fusion.65 = (bf16[1,1,64,2432]{2,1,3,0:T(2,128)(2,1)}, bf16[1,1,64,2432]{2,1,3,0:T(2,128)(2,1)S(1)}) fusion(bf16[1,2,64,2432]{2,1,3,0:T(2,128)(2,1)S(1)} %bitcast.155), kind=kLoop, calls=%fused_computation.128 | loop fusion | bytes 1245184 | tf_op jit(solution)/shard_map/slice | solution.py:64
  58.8 2.5 %copy.166 = bf16[1,1,64,2432]{3,2,1,0:T(8,128)(2,1)S(1)} copy(bf16[1,1,64,2432]{2,1,3,0:T(2,128)(2,1)} %get-tuple-element.3) | data formatting | bytes 622592
  61.4 0.4 fusion.16
  62.0 1.2 copy.165
  63.2 0.2 convolution_bitcast_fusion.2
  63.4 2.8 %convolution_bitcast_fusion.1 = f32[1,64,608]{2,1,0:T(8,128)S(1)} fusion(bf16[608,2432]{1,0:T(8,128)(2,1)} %param.10, bf16[1,1,64,2432]{3,2,1,0:T(8,128)(2,1)S(1)} %copy.165), kind=kOutput, calls=%fused_computation.19 | convolution fusion | flops 189267968 | bytes 3424256 | tf_op jit(solution)/shard_map/prd,ed->pre/dot_general | solution.py:72
  66.3 0.8 copy.138
  67.1 30.4 %all_gather.7 = f32[1,64,2944]{1,0,2:T(1,128)S(1)} all-gather(f32[1,64,736]{1,0,2:T(1,128)S(1)} %copy.138), channel_id=1, replica_groups=mesh['dp'=64,'fsdp'=4] {'fsdp'}, dimensions={2}, use_global_device_ids=true | all-gather | bytes 942080 | tf_op jit(solution)/shard_map/all_gather | solution.py:76
  97.7 1.2 fusion.24
  98.9 0.2 fusion.69
  99.1 0.5 fusion.50
  99.7 10.8 %psum.7 = f32[1,2]{1,0:T(1,128)S(1)} all-reduce(f32[1,2]{1,0:T(1,128)S(1)} %bitcast.171), channel_id=1, replica_groups=mesh['dp'=64,'fsdp'=4] {'fsdp'}, use_global_device_ids=true, to_apply=%region_1.2 | all-reduce | flops 2 | bytes 16 | tf_op jit(solution)/shard_map/psum | solution.py:105
  110.5 0.6 fusion.67
  114.0 0.6 gather_fusion.1
  114.6 1.4 fusion.13
  116.0 4.0 %fusion.7 = f32[1,128,2432]{2,1,0:T(8,128)S(1)} fusion(bf16[1,64,2432]{2,1,0:T(8,128)(2,1)S(1)} %bitcast.163, bf16[1,608,2432]{2,1,0:T(8,128)(2,1)} %bitcast.162, bf16[1,128,2432]{2,1,0:T(8,128)(2,1)S(1)} %bitcast.164, bf16[1,128,2432]{2,1,0:T(8,128)(2,1)S(1)} %bitcast.156, f32[1,64,64]{1,2,0:T(8,128)S(1)} %copy.173, f32[1,608,64]{1,2,0:T(8,128)S(1)} %bitcast.172, ...), kind=kOutput, calls=%fused_computation.10 | convolution fusion | flops 3486429184 | bytes 5996544 | tf_op jit(solution)/shard_map/pjc,pjd->pcd/dot_general | solution.py:142
  120.1 0.4 copy.154
  120.6 1.3 copy.155
  121.9 25.9 %all_to_all.10 = f32[64,1,38,128]{3,1,2,0:T(1,128)S(1)} all-to-all(f32[64,1,38,128]{3,1,2,0:T(1,128)S(1)} %copy.155), channel_id=1, replica_groups=mesh['dp'=64,'fsdp'=4] {'dp'}, dimensions={0} | all-to-all | bytes 2490368 | tf_op jit(solution)/shard_map/all_to_all | solution.py:145
  147.8 3.0 %reduce.7 = f32[64,38,128]{2,1,0:T(8,128)S(1)} reduce(f32[64,1,38,128]{3,1,2,0:T(1,128)S(1)} %all_to_all.10, f32[]{:T(128)} %constant.138), dimensions={1}, to_apply=%all_to_all.7.reduce_sub_computation | reduce | bytes 2490372 | tf_op jit(solution)/shard_map/all_to_all | solution.py:145
  150.7 0.6 fusion.8
  151.3 1.5 collective-permute-start.3
  152.9 3.5 %collective-permute-start.4 = (f32[7,4864]{1,0:T(8,128)S(1)}, f32[7,4864]{1,0:T(8,128)S(1)}, u32[]{:S(2)}, u32[]{:S(2)}) collective-permute-start(f32[7,4864]{1,0:T(8,128)S(1)} %fusion.8), channel_id=1, source_target_pairs={{0,2},{1,3},{2,0},{3,1},{4,6},{5,7},{6,4},{7,5},{8,10},{9,11},{10,... | collective-permute-start | bytes 408584 | tf_op jit(solution)/shard_map/ppermute | solution.py:13
  156.4 1.6 collective-permute-start.5
  158.0 4.0 %collective-permute-done.3 = f32[7,4864]{1,0:T(8,128)S(1)} collective-permute-done((f32[7,4864]{1,0:T(8,128)S(1)}, f32[7,4864]{1,0:T(8,128)S(1)}, u32[]{:S(2)}, u32[]{:S(2)}) %collective-permute-start.3) | collective-permute-done | bytes 136224 | tf_op jit(solution)/shard_map/ppermute | solution.py:13
  162.0 7.0 %collective-permute-done.4 = f32[7,4864]{1,0:T(8,128)S(1)} collective-permute-done((f32[7,4864]{1,0:T(8,128)S(1)}, f32[7,4864]{1,0:T(8,128)S(1)}, u32[]{:S(2)}, u32[]{:S(2)}) %collective-permute-start.4) | collective-permute-done | bytes 136224 | tf_op jit(solution)/shard_map/ppermute | solution.py:13
  169.1 2.0 %collective-permute-done.5 = f32[7,4864]{1,0:T(8,128)S(1)} collective-permute-done((f32[7,4864]{1,0:T(8,128)S(1)}, f32[7,4864]{1,0:T(8,128)S(1)}, u32[]{:S(2)}, u32[]{:S(2)}) %collective-permute-start.5) | collective-permute-done | bytes 136224 | tf_op jit(solution)/shard_map/ppermute | solution.py:13
  171.4 0.2 fusion.66
  171.6 0.7 copy_bitcast_fusion.4
  (50 shorter events, 1.7 us)
Async XLA Ops:
  28.6 8.6 %copy-start = (bf16[1,2,64,2432]{3,2,1,0:T(8,128)(2,1)S(1)}, bf16[1,2,64,2432]{3,2,1,0:T(8,128)(2,1)}, u32[]{:S(2)}) copy-start(bf16[1,2,64,2432]{3,2,1,0:T(8,128)(2,1)} %param.8) | copy-start | bytes 1867780
  30.2 22.6 %all-to-all-start = ((bf16[64,2,2432]{2,1,0:T(2,128)(2,1)}), bf16[64,2,2432]{2,1,0:T(2,128)(2,1)}, u32[]{:S(2)}, u32[]{:S(2)}) async-start(bf16[64,2,2432]{2,1,0:T(2,128)(2,1)} %reshape.293), calls=%async_computation | async-start | bytes 1245184 | tf_op jit(solution)/shard_map/all_to_all | solution.py:60
  39.4 75.2 %collective-permute-start = (bf16[1,2,64,608]{3,2,1,0:T(8,128)(2,1)S(1)}, bf16[1,2,64,608]{3,2,1,0:T(8,128)(2,1)}, u32[]{:S(2)}, u32[]{:S(2)}) collective-permute-start(bf16[1,2,64,608]{3,2,1,0:T(8,128)(2,1)S(1)} %bitcast.166), channel_id=1, source_target_pairs={{0,1},{1,2},{2,3},{3,0},{4,5},{5,6},{6,7},{7,4},{8,9},{9,10},{10,1... | collective-permute-start | bytes 466952 | tf_op jit(solution)/shard_map/ppermute | solution.py:38
  42.8 71.8 %collective-permute-start.1 = (bf16[1,2,64,608]{3,2,1,0:T(8,128)(2,1)S(1)}, bf16[1,2,64,608]{3,2,1,0:T(8,128)(2,1)}, u32[]{:S(2)}, u32[]{:S(2)}) collective-permute-start(bf16[1,2,64,608]{3,2,1,0:T(8,128)(2,1)S(1)} %bitcast.167), channel_id=1, source_target_pairs={{0,2},{1,3},{2,0},{3,1},{4,6},{5,7},{6,4},{7,5},{8,10},{9,11},{10,... | collective-permute-start | bytes 466952 | tf_op jit(solution)/shard_map/ppermute | solution.py:38
  48.0 66.5 %collective-permute-start.2 = (bf16[1,2,64,608]{3,2,1,0:T(8,128)(2,1)}, bf16[1,2,64,608]{3,2,1,0:T(8,128)(2,1)}, u32[]{:S(2)}, u32[]{:S(2)}) collective-permute-start(bf16[1,2,64,608]{3,2,1,0:T(8,128)(2,1)} %bitcast.150), channel_id=1, source_target_pairs={{0,3},{1,0},{2,1},{3,2},{4,7},{5,4},{6,5},{7,6},{8,11},{9,8},{10,9... | collective-permute-start | bytes 466952 | tf_op jit(solution)/shard_map/ppermute | solution.py:38
  97.6 1.5 copy-start.1
  97.7 15.5 %copy-start.3 = (f32[2]{0:T(128)S(1)}, f32[2]{0:T(128)}, u32[]{:S(2)}) copy-start(f32[2]{0:T(128)} %constant.117.clone) | copy-start | bytes 28
  99.1 15.4 %copy-start.2 = (bf16[1,2,64,1,608]{4,2,1,3,0:T(8,128)(2,1)S(1)}, bf16[1,2,64,1,608]{4,2,1,3,0:T(8,128)(2,1)}, u32[]{:S(2)}) copy-start(bf16[1,2,64,1,608]{4,2,1,3,0:T(8,128)(2,1)} %copy.191) | copy-start | bytes 466948
  151.3 10.7 %collective-permute-start.3 = (f32[7,4864]{1,0:T(8,128)S(1)}, f32[7,4864]{1,0:T(8,128)S(1)}, u32[]{:S(2)}, u32[]{:S(2)}) collective-permute-start(f32[7,4864]{1,0:T(8,128)S(1)} %fusion.8), channel_id=1, source_target_pairs={{0,3},{1,0},{2,1},{3,2},{4,7},{5,4},{6,5},{7,6},{8,11},{9,8},{10,9... | collective-permute-start | bytes 408584 | tf_op jit(solution)/shard_map/ppermute | solution.py:13
  152.9 16.1 %collective-permute-start.4 = (f32[7,4864]{1,0:T(8,128)S(1)}, f32[7,4864]{1,0:T(8,128)S(1)}, u32[]{:S(2)}, u32[]{:S(2)}) collective-permute-start(f32[7,4864]{1,0:T(8,128)S(1)} %fusion.8), channel_id=1, source_target_pairs={{0,2},{1,3},{2,0},{3,1},{4,6},{5,7},{6,4},{7,5},{8,10},{9,11},{10,... | collective-permute-start | bytes 408584 | tf_op jit(solution)/shard_map/ppermute | solution.py:13
  156.4 14.6 %collective-permute-start.5 = (f32[7,4864]{1,0:T(8,128)S(1)}, f32[7,4864]{1,0:T(8,128)S(1)}, u32[]{:S(2)}, u32[]{:S(2)}) collective-permute-start(f32[7,4864]{1,0:T(8,128)S(1)} %fusion.8), channel_id=1, source_target_pairs={{0,1},{1,2},{2,3},{3,0},{4,5},{5,6},{6,7},{7,4},{8,9},{9,10},{10,1... | collective-permute-start | bytes 408584 | tf_op jit(solution)/shard_map/ppermute | solution.py:13

commit v13 on v12

--- a/solution.py
+++ b/solution.py
@@ -102,7 +102,7 @@
     onehot = (categories[:, None] == jnp.arange(class_total, dtype=jnp.int32)[None, :]).astype(
         jnp.float32
     )
-    errdiff = lax.psum(partial_err, "fsdp") / sample_rows
+    errdiff = fsdp_sum(partial_err, fsdp_size) / sample_rows
     kappa = BETA * (0.5 + timesteps.astype(jnp.float32) / 1000.0)
     zvalue = kappa * (errdiff[:, 0] - errdiff[:, 1])
     losses = jax.nn.softplus(zvalue)

time: 174 us -> 175 us (level)
  blocking collectives: 85.8 us -> 75.6 us
  starting transfers between devices: 24.2 us -> 29.5 us
  waiting for transfers between devices: 13 us -> 18.2 us
    psum x1 -> x0, blocking collectives: 10.8 us -> none  [local(): errdiff = lax.psum(partial_err, 'fsdp') / sample_rows]
    ppermute x3 -> x6, starting transfers between devices: 6.62 us -> 12 us  [fsdp_sum(): lax.ppermute(value, 'fsdp', [(src, (src + shift) % fsdp_size) for src in...]
    ppermute x3 -> x6, waiting for transfers between devices: 12.9 us -> 18.2 us  [fsdp_sum(): lax.ppermute(value, 'fsdp', [(src, (src + shift) % fsdp_size) for src in...]
  transfers between devices with their start and end apart: 7 -> 10, of which waited for: 3 -> 5; matrix products, arithmetic and copies ran while one was open for 13% -> 13% of each run, Pallas kernels for 0% -> 0%
where the time goes in v13:
time: 175 us
  blocking collectives  75.6 us (43%)
  starting transfers between devices  29.5 us (17%)
  local copies, waits for them, and re-layouts  28.2 us (16%)
  waiting for transfers between devices  18.2 us (10%)
  matrix products  11.6 us (7%)
  between operations  5.77 us (3%)
  other arithmetic  5.75 us (3%)
    all_gather x1, blocking collectives, local(): lax.all_gather(jnp.concatenate([v_block, hidden_cols], axis=2), 'fsdp', a...  30.4 us
    all_to_all x1, blocking collectives, local(): lax.all_to_all(grads.transpose(1, 0, 2, 3), 'dp', 0, 0, tiled=True)  26.6 us
    unnamed x1, blocking collectives  18.6 us
    ppermute x6, waiting for transfers between devices, fsdp_sum(): lax.ppermute(value, 'fsdp', [(src, (src + shift) % fsdp_size) for src in...  18.2 us
    unnamed x27, local copies, waits for them, and re-layouts  12.3 us
    ppermute x6, starting transfers between devices, fsdp_sum(): lax.ppermute(value, 'fsdp', [(src, (src + shift) % fsdp_size) for src in...  12 us
    ppermute x3, starting transfers between devices, local(): lax.ppermute(lax.dynamic_index_in_dim(latents_split, (own + shift) % fsdp...  10.6 us
    all_to_all x1, starting transfers between devices, local(): recv = lax.all_to_all(send, 'dp', 0, 0, tiled=True)  6.95 us
  transfers between devices with their start and end apart: 10, of which 5 were waited for; matrix products, arithmetic and copies ran while one was open for 13% of the time, Pallas kernels for 0%

profile of v13, /device:TPU:32, one launch (start us, length us, event | category | flops | bytes accessed | tf_op | source)
XLA Modules:
  0.0 174.6 jit_solution(4686243215251555997)
XLA Ops:
  1.3 1.3 dynamic-slice
  2.5 0.8 dynamic-update-slice
  3.3 18.6 %all-reduce.4 = s32[64]{0:T(128)S(1)} all-reduce(s32[64]{0:T(128)S(1)} %dynamic-update-slice), channel_id=1, replica_groups=mesh['dp'=64,'fsdp'=4] {'dp'}, use_global_device_ids=true, to_apply=%add.4 | all-reduce | flops 64 | bytes 512
  22.0 1.0 copy.155
  23.0 1.0 copy.156
  24.0 0.4 pad_maximum_fusion.1
  24.3 3.1 %gather_fusion = bf16[64,2,64,38]{2,1,3,0:T(2,128)(2,1)S(1)} fusion(bf16[7,2,64,38]{2,1,3,0:T(2,128)(2,1)S(1)} %pad_maximum_fusion.1, s32[1024]{0:T(1024)S(1)} %pad_clamp_fusion.1), kind=kCustom, calls=%fused_computation | custom fusion | bytes 1245440 | tf_op jit(solution)/shard_map/jit(_take)/gather | solution.py:59
  27.4 1.2 fusion.68
  28.6 1.6 reshape.348
  30.2 7.0 %all-to-all-start = ((bf16[64,2,2432]{2,1,0:T(2,128)(2,1)}), bf16[64,2,2432]{2,1,0:T(2,128)(2,1)}, u32[]{:S(2)}, u32[]{:S(2)}) async-start(bf16[64,2,2432]{2,1,0:T(2,128)(2,1)} %reshape.348), calls=%async_computation | async-start | bytes 1245184 | tf_op jit(solution)/shard_map/all_to_all | solution.py:60
  37.2 0.7 reshape.306
  38.0 1.4 constant_dynamic-slice_fusion.3
  39.4 3.3 %collective-permute-start.3 = (bf16[1,2,64,608]{3,2,1,0:T(8,128)(2,1)S(1)}, bf16[1,2,64,608]{3,2,1,0:T(8,128)(2,1)}, u32[]{:S(2)}, u32[]{:S(2)}) collective-permute-start(bf16[1,2,64,608]{3,2,1,0:T(8,128)(2,1)S(1)} %bitcast.171), channel_id=1, source_target_pairs={{0,1},{1,2},{2,3},{3,0},{4,5},{5,6},{6,7},{7,4},{8,9},{9,10},{10,1... | collective-permute-start | bytes 466952 | tf_op jit(solution)/shard_map/ppermute | solution.py:38
  42.7 4.6 %collective-permute-start.4 = (bf16[1,2,64,608]{3,2,1,0:T(8,128)(2,1)S(1)}, bf16[1,2,64,608]{3,2,1,0:T(8,128)(2,1)}, u32[]{:S(2)}, u32[]{:S(2)}) collective-permute-start(bf16[1,2,64,608]{3,2,1,0:T(8,128)(2,1)S(1)} %bitcast.172), channel_id=1, source_target_pairs={{0,2},{1,3},{2,0},{3,1},{4,6},{5,7},{6,4},{7,5},{8,10},{9,11},{10,... | collective-permute-start | bytes 466952 | tf_op jit(solution)/shard_map/ppermute | solution.py:38
  47.3 0.7 copy.220
  48.0 2.7 %collective-permute-start.5 = (bf16[1,2,64,608]{3,2,1,0:T(8,128)(2,1)}, bf16[1,2,64,608]{3,2,1,0:T(8,128)(2,1)}, u32[]{:S(2)}, u32[]{:S(2)}) collective-permute-start(bf16[1,2,64,608]{3,2,1,0:T(8,128)(2,1)} %bitcast.155), channel_id=1, source_target_pairs={{0,3},{1,0},{2,1},{3,2},{4,7},{5,4},{6,5},{7,6},{8,11},{9,8},{10,9... | collective-permute-start | bytes 466952 | tf_op jit(solution)/shard_map/ppermute | solution.py:38
  51.3 0.7 copy.223
  52.2 0.6 fusion.53
  52.8 3.4 %reshape.349 = bf16[64,1,38,2,64]{4,3,2,1,0:T(2,128)(2,1)S(1)} reshape(bf16[64,2,2432]{2,1,0:T(2,128)(2,1)} %all-to-all-done) | data formatting | bytes 1245184
  56.1 2.7 %fusion.65 = (bf16[1,1,64,2432]{2,1,3,0:T(2,128)(2,1)}, bf16[1,1,64,2432]{2,1,3,0:T(2,128)(2,1)S(1)}) fusion(bf16[1,2,64,2432]{2,1,3,0:T(2,128)(2,1)S(1)} %bitcast.160), kind=kLoop, calls=%fused_computation.129 | loop fusion | bytes 1245184 | tf_op jit(solution)/shard_map/slice | solution.py:64
  58.8 2.5 %copy.198 = bf16[1,1,64,2432]{3,2,1,0:T(8,128)(2,1)S(1)} copy(bf16[1,1,64,2432]{2,1,3,0:T(2,128)(2,1)} %get-tuple-element.3) | data formatting | bytes 622592
  61.3 0.4 fusion.16
  62.0 1.2 copy.197
  63.4 2.8 %convolution_bitcast_fusion.1 = f32[1,64,608]{2,1,0:T(8,128)S(1)} fusion(bf16[608,2432]{1,0:T(8,128)(2,1)} %param.10, bf16[1,1,64,2432]{3,2,1,0:T(8,128)(2,1)S(1)} %copy.197), kind=kOutput, calls=%fused_computation.19 | convolution fusion | flops 189267968 | bytes 3424256 | tf_op jit(solution)/shard_map/prd,ed->pre/dot_general | solution.py:72
  66.2 0.8 copy.162
  67.1 30.4 %all_gather.7 = f32[1,64,2944]{1,0,2:T(1,128)S(1)} all-gather(f32[1,64,736]{1,0,2:T(1,128)S(1)} %copy.162), channel_id=1, replica_groups=mesh['dp'=64,'fsdp'=4] {'fsdp'}, dimensions={2}, use_global_device_ids=true | all-gather | bytes 942080 | tf_op jit(solution)/shard_map/all_gather | solution.py:76
  97.6 1.2 fusion.24
  99.0 0.5 fusion.50
  99.6 2.3 %collective-permute-start = (f32[1,2]{1,0:T(1,128)S(1)}, f32[1,2]{1,0:T(1,128)S(1)}, u32[]{:S(2)}, u32[]{:S(2)}) collective-permute-start(f32[1,2]{1,0:T(1,128)S(1)} %bitcast.177), channel_id=1, source_target_pairs={{0,3},{1,0},{2,1},{3,2},{4,7},{5,4},{6,5},{7,6},{8,11},{9,8},{10,9... | collective-permute-start | bytes 32 | tf_op jit(solution)/shard_map/ppermute | solution.py:13
  101.9 2.8 %collective-permute-start.1 = (f32[1,2]{1,0:T(1,128)S(1)}, f32[1,2]{1,0:T(1,128)S(1)}, u32[]{:S(2)}, u32[]{:S(2)}) collective-permute-start(f32[1,2]{1,0:T(1,128)S(1)} %bitcast.178), channel_id=1, source_target_pairs={{0,2},{1,3},{2,0},{3,1},{4,6},{5,7},{6,4},{7,5},{8,10},{9,11},{10,... | collective-permute-start | bytes 32 | tf_op jit(solution)/shard_map/ppermute | solution.py:13
  104.9 0.6 gather_fusion.1
  105.5 1.4 collective-permute-start.2
  107.0 2.4 %collective-permute-done.1 = f32[1,2]{1,0:T(1,128)S(1)} collective-permute-done((f32[1,2]{1,0:T(1,128)S(1)}, f32[1,2]{1,0:T(1,128)S(1)}, u32[]{:S(2)}, u32[]{:S(2)}) %collective-permute-start.1) | collective-permute-done | bytes 40 | tf_op jit(solution)/shard_map/ppermute | solution.py:13
  109.4 2.0 %collective-permute-done.2 = f32[1,2]{1,0:T(1,128)S(1)} collective-permute-done((f32[1,2]{1,0:T(1,128)S(1)}, f32[1,2]{1,0:T(1,128)S(1)}, u32[]{:S(2)}, u32[]{:S(2)}) %collective-permute-start.2) | collective-permute-done | bytes 40 | tf_op jit(solution)/shard_map/ppermute | solution.py:13
  111.9 0.6 fusion.67
  115.3 1.4 fusion.13
  116.7 4.0 %fusion.7 = f32[1,128,2432]{2,1,0:T(8,128)S(1)} fusion(bf16[1,64,2432]{2,1,0:T(8,128)(2,1)S(1)} %bitcast.168, bf16[1,608,2432]{2,1,0:T(8,128)(2,1)} %bitcast.167, bf16[1,128,2432]{2,1,0:T(8,128)(2,1)S(1)} %bitcast.169, bf16[1,128,2432]{2,1,0:T(8,128)(2,1)S(1)} %bitcast.161, f32[1,64,64]{1,2,0:T(8,128)S(1)} %copy.205, f32[1,608,64]{1,2,0:T(8,128)S(1)} %bitcast.184, ...), kind=kOutput, calls=%fused_computation.10 | convolution fusion | flops 3486429184 | bytes 5996544 | tf_op jit(solution)/shard_map/pjc,pjd->pcd/dot_general | solution.py:142
  120.7 0.4 copy.186
  121.2 1.3 copy.187
  122.5 26.6 %all_to_all.10 = f32[64,1,38,128]{3,1,2,0:T(1,128)S(1)} all-to-all(f32[64,1,38,128]{3,1,2,0:T(1,128)S(1)} %copy.187), channel_id=1, replica_groups=mesh['dp'=64,'fsdp'=4] {'dp'}, dimensions={0} | all-to-all | bytes 2490368 | tf_op jit(solution)/shard_map/all_to_all | solution.py:145
  149.2 3.0 %reduce.8 = f32[64,38,128]{2,1,0:T(8,128)S(1)} reduce(f32[64,1,38,128]{3,1,2,0:T(1,128)S(1)} %all_to_all.10, f32[]{:T(128)} %constant.140), dimensions={1}, to_apply=%all_to_all.7.reduce_sub_computation | reduce | bytes 2490372 | tf_op jit(solution)/shard_map/all_to_all | solution.py:145
  152.1 0.6 fusion.8
  153.1 3.2 %collective-permute-start.7 = (f32[7,4864]{1,0:T(8,128)S(1)}, f32[7,4864]{1,0:T(8,128)S(1)}, u32[]{:S(2)}, u32[]{:S(2)}) collective-permute-start(f32[7,4864]{1,0:T(8,128)S(1)} %fusion.8), channel_id=1, source_target_pairs={{0,2},{1,3},{2,0},{3,1},{4,6},{5,7},{6,4},{7,5},{8,10},{9,11},{10,... | collective-permute-start | bytes 408584 | tf_op jit(solution)/shard_map/ppermute | solution.py:13
  156.3 2.0 %collective-permute-start.8 = (f32[7,4864]{1,0:T(8,128)S(1)}, f32[7,4864]{1,0:T(8,128)S(1)}, u32[]{:S(2)}, u32[]{:S(2)}) collective-permute-start(f32[7,4864]{1,0:T(8,128)S(1)} %fusion.8), channel_id=1, source_target_pairs={{0,1},{1,2},{2,3},{3,0},{4,5},{5,6},{6,7},{7,4},{8,9},{9,10},{10,1... | collective-permute-start | bytes 408584 | tf_op jit(solution)/shard_map/ppermute | solution.py:13
  158.3 5.6 %collective-permute-done.6 = f32[7,4864]{1,0:T(8,128)S(1)} collective-permute-done((f32[7,4864]{1,0:T(8,128)S(1)}, f32[7,4864]{1,0:T(8,128)S(1)}, u32[]{:S(2)}, u32[]{:S(2)}) %collective-permute-start.6) | collective-permute-done | bytes 136224 | tf_op jit(solution)/shard_map/ppermute | solution.py:13
  163.9 3.3 %collective-permute-done.7 = f32[7,4864]{1,0:T(8,128)S(1)} collective-permute-done((f32[7,4864]{1,0:T(8,128)S(1)}, f32[7,4864]{1,0:T(8,128)S(1)}, u32[]{:S(2)}, u32[]{:S(2)}) %collective-permute-start.7) | collective-permute-done | bytes 136224 | tf_op jit(solution)/shard_map/ppermute | solution.py:13
  167.3 4.9 %collective-permute-done.8 = f32[7,4864]{1,0:T(8,128)S(1)} collective-permute-done((f32[7,4864]{1,0:T(8,128)S(1)}, f32[7,4864]{1,0:T(8,128)S(1)}, u32[]{:S(2)}, u32[]{:S(2)}) %collective-permute-start.8) | collective-permute-done | bytes 136224 | tf_op jit(solution)/shard_map/ppermute | solution.py:13
  172.7 0.7 copy_bitcast_fusion.4
  (61 shorter events, 3.5 us)
Async XLA Ops:
  28.6 8.6 %copy-start = (bf16[1,2,64,2432]{3,2,1,0:T(8,128)(2,1)S(1)}, bf16[1,2,64,2432]{3,2,1,0:T(8,128)(2,1)}, u32[]{:S(2)}) copy-start(bf16[1,2,64,2432]{3,2,1,0:T(8,128)(2,1)} %param.8) | copy-start | bytes 1867780
  30.2 22.6 %all-to-all-start = ((bf16[64,2,2432]{2,1,0:T(2,128)(2,1)}), bf16[64,2,2432]{2,1,0:T(2,128)(2,1)}, u32[]{:S(2)}, u32[]{:S(2)}) async-start(bf16[64,2,2432]{2,1,0:T(2,128)(2,1)} %reshape.348), calls=%async_computation | async-start | bytes 1245184 | tf_op jit(solution)/shard_map/all_to_all | solution.py:60
  39.4 75.9 %collective-permute-start.3 = (bf16[1,2,64,608]{3,2,1,0:T(8,128)(2,1)S(1)}, bf16[1,2,64,608]{3,2,1,0:T(8,128)(2,1)}, u32[]{:S(2)}, u32[]{:S(2)}) collective-permute-start(bf16[1,2,64,608]{3,2,1,0:T(8,128)(2,1)S(1)} %bitcast.171), channel_id=1, source_target_pairs={{0,1},{1,2},{2,3},{3,0},{4,5},{5,6},{6,7},{7,4},{8,9},{9,10},{10,1... | collective-permute-start | bytes 466952 | tf_op jit(solution)/shard_map/ppermute | solution.py:38
  42.7 72.5 %collective-permute-start.4 = (bf16[1,2,64,608]{3,2,1,0:T(8,128)(2,1)S(1)}, bf16[1,2,64,608]{3,2,1,0:T(8,128)(2,1)}, u32[]{:S(2)}, u32[]{:S(2)}) collective-permute-start(bf16[1,2,64,608]{3,2,1,0:T(8,128)(2,1)S(1)} %bitcast.172), channel_id=1, source_target_pairs={{0,2},{1,3},{2,0},{3,1},{4,6},{5,7},{6,4},{7,5},{8,10},{9,11},{10,... | collective-permute-start | bytes 466952 | tf_op jit(solution)/shard_map/ppermute | solution.py:38
  48.0 67.2 %collective-permute-start.5 = (bf16[1,2,64,608]{3,2,1,0:T(8,128)(2,1)}, bf16[1,2,64,608]{3,2,1,0:T(8,128)(2,1)}, u32[]{:S(2)}, u32[]{:S(2)}) collective-permute-start(bf16[1,2,64,608]{3,2,1,0:T(8,128)(2,1)} %bitcast.155), channel_id=1, source_target_pairs={{0,3},{1,0},{2,1},{3,2},{4,7},{5,4},{6,5},{7,6},{8,11},{9,8},{10,9... | collective-permute-start | bytes 466952 | tf_op jit(solution)/shard_map/ppermute | solution.py:38
  97.6 1.5 copy-start.1
  98.8 15.8 %copy-start.3 = (f32[2]{0:T(128)S(1)}, f32[2]{0:T(128)}, u32[]{:S(2)}) copy-start(f32[2]{0:T(128)} %constant.119.clone) | copy-start | bytes 28
  99.0 16.2 %copy-start.2 = (bf16[1,2,64,1,608]{4,2,1,3,0:T(8,128)(2,1)S(1)}, bf16[1,2,64,1,608]{4,2,1,3,0:T(8,128)(2,1)}, u32[]{:S(2)}) copy-start(bf16[1,2,64,1,608]{4,2,1,3,0:T(8,128)(2,1)} %copy.223) | copy-start | bytes 466948
  99.6 5.9 %collective-permute-start = (f32[1,2]{1,0:T(1,128)S(1)}, f32[1,2]{1,0:T(1,128)S(1)}, u32[]{:S(2)}, u32[]{:S(2)}) collective-permute-start(f32[1,2]{1,0:T(1,128)S(1)} %bitcast.177), channel_id=1, source_target_pairs={{0,3},{1,0},{2,1},{3,2},{4,7},{5,4},{6,5},{7,6},{8,11},{9,8},{10,9... | collective-permute-start | bytes 32 | tf_op jit(solution)/shard_map/ppermute | solution.py:13
  101.9 7.5 %collective-permute-start.1 = (f32[1,2]{1,0:T(1,128)S(1)}, f32[1,2]{1,0:T(1,128)S(1)}, u32[]{:S(2)}, u32[]{:S(2)}) collective-permute-start(f32[1,2]{1,0:T(1,128)S(1)} %bitcast.178), channel_id=1, source_target_pairs={{0,2},{1,3},{2,0},{3,1},{4,6},{5,7},{6,4},{7,5},{8,10},{9,11},{10,... | collective-permute-start | bytes 32 | tf_op jit(solution)/shard_map/ppermute | solution.py:13
  105.5 6.0 %collective-permute-start.2 = (f32[1,2]{1,0:T(1,128)S(1)}, f32[1,2]{1,0:T(1,128)S(1)}, u32[]{:S(2)}, u32[]{:S(2)}) collective-permute-start(f32[1,2]{1,0:T(1,128)S(1)} %bitcast.180), channel_id=1, source_target_pairs={{0,1},{1,2},{2,3},{3,0},{4,5},{5,6},{6,7},{7,4},{8,9},{9,10},{10,1... | collective-permute-start | bytes 32 | tf_op jit(solution)/shard_map/ppermute | solution.py:13
  152.7 11.2 %collective-permute-start.6 = (f32[7,4864]{1,0:T(8,128)S(1)}, f32[7,4864]{1,0:T(8,128)S(1)}, u32[]{:S(2)}, u32[]{:S(2)}) collective-permute-start(f32[7,4864]{1,0:T(8,128)S(1)} %fusion.8), channel_id=1, source_target_pairs={{0,3},{1,0},{2,1},{3,2},{4,7},{5,4},{6,5},{7,6},{8,11},{9,8},{10,9... | collective-permute-start | bytes 408584 | tf_op jit(solution)/shard_map/ppermute | solution.py:13
  153.1 14.1 %collective-permute-start.7 = (f32[7,4864]{1,0:T(8,128)S(1)}, f32[7,4864]{1,0:T(8,128)S(1)}, u32[]{:S(2)}, u32[]{:S(2)}) collective-permute-start(f32[7,4864]{1,0:T(8,128)S(1)} %fusion.8), channel_id=1, source_target_pairs={{0,2},{1,3},{2,0},{3,1},{4,6},{5,7},{6,4},{7,5},{8,10},{9,11},{10,... | collective-permute-start | bytes 408584 | tf_op jit(solution)/shard_map/ppermute | solution.py:13
  156.3 15.8 %collective-permute-start.8 = (f32[7,4864]{1,0:T(8,128)S(1)}, f32[7,4864]{1,0:T(8,128)S(1)}, u32[]{:S(2)}, u32[]{:S(2)}) collective-permute-start(f32[7,4864]{1,0:T(8,128)S(1)} %fusion.8), channel_id=1, source_target_pairs={{0,1},{1,2},{2,3},{3,0},{4,5},{5,6},{6,7},{7,4},{8,9},{9,10},{10,1... | collective-permute-start | bytes 408584 | tf_op jit(solution)/shard_map/ppermute | solution.py:13

commit v14 on v12

--- a/solution.py
+++ b/solution.py
@@ -139,7 +139,12 @@
         ],
         axis=1,
     )
-    grads = lax.optimization_barrier(jnp.einsum("pjc,pjd->pcd", rhs, lhs, precision=highest))
+    rhs_high = rhs.astype(jnp.bfloat16)
+    rhs_low = (rhs - rhs_high.astype(jnp.float32)).astype(jnp.bfloat16)
+    grads = lax.optimization_barrier(
+        jnp.einsum("pjc,pjd->pcd", rhs_high, lhs, preferred_element_type=jnp.float32)
+        + jnp.einsum("pjc,pjd->pcd", rhs_low, lhs, preferred_element_type=jnp.float32)
+    )
     grads = grads.reshape(pair_local, 2 * adapter_rank_width, dp_size, col_local).transpose(0, 2, 3, 1)
 
     gathered = lax.all_to_all(grads.transpose(1, 0, 2, 3), "dp", 0, 0, tiled=True).reshape(

time: 174 us -> 175 us (level)
    unnamed x27 -> x28, local copies, waits for them, and re-layouts: 12.3 us -> 14.2 us
    dot_general x1 -> x2, matrix products: 4.05 us -> 3.73 us  [the longest x1 2.85 us: local(): jnp.einsum('pjc,pjd->pcd', rhs_high, lhs, preferred_element_type=jnp.floa...]
where the time goes in v14:
time: 175 us
  blocking collectives  86 us (49%)
  local copies, waits for them, and re-layouts  29.1 us (17%)
  starting transfers between devices  23.5 us (13%)
  waiting for transfers between devices  13.6 us (8%)
  matrix products  11.3 us (6%)
  between operations  5.8 us (3%)
  other arithmetic  5.57 us (3%)
    all_gather x1, blocking collectives, local(): lax.all_gather(jnp.concatenate([v_block, hidden_cols], axis=2), 'fsdp', a...  29.9 us
    all_to_all x1, blocking collectives, local(): lax.all_to_all(grads.transpose(1, 0, 2, 3), 'dp', 0, 0, tiled=True)  26.6 us
    unnamed x1, blocking collectives  18.6 us
    unnamed x28, local copies, waits for them, and re-layouts  14.2 us
    ppermute x3, waiting for transfers between devices, fsdp_sum(): lax.ppermute(value, 'fsdp', [(src, (src + shift) % fsdp_size) for src in...  13.6 us
    psum x1, blocking collectives, local(): errdiff = lax.psum(partial_err, 'fsdp') / sample_rows  10.9 us
    ppermute x3, starting transfers between devices, local(): lax.ppermute(lax.dynamic_index_in_dim(latents_split, (own + shift) % fsdp...  10.5 us
    all_to_all x1, starting transfers between devices, local(): recv = lax.all_to_all(send, 'dp', 0, 0, tiled=True)  6.95 us
  transfers between devices with their start and end apart: 7, of which 3 were waited for; matrix products, arithmetic and copies ran while one was open for 13% of the time, Pallas kernels for 0%

profile of v14, /device:TPU:32, one launch (start us, length us, event | category | flops | bytes accessed | tf_op | source)
XLA Modules:
  0.0 174.8 jit_solution(4467836367241656553)
XLA Ops:
  1.3 1.3 dynamic-slice
  2.5 0.8 dynamic-update-slice
  3.3 18.6 %all-reduce.4 = s32[64]{0:T(128)S(1)} all-reduce(s32[64]{0:T(128)S(1)} %dynamic-update-slice), channel_id=1, replica_groups=mesh['dp'=64,'fsdp'=4] {'dp'}, use_global_device_ids=true, to_apply=%add.4 | all-reduce | flops 64 | bytes 512
  22.0 1.0 copy.131
  23.0 1.0 copy.132
  24.0 0.4 pad_maximum_fusion.2
  24.3 3.1 %gather_fusion = bf16[64,2,64,38]{2,1,3,0:T(2,128)(2,1)S(1)} fusion(bf16[7,2,64,38]{2,1,3,0:T(2,128)(2,1)S(1)} %pad_maximum_fusion.2, s32[1024]{0:T(1024)S(1)} %pad_clamp_fusion.1), kind=kCustom, calls=%fused_computation | custom fusion | bytes 1245440 | tf_op jit(solution)/shard_map/jit(_take)/gather | solution.py:59
  27.4 1.2 fusion.48
  28.6 1.6 reshape.354
  30.2 7.0 %all-to-all-start = ((bf16[64,2,2432]{2,1,0:T(2,128)(2,1)}), bf16[64,2,2432]{2,1,0:T(2,128)(2,1)}, u32[]{:S(2)}, u32[]{:S(2)}) async-start(bf16[64,2,2432]{2,1,0:T(2,128)(2,1)} %reshape.354), calls=%async_computation | async-start | bytes 1245184 | tf_op jit(solution)/shard_map/all_to_all | solution.py:60
  37.2 0.7 reshape.314
  38.0 1.4 constant_dynamic-slice_fusion.3
  39.4 3.3 %collective-permute-start = (bf16[1,2,64,608]{3,2,1,0:T(8,128)(2,1)S(1)}, bf16[1,2,64,608]{3,2,1,0:T(8,128)(2,1)}, u32[]{:S(2)}, u32[]{:S(2)}) collective-permute-start(bf16[1,2,64,608]{3,2,1,0:T(8,128)(2,1)S(1)} %bitcast.176), channel_id=1, source_target_pairs={{0,1},{1,2},{2,3},{3,0},{4,5},{5,6},{6,7},{7,4},{8,9},{9,10},{10,1... | collective-permute-start | bytes 466952 | tf_op jit(solution)/shard_map/ppermute | solution.py:38
  42.7 0.7 copy.188
  43.4 4.5 %collective-permute-start.1 = (bf16[1,2,64,608]{3,2,1,0:T(8,128)(2,1)}, bf16[1,2,64,608]{3,2,1,0:T(8,128)(2,1)}, u32[]{:S(2)}, u32[]{:S(2)}) collective-permute-start(bf16[1,2,64,608]{3,2,1,0:T(8,128)(2,1)} %bitcast.155), channel_id=1, source_target_pairs={{0,2},{1,3},{2,0},{3,1},{4,6},{5,7},{6,4},{7,5},{8,10},{9,11},{10,... | collective-permute-start | bytes 466952 | tf_op jit(solution)/shard_map/ppermute | solution.py:38
  47.9 0.7 copy.187
  48.6 2.7 %collective-permute-start.2 = (bf16[1,2,64,608]{3,2,1,0:T(8,128)(2,1)}, bf16[1,2,64,608]{3,2,1,0:T(8,128)(2,1)}, u32[]{:S(2)}, u32[]{:S(2)}) collective-permute-start(bf16[1,2,64,608]{3,2,1,0:T(8,128)(2,1)} %bitcast.154), channel_id=1, source_target_pairs={{0,3},{1,0},{2,1},{3,2},{4,7},{5,4},{6,5},{7,6},{8,11},{9,8},{10,9... | collective-permute-start | bytes 466952 | tf_op jit(solution)/shard_map/ppermute | solution.py:38
  51.9 0.7 copy.190
  52.8 0.6 fusion.35
  53.4 3.4 %reshape.355 = bf16[64,1,38,2,64]{4,3,2,1,0:T(2,128)(2,1)S(1)} reshape(bf16[64,2,2432]{2,1,0:T(2,128)(2,1)} %all-to-all-done) | data formatting | bytes 1245184
  56.8 2.7 %fusion.45 = (bf16[1,1,64,2432]{2,1,3,0:T(2,128)(2,1)}, bf16[1,1,64,2432]{2,1,3,0:T(2,128)(2,1)S(1)}) fusion(bf16[1,2,64,2432]{2,1,3,0:T(2,128)(2,1)S(1)} %bitcast.161), kind=kLoop, calls=%fused_computation.107 | loop fusion | bytes 1245184 | tf_op jit(solution)/shard_map/slice | solution.py:64
  59.4 2.5 %copy.166 = bf16[1,1,64,2432]{3,2,1,0:T(8,128)(2,1)S(1)} copy(bf16[1,1,64,2432]{2,1,3,0:T(2,128)(2,1)} %get-tuple-element.3) | data formatting | bytes 622592
  61.9 0.4 fusion.9
  62.6 1.2 copy.165
  64.0 2.8 %convolution_bitcast_fusion.1 = f32[1,64,608]{2,1,0:T(8,128)S(1)} fusion(bf16[608,2432]{1,0:T(8,128)(2,1)} %param.10, bf16[1,1,64,2432]{3,2,1,0:T(8,128)(2,1)S(1)} %copy.165), kind=kOutput, calls=%fused_computation.13 | convolution fusion | flops 189267968 | bytes 3424256 | tf_op jit(solution)/shard_map/prd,ed->pre/dot_general | solution.py:72
  66.9 0.8 copy.138
  67.7 29.9 %all_gather.7 = f32[1,64,2944]{1,0,2:T(1,128)S(1)} all-gather(f32[1,64,736]{1,0,2:T(1,128)S(1)} %copy.138), channel_id=1, replica_groups=mesh['dp'=64,'fsdp'=4] {'fsdp'}, dimensions={2}, use_global_device_ids=true | all-gather | bytes 942080 | tf_op jit(solution)/shard_map/all_gather | solution.py:76
  97.7 1.2 fusion.18
  99.1 0.5 fusion.32
  99.6 10.9 %psum.7 = f32[1,2]{1,0:T(1,128)S(1)} all-reduce(f32[1,2]{1,0:T(1,128)S(1)} %bitcast.183), channel_id=1, replica_groups=mesh['dp'=64,'fsdp'=4] {'fsdp'}, use_global_device_ids=true, to_apply=%region_1.2 | all-reduce | flops 2 | bytes 16 | tf_op jit(solution)/shard_map/psum | solution.py:105
  110.5 0.6 fusion.47
  113.8 0.6 gather_fusion.1
  114.5 1.5 fusion.6
  116.3 2.8 %fusion.10 = f32[128,2432]{1,0:T(8,128)S(1)} fusion(bf16[1,64,2432]{2,1,0:T(8,128)(2,1)S(1)} %bitcast.171, bf16[1,608,2432]{2,1,0:T(8,128)(2,1)} %bitcast.169, bf16[1,128,2432]{2,1,0:T(8,128)(2,1)S(1)} %bitcast.173, bf16[1,128,2432]{2,1,0:T(8,128)(2,1)S(1)} %bitcast.162, f32[64,128]{0,1:T(8,128)S(1)} %copy.153, f32[608,128]{0,1:T(8,128)S(1)} %pad_bitcast_fusion, ...), kind=kOutput, calls=%fused_computation.21 | convolution fusion | flops 596770816 | bytes 6234112 | tf_op jit(solution)/shard_map/pjc,pjd->pcd/dot_general | solution.py:145
  119.2 0.9 fusion
  120.0 0.4 copy.154
  120.5 1.3 copy.155
  121.8 26.6 %all_to_all.10 = f32[64,1,38,128]{3,1,2,0:T(1,128)S(1)} all-to-all(f32[64,1,38,128]{3,1,2,0:T(1,128)S(1)} %copy.155), channel_id=1, replica_groups=mesh['dp'=64,'fsdp'=4] {'dp'}, dimensions={0} | all-to-all | bytes 2490368 | tf_op jit(solution)/shard_map/all_to_all | solution.py:150
  148.5 3.0 %reduce.7 = f32[64,38,128]{2,1,0:T(8,128)S(1)} reduce(f32[64,1,38,128]{3,1,2,0:T(1,128)S(1)} %all_to_all.10, f32[]{:T(128)} %constant.138), dimensions={1}, to_apply=%all_to_all.7.reduce_sub_computation | reduce | bytes 2490372 | tf_op jit(solution)/shard_map/all_to_all | solution.py:150
  151.4 0.6 fusion.1
  152.0 1.3 collective-permute-start.3
  153.5 3.4 %collective-permute-start.4 = (f32[7,4864]{1,0:T(8,128)S(1)}, f32[7,4864]{1,0:T(8,128)S(1)}, u32[]{:S(2)}, u32[]{:S(2)}) collective-permute-start(f32[7,4864]{1,0:T(8,128)S(1)} %fusion.1), channel_id=1, source_target_pairs={{0,2},{1,3},{2,0},{3,1},{4,6},{5,7},{6,4},{7,5},{8,10},{9,11},{10,... | collective-permute-start | bytes 408584 | tf_op jit(solution)/shard_map/ppermute | solution.py:13
  156.9 1.3 collective-permute-start.5
  158.1 4.5 %collective-permute-done.3 = f32[7,4864]{1,0:T(8,128)S(1)} collective-permute-done((f32[7,4864]{1,0:T(8,128)S(1)}, f32[7,4864]{1,0:T(8,128)S(1)}, u32[]{:S(2)}, u32[]{:S(2)}) %collective-permute-start.3) | collective-permute-done | bytes 136224 | tf_op jit(solution)/shard_map/ppermute | solution.py:13
  162.7 7.0 %collective-permute-done.4 = f32[7,4864]{1,0:T(8,128)S(1)} collective-permute-done((f32[7,4864]{1,0:T(8,128)S(1)}, f32[7,4864]{1,0:T(8,128)S(1)}, u32[]{:S(2)}, u32[]{:S(2)}) %collective-permute-start.4) | collective-permute-done | bytes 136224 | tf_op jit(solution)/shard_map/ppermute | solution.py:13
  169.7 2.0 %collective-permute-done.5 = f32[7,4864]{1,0:T(8,128)S(1)} collective-permute-done((f32[7,4864]{1,0:T(8,128)S(1)}, f32[7,4864]{1,0:T(8,128)S(1)}, u32[]{:S(2)}, u32[]{:S(2)}) %collective-permute-start.5) | collective-permute-done | bytes 136224 | tf_op jit(solution)/shard_map/ppermute | solution.py:13
  172.3 0.7 copy.191
  173.0 0.7 copy.192
  (55 shorter events, 2.5 us)
Async XLA Ops:
  28.6 8.6 %copy-start = (bf16[1,2,64,2432]{3,2,1,0:T(8,128)(2,1)S(1)}, bf16[1,2,64,2432]{3,2,1,0:T(8,128)(2,1)}, u32[]{:S(2)}) copy-start(bf16[1,2,64,2432]{3,2,1,0:T(8,128)(2,1)} %param.8) | copy-start | bytes 1867780
  30.2 23.2 %all-to-all-start = ((bf16[64,2,2432]{2,1,0:T(2,128)(2,1)}), bf16[64,2,2432]{2,1,0:T(2,128)(2,1)}, u32[]{:S(2)}, u32[]{:S(2)}) async-start(bf16[64,2,2432]{2,1,0:T(2,128)(2,1)} %reshape.354), calls=%async_computation | async-start | bytes 1245184 | tf_op jit(solution)/shard_map/all_to_all | solution.py:60
  39.4 75.1 %collective-permute-start = (bf16[1,2,64,608]{3,2,1,0:T(8,128)(2,1)S(1)}, bf16[1,2,64,608]{3,2,1,0:T(8,128)(2,1)}, u32[]{:S(2)}, u32[]{:S(2)}) collective-permute-start(bf16[1,2,64,608]{3,2,1,0:T(8,128)(2,1)S(1)} %bitcast.176), channel_id=1, source_target_pairs={{0,1},{1,2},{2,3},{3,0},{4,5},{5,6},{6,7},{7,4},{8,9},{9,10},{10,1... | collective-permute-start | bytes 466952 | tf_op jit(solution)/shard_map/ppermute | solution.py:38
  43.4 71.1 %collective-permute-start.1 = (bf16[1,2,64,608]{3,2,1,0:T(8,128)(2,1)}, bf16[1,2,64,608]{3,2,1,0:T(8,128)(2,1)}, u32[]{:S(2)}, u32[]{:S(2)}) collective-permute-start(bf16[1,2,64,608]{3,2,1,0:T(8,128)(2,1)} %bitcast.155), channel_id=1, source_target_pairs={{0,2},{1,3},{2,0},{3,1},{4,6},{5,7},{6,4},{7,5},{8,10},{9,11},{10,... | collective-permute-start | bytes 466952 | tf_op jit(solution)/shard_map/ppermute | solution.py:38
  48.6 65.9 %collective-permute-start.2 = (bf16[1,2,64,608]{3,2,1,0:T(8,128)(2,1)}, bf16[1,2,64,608]{3,2,1,0:T(8,128)(2,1)}, u32[]{:S(2)}, u32[]{:S(2)}) collective-permute-start(bf16[1,2,64,608]{3,2,1,0:T(8,128)(2,1)} %bitcast.154), channel_id=1, source_target_pairs={{0,3},{1,0},{2,1},{3,2},{4,7},{5,4},{6,5},{7,6},{8,11},{9,8},{10,9... | collective-permute-start | bytes 466952 | tf_op jit(solution)/shard_map/ppermute | solution.py:38
  97.6 1.5 copy-start.2
  97.7 15.5 %copy-start.3 = (f32[2]{0:T(128)S(1)}, f32[2]{0:T(128)}, u32[]{:S(2)}) copy-start(f32[2]{0:T(128)} %constant.117.clone) | copy-start | bytes 28
  116.3 2.9 %copy-start.1 = (bf16[608,2432]{1,0:T(8,128)(2,1)S(1)}, bf16[608,2432]{1,0:T(8,128)(2,1)}, u32[]{:S(2)}) copy-start(bf16[608,2432]{1,0:T(8,128)(2,1)} %param.10) | copy-start | bytes 8871940
  152.0 10.6 %collective-permute-start.3 = (f32[7,4864]{1,0:T(8,128)S(1)}, f32[7,4864]{1,0:T(8,128)S(1)}, u32[]{:S(2)}, u32[]{:S(2)}) collective-permute-start(f32[7,4864]{1,0:T(8,128)S(1)} %fusion.1), channel_id=1, source_target_pairs={{0,3},{1,0},{2,1},{3,2},{4,7},{5,4},{6,5},{7,6},{8,11},{9,8},{10,9... | collective-permute-start | bytes 408584 | tf_op jit(solution)/shard_map/ppermute | solution.py:13
  153.5 16.3 %collective-permute-start.4 = (f32[7,4864]{1,0:T(8,128)S(1)}, f32[7,4864]{1,0:T(8,128)S(1)}, u32[]{:S(2)}, u32[]{:S(2)}) collective-permute-start(f32[7,4864]{1,0:T(8,128)S(1)} %fusion.1), channel_id=1, source_target_pairs={{0,2},{1,3},{2,0},{3,1},{4,6},{5,7},{6,4},{7,5},{8,10},{9,11},{10,... | collective-permute-start | bytes 408584 | tf_op jit(solution)/shard_map/ppermute | solution.py:13
  156.9 14.9 %collective-permute-start.5 = (f32[7,4864]{1,0:T(8,128)S(1)}, f32[7,4864]{1,0:T(8,128)S(1)}, u32[]{:S(2)}, u32[]{:S(2)}) collective-permute-start(f32[7,4864]{1,0:T(8,128)S(1)} %fusion.1), channel_id=1, source_target_pairs={{0,1},{1,2},{2,3},{3,0},{4,5},{5,6},{6,7},{7,4},{8,9},{9,10},{10,1... | collective-permute-start | bytes 408584 | tf_op jit(solution)/shard_map/ppermute | solution.py:13

commit v15 on v12

--- a/solution.py
+++ b/solution.py
@@ -122,24 +122,27 @@
         [
             latents.reshape(pair_local, token_rows, feat_width),
             targets.reshape(pair_local, token_rows, feat_width),
-            jnp.broadcast_to(frozen_weight[None], (pair_local, in_local, feat_width)),
             selected_up,
         ],
         axis=1,
     )
     zero_tok = jnp.zeros((pair_local, token_rows, adapter_rank_width), jnp.float32)
-    zero_in = jnp.zeros((pair_local, in_local, adapter_rank_width), jnp.float32)
     zero_rank = jnp.zeros((pair_local, adapter_rank_width, adapter_rank_width), jnp.float32)
     rhs = jnp.concatenate(
         [
             jnp.concatenate([(back * scale_k).reshape(pair_local, token_rows, -1), zero_tok], axis=2),
             jnp.concatenate([zero_tok, -(hidden_f * scale_k).reshape(pair_local, token_rows, -1)], axis=2),
-            jnp.concatenate([zero_in, a_weighted.transpose(0, 2, 1)], axis=2),
             jnp.concatenate([zero_rank, gram_weighted.transpose(0, 2, 1)], axis=2),
         ],
         axis=1,
     )
-    grads = lax.optimization_barrier(jnp.einsum("pjc,pjd->pcd", rhs, lhs, precision=highest))
+    small = jnp.einsum("pjc,pjd->pcd", rhs, lhs, precision=highest)
+    w_term = jnp.einsum("pre,ed->prd", a_weighted, frozen_weight, precision=highest)
+    grads = lax.optimization_barrier(
+        jnp.concatenate(
+            [small[:, :adapter_rank_width], small[:, adapter_rank_width:] + w_term], axis=1
+        )
+    )
     grads = grads.reshape(pair_local, 2 * adapter_rank_width, dp_size, col_local).transpose(0, 2, 3, 1)
 
     gathered = lax.all_to_all(grads.transpose(1, 0, 2, 3), "dp", 0, 0, tiled=True).reshape(

time: 174 us -> 210 us (1.21)
  local copies, waits for them, and re-layouts: 27.7 us -> 54.2 us
  other arithmetic: 5.57 us -> 12.6 us
    unnamed x27 -> x37, local copies, waits for them, and re-layouts: 12.3 us -> 22.6 us
    all_to_all x1, blocking collectives: 25.9 us -> 29 us  [local(): lax.all_to_all(grads.transpose(1, 0, 2, 3), 'dp', 0, 0, tiled=True)]
    slice x1 -> x3, local copies, waits for them, and re-layouts: 2.67 us -> 5.13 us  [the longest x1 5.13 us: local(): selected_up = selected[:, 1]]
    optimization_barrier x1, local copies, waits for them, and re-layouts: 0.39 us -> 2.76 us  [local(): lax.optimization_barrier(jnp.concatenate([small[:, :adapter_rank_width],...]
    all_to_all x1, other arithmetic: 2.96 us -> 5.32 us  [local(): lax.all_to_all(grads.transpose(1, 0, 2, 3), 'dp', 0, 0, tiled=True)]
    unnamed x1, other arithmetic: 1.23 us -> 3.57 us
    reshape x1, local copies, waits for them, and re-layouts: 0.1 us -> 2.39 us  [local(): grads.reshape(pair_local, 2 * adapter_rank_width, dp_size, col_local)]
  transfers between devices with their start and end apart: 7 -> 7, of which waited for: 3 -> 3; matrix products, arithmetic and copies ran while one was open for 13% -> 19% of each run, Pallas kernels for 0% -> 0%
where the time goes in v15:
time: 210 us; the launch traced here: 209 us
  blocking collectives  87.4 us (42%)
  local copies, waits for them, and re-layouts  54.2 us (26%)
  starting transfers between devices  22.4 us (11%)
  waiting for transfers between devices  13.3 us (6%)
  matrix products  12.8 us (6%)
  other arithmetic  12.6 us (6%)
  between operations  5.82 us (3%)
    all_gather x1, blocking collectives, local(): lax.all_gather(jnp.concatenate([v_block, hidden_cols], axis=2), 'fsdp', a...  29.1 us
    all_to_all x1, blocking collectives, local(): lax.all_to_all(grads.transpose(1, 0, 2, 3), 'dp', 0, 0, tiled=True)  29 us
    unnamed x37, local copies, waits for them, and re-layouts  22.6 us
    unnamed x1, blocking collectives  18.6 us
    ppermute x3, waiting for transfers between devices, fsdp_sum(): lax.ppermute(value, 'fsdp', [(src, (src + shift) % fsdp_size) for src in...  13.3 us
    psum x1, blocking collectives, local(): errdiff = lax.psum(partial_err, 'fsdp') / sample_rows  10.7 us
    ppermute x3, starting transfers between devices, local(): lax.ppermute(lax.dynamic_index_in_dim(latents_split, (own + shift) % fsdp...  9.22 us
    all_to_all x1, starting transfers between devices, local(): recv = lax.all_to_all(send, 'dp', 0, 0, tiled=True)  6.95 us
  transfers between devices with their start and end apart: 7, of which 3 were waited for; matrix products, arithmetic and copies ran while one was open for 19% of the time, Pallas kernels for 0%

profile of v15, /device:TPU:32, one launch (start us, length us, event | category | flops | bytes accessed | tf_op | source)
XLA Modules:
  0.0 208.6 jit_solution(11439561911935645324)
XLA Ops:
  1.4 1.4 dynamic-slice
  2.8 0.8 dynamic-update-slice
  3.6 18.6 %all-reduce.3 = s32[64]{0:T(128)S(1)} all-reduce(s32[64]{0:T(128)S(1)} %dynamic-update-slice), channel_id=1, replica_groups=mesh['dp'=64,'fsdp'=4] {'dp'}, use_global_device_ids=true, to_apply=%add.3 | all-reduce | flops 64 | bytes 512
  22.2 1.0 copy.136
  23.2 1.0 copy.135
  24.6 4.0 %gather_fusion = bf16[64,2,64,38]{2,1,3,0:T(2,128)(2,1)} fusion(bf16[7,2,64,38]{2,1,3,0:T(2,128)(2,1)S(1)} %pad_maximum_fusion.2, s32[1024]{0:T(1024)S(1)} %pad_clamp_fusion.1), kind=kCustom, calls=%fused_computation | custom fusion | bytes 1245440 | tf_op jit(solution)/shard_map/jit(_take)/gather | solution.py:59
  28.6 3.6 %fusion.60 = bf16[64,1,38,2,64]{4,3,2,1,0:T(2,128)(2,1)} fusion(bf16[64,2,64,38]{2,1,3,0:T(2,128)(2,1)} %gather_fusion, pred[64]{0:T(512)(128)(4,1)S(1)} %compare_and_fusion.1), kind=kLoop, calls=%fused_computation.124 | loop fusion | flops 311296 | bytes 1245248
  32.2 4.2 %reshape.296 = bf16[64,2,2432]{2,1,0:T(2,128)(2,1)} reshape(bf16[64,1,38,2,64]{4,3,2,1,0:T(2,128)(2,1)} %fusion.60) | data formatting | bytes 1245184
  36.4 7.0 %all-to-all-start = ((bf16[64,2,2432]{2,1,0:T(2,128)(2,1)}), bf16[64,2,2432]{2,1,0:T(2,128)(2,1)}, u32[]{:S(2)}, u32[]{:S(2)}) async-start(bf16[64,2,2432]{2,1,0:T(2,128)(2,1)} %reshape.296), calls=%async_computation | async-start | bytes 1245184 | tf_op jit(solution)/shard_map/all_to_all | solution.py:60
  43.4 2.8 %reshape.259 = bf16[1,2,64,4,608]{4,3,2,1,0:T(4,128)(2,1)} reshape(bf16[1,2,64,2432]{3,2,1,0:T(8,128)(2,1)} %param.8) | data formatting | bytes 1245184 | tf_op jit(solution)/shard_map/reshape | solution.py:35
  46.2 3.3 %constant_dynamic-slice_fusion.3 = (bf16[1,2,64,1,608]{4,3,2,1,0:T(2,128)(2,1)S(1)}, bf16[1,2,64,1,608]{4,3,2,1,0:T(2,128)(2,1)S(1)}, bf16[1,2,64,1,608]{4,3,2,1,0:T(2,128)(2,1)S(1)}, bf16[1,2,64,1,608]{4,3,2,1,0:T(2,128)(2,1)S(1)}) fusion(bf16[1,2,64,4,608]{4,3,2,1,0:T(4,128)(2,1)} %reshape.259, s32[]{:T(128)S(6)} %select_n.104, s32[]{:T(128)S(6)} %select_n.110, ...), kind=kLoop, calls=%fused_computation.101 | loop fusion | bytes 1245200 | tf_op jit(solution)/shard_map/jit(dynamic_index_in_dim)/dynamic_slice | solution.py:46
  50.2 5.4 %collective-permute-start.2 = (bf16[1,2,64,608]{3,2,1,0:T(8,128)(2,1)}, bf16[1,2,64,608]{3,2,1,0:T(8,128)(2,1)}, u32[]{:S(2)}, u32[]{:S(2)}) collective-permute-start(bf16[1,2,64,608]{3,2,1,0:T(8,128)(2,1)} %bitcast.152), channel_id=1, source_target_pairs={{0,3},{1,0},{2,1},{3,2},{4,7},{5,4},{6,5},{7,6},{8,11},{9,8},{10,9... | collective-permute-start | bytes 466952 | tf_op jit(solution)/shard_map/ppermute | solution.py:38
  56.3 1.4 collective-permute-start.1
  58.4 2.4 %collective-permute-start = (bf16[1,2,64,608]{3,2,1,0:T(8,128)(2,1)}, bf16[1,2,64,608]{3,2,1,0:T(8,128)(2,1)}, u32[]{:S(2)}, u32[]{:S(2)}) collective-permute-start(bf16[1,2,64,608]{3,2,1,0:T(8,128)(2,1)} %bitcast.154), channel_id=1, source_target_pairs={{0,1},{1,2},{2,3},{3,0},{4,5},{5,6},{6,7},{7,4},{8,9},{9,10},{10,1... | collective-permute-start | bytes 466952 | tf_op jit(solution)/shard_map/ppermute | solution.py:38
  62.9 4.2 %reshape.297 = bf16[64,1,38,2,64]{4,3,2,1,0:T(2,128)(2,1)} reshape(bf16[64,2,2432]{2,1,0:T(2,128)(2,1)} %all-to-all-done) | data formatting | bytes 1245184
  67.0 5.1 %fusion.57 = (bf16[1,1,64,2432]{2,1,3,0:T(2,128)(2,1)}, bf16[1,1,64,2432]{2,1,3,0:T(2,128)(2,1)}) fusion(bf16[1,2,64,2432]{2,1,3,0:T(2,128)(2,1)} %bitcast.157), kind=kLoop, calls=%fused_computation.121 | loop fusion | bytes 1245184 | tf_op jit(solution)/shard_map/slice | solution.py:65
  72.2 2.5 %copy.171 = bf16[1,1,64,2432]{3,2,1,0:T(8,128)(2,1)S(1)} copy(bf16[1,1,64,2432]{2,1,3,0:T(2,128)(2,1)} %get-tuple-element.4) | data formatting | bytes 622592
  74.7 1.5 fusion.13
  76.2 2.5 %copy.170 = bf16[1,1,64,2432]{3,2,1,0:T(8,128)(2,1)S(1)} copy(bf16[1,1,64,2432]{2,1,3,0:T(2,128)(2,1)} %get-tuple-element.3) | data formatting | bytes 622592
  79.0 0.9 fusion.61
  80.0 1.0 convolution_bitcast_fusion.3
  81.1 1.0 copy.142
  82.1 29.1 %all_gather.7 = f32[1,64,2944]{1,0,2:T(1,128)S(1)} all-gather(f32[1,64,736]{1,0,2:T(1,128)} %copy.142), channel_id=1, replica_groups=mesh['dp'=64,'fsdp'=4] {'fsdp'}, dimensions={2}, use_global_device_ids=true | all-gather | bytes 942080 | tf_op jit(solution)/shard_map/all_gather | solution.py:76
  111.3 1.0 copy-done.2
  112.7 1.2 fusion.21
  114.5 10.7 %psum.7 = f32[1,2]{1,0:T(1,128)S(1)} all-reduce(f32[1,2]{1,0:T(1,128)S(1)} %bitcast.170), channel_id=1, replica_groups=mesh['dp'=64,'fsdp'=4] {'fsdp'}, use_global_device_ids=true, to_apply=%region_1.2 | all-reduce | flops 2 | bytes 16 | tf_op jit(solution)/shard_map/psum | solution.py:105
  128.0 0.7 add_multiply_fusion
  129.3 1.0 slice.65
  130.4 1.5 copy.174
  131.9 0.9 copy.148
  132.9 0.9 copy.147
  133.9 2.5 %convolution_bitcast_fusion = f32[1,128,2432]{2,1,0:T(8,128)S(1)} fusion(bf16[1,64,2432]{2,1,0:T(8,128)(2,1)S(1)} %bitcast.164, bf16[1,128,2432]{2,1,0:T(8,128)(2,1)} %bitcast.165, bf16[1,128,2432]{2,1,0:T(8,128)(2,1)} %bitcast.158, f32[1,64,64]{1,2,0:T(8,128)} %copy.174, f32[1,128,64]{1,2,0:T(8,128)S(1)} %neg.23, f32[1,128,64]{1,2,0:T(8,128)S(1)} %reshape.253), kind=kOutput, calls=%fused_computation.2 | convolution fusion | flops 1200455680 | bytes 2883584 | tf_op jit(solution)/shard_map/pjc,pjd->pcd/dot_general | solution.py:139
  136.4 1.0 copy-done.3
  138.3 1.5 fusion.10
  139.9 1.5 fusion
  141.4 1.1 pad_maximum_fusion
  142.5 2.8 %copy.155 = f32[1,128,2432]{1,2,0:T(8,128)} copy(f32[1,128,2432]{2,1,0:T(8,128)} %pad_maximum_fusion) | data formatting | bytes 2490368 | tf_op jit(solution)/shard_map/optimization_barrier | solution.py:141
  145.3 2.4 %reshape.261 = f32[1,128,64,38]{1,3,2,0:T(8,128)} reshape(f32[1,128,2432]{1,2,0:T(8,128)} %copy.155) | data formatting | bytes 2490368 | tf_op jit(solution)/shard_map/reshape | solution.py:146
  147.7 2.6 %copy.156 = f32[64,1,38,128]{3,1,2,0:T(1,128)S(1)} copy(f32[64,1,38,128]{3,2,0,1:T(8,128)} %bitcast.161) | data formatting | bytes 2490368 | tf_op jit(solution)/shard_map/transpose;transpose | solution.py:148
  150.3 29.0 %all_to_all.10 = f32[64,1,38,128]{3,1,2,0:T(1,128)} all-to-all(f32[64,1,38,128]{3,1,2,0:T(1,128)S(1)} %copy.156), channel_id=1, replica_groups=mesh['dp'=64,'fsdp'=4] {'dp'}, dimensions={0} | all-to-all | bytes 2490368 | tf_op jit(solution)/shard_map/all_to_all | solution.py:148
  179.3 5.3 %reduce.7 = f32[64,38,128]{2,1,0:T(8,128)} reduce(f32[64,1,38,128]{3,1,2,0:T(1,128)} %all_to_all.10, f32[]{:T(128)} %constant.135), dimensions={1}, to_apply=%all_to_all.7.reduce_sub_computation | reduce | bytes 2490372 | tf_op jit(solution)/shard_map/all_to_all | solution.py:148
  184.6 1.9 fusion.5
  186.5 2.2 %collective-permute-start.3 = (f32[7,4864]{1,0:T(8,128)S(1)}, f32[7,4864]{1,0:T(8,128)S(1)}, u32[]{:S(2)}, u32[]{:S(2)}) collective-permute-start(f32[7,4864]{1,0:T(8,128)S(1)} %fusion.5), channel_id=1, source_target_pairs={{0,3},{1,0},{2,1},{3,2},{4,7},{5,4},{6,5},{7,6},{8,11},{9,8},{10,9... | collective-permute-start | bytes 408584 | tf_op jit(solution)/shard_map/ppermute | solution.py:13
  188.7 2.4 %collective-permute-start.4 = (f32[7,4864]{1,0:T(8,128)S(1)}, f32[7,4864]{1,0:T(8,128)S(1)}, u32[]{:S(2)}, u32[]{:S(2)}) collective-permute-start(f32[7,4864]{1,0:T(8,128)S(1)} %fusion.5), channel_id=1, source_target_pairs={{0,2},{1,3},{2,0},{3,1},{4,6},{5,7},{6,4},{7,5},{8,10},{9,11},{10,... | collective-permute-start | bytes 408584 | tf_op jit(solution)/shard_map/ppermute | solution.py:13
  191.2 1.7 collective-permute-start.5
  192.9 4.3 %collective-permute-done.3 = f32[7,4864]{1,0:T(8,128)S(1)} collective-permute-done((f32[7,4864]{1,0:T(8,128)S(1)}, f32[7,4864]{1,0:T(8,128)S(1)}, u32[]{:S(2)}, u32[]{:S(2)}) %collective-permute-start.3) | collective-permute-done | bytes 136224 | tf_op jit(solution)/shard_map/ppermute | solution.py:13
  197.2 6.8 %collective-permute-done.4 = f32[7,4864]{1,0:T(8,128)S(1)} collective-permute-done((f32[7,4864]{1,0:T(8,128)S(1)}, f32[7,4864]{1,0:T(8,128)S(1)}, u32[]{:S(2)}, u32[]{:S(2)}) %collective-permute-start.4) | collective-permute-done | bytes 136224 | tf_op jit(solution)/shard_map/ppermute | solution.py:13
  204.1 2.1 %collective-permute-done.5 = f32[7,4864]{1,0:T(8,128)S(1)} collective-permute-done((f32[7,4864]{1,0:T(8,128)S(1)}, f32[7,4864]{1,0:T(8,128)S(1)}, u32[]{:S(2)}, u32[]{:S(2)}) %collective-permute-start.5) | collective-permute-done | bytes 136224 | tf_op jit(solution)/shard_map/ppermute | solution.py:13
  (64 shorter events, 9.2 us)
Async XLA Ops:
  0.6 79.4 %copy-start = (bf16[608,2432]{1,0:T(8,128)(2,1)S(1)}, bf16[608,2432]{1,0:T(8,128)(2,1)}, u32[]{:S(2)}) copy-start(bf16[608,2432]{1,0:T(8,128)(2,1)} %param.10) | copy-start | bytes 8871940
  36.4 26.5 %all-to-all-start = ((bf16[64,2,2432]{2,1,0:T(2,128)(2,1)}), bf16[64,2,2432]{2,1,0:T(2,128)(2,1)}, u32[]{:S(2)}, u32[]{:S(2)}) async-start(bf16[64,2,2432]{2,1,0:T(2,128)(2,1)} %reshape.296), calls=%async_computation | async-start | bytes 1245184 | tf_op jit(solution)/shard_map/all_to_all | solution.py:60
  50.2 87.8 %collective-permute-start.2 = (bf16[1,2,64,608]{3,2,1,0:T(8,128)(2,1)}, bf16[1,2,64,608]{3,2,1,0:T(8,128)(2,1)}, u32[]{:S(2)}, u32[]{:S(2)}) collective-permute-start(bf16[1,2,64,608]{3,2,1,0:T(8,128)(2,1)} %bitcast.152), channel_id=1, source_target_pairs={{0,3},{1,0},{2,1},{3,2},{4,7},{5,4},{6,5},{7,6},{8,11},{9,8},{10,9... | collective-permute-start | bytes 466952 | tf_op jit(solution)/shard_map/ppermute | solution.py:38
  56.3 81.7 %collective-permute-start.1 = (bf16[1,2,64,608]{3,2,1,0:T(8,128)(2,1)}, bf16[1,2,64,608]{3,2,1,0:T(8,128)(2,1)}, u32[]{:S(2)}, u32[]{:S(2)}) collective-permute-start(bf16[1,2,64,608]{3,2,1,0:T(8,128)(2,1)} %bitcast.153), channel_id=1, source_target_pairs={{0,2},{1,3},{2,0},{3,1},{4,6},{5,7},{6,4},{7,5},{8,10},{9,11},{10,... | collective-permute-start | bytes 466952 | tf_op jit(solution)/shard_map/ppermute | solution.py:38
  58.4 79.6 %collective-permute-start = (bf16[1,2,64,608]{3,2,1,0:T(8,128)(2,1)}, bf16[1,2,64,608]{3,2,1,0:T(8,128)(2,1)}, u32[]{:S(2)}, u32[]{:S(2)}) collective-permute-start(bf16[1,2,64,608]{3,2,1,0:T(8,128)(2,1)} %bitcast.154), channel_id=1, source_target_pairs={{0,1},{1,2},{2,3},{3,0},{4,5},{5,6},{6,7},{7,4},{8,9},{9,10},{10,1... | collective-permute-start | bytes 466952 | tf_op jit(solution)/shard_map/ppermute | solution.py:38
  111.2 1.1 copy-start.2
  111.2 1.5 copy-start.1
  112.3 1.6 copy-start.5
  112.3 1.6 copy-start.6
  112.7 15.1 %copy-start.8 = (f32[2]{0:T(128)S(1)}, f32[2]{0:T(128)}, u32[]{:S(2)}) copy-start(f32[2]{0:T(128)} %constant.116.clone) | copy-start | bytes 28
  136.4 1.0 copy-start.3
  137.4 0.9 copy-start.7
  138.3 1.5 copy-start.4
  139.9 1.5 slice-start
  186.5 10.7 %collective-permute-start.3 = (f32[7,4864]{1,0:T(8,128)S(1)}, f32[7,4864]{1,0:T(8,128)S(1)}, u32[]{:S(2)}, u32[]{:S(2)}) collective-permute-start(f32[7,4864]{1,0:T(8,128)S(1)} %fusion.5), channel_id=1, source_target_pairs={{0,3},{1,0},{2,1},{3,2},{4,7},{5,4},{6,5},{7,6},{8,11},{9,8},{10,9... | collective-permute-start | bytes 408584 | tf_op jit(solution)/shard_map/ppermute | solution.py:13
  188.7 15.3 %collective-permute-start.4 = (f32[7,4864]{1,0:T(8,128)S(1)}, f32[7,4864]{1,0:T(8,128)S(1)}, u32[]{:S(2)}, u32[]{:S(2)}) collective-permute-start(f32[7,4864]{1,0:T(8,128)S(1)} %fusion.5), channel_id=1, source_target_pairs={{0,2},{1,3},{2,0},{3,1},{4,6},{5,7},{6,4},{7,5},{8,10},{9,11},{10,... | collective-permute-start | bytes 408584 | tf_op jit(solution)/shard_map/ppermute | solution.py:13
  191.2 15.0 %collective-permute-start.5 = (f32[7,4864]{1,0:T(8,128)S(1)}, f32[7,4864]{1,0:T(8,128)S(1)}, u32[]{:S(2)}, u32[]{:S(2)}) collective-permute-start(f32[7,4864]{1,0:T(8,128)S(1)} %fusion.5), channel_id=1, source_target_pairs={{0,1},{1,2},{2,3},{3,0},{4,5},{5,6},{6,7},{7,4},{8,9},{9,10},{10,1... | collective-permute-start | bytes 408584 | tf_op jit(solution)/shard_map/ppermute | solution.py:13
